TPU v7x, 32 devices: a whole 2x2x4 slice. The times are simulated.
32 devices in a mesh: dp: 4 (over x, core), mp: 8 (over z, y).
Axes of the slice: x: 2, y: 2, z: 4, core: 2. Of those that a mesh axis runs over, the one named last changes fastest.
Arguments:
- queries: bfloat16 [512, 4096], P('dp'), may hold values from -103 to 103
- new_kv: bfloat16 [2, 512, 1024], P(None, 'dp'), may hold values from -6 to 6
- residual: bfloat16 [512, 4096], P('dp', 'mp'), may hold values from -2.4 to 2.4
- out_weight: bfloat16 [4096, 4096], P('mp'), may hold values from -0.125 to 0.125
- norm_gain: float32 [4096], replicated, may hold values from 0.5 to 1.5
- router: bfloat16 [4096, 8], replicated, may hold values from -0.09375 to 0.09375
- expert_in: bfloat16 [8, 2, 8192, 4096], P('dp', None, 'mp'), may hold values from -0.09375 to 0.09375
- expert_out: bfloat16 [8, 8192, 4096], P('dp', 'mp'), may hold values from -0.09375 to 0.09375
- node_cache: bfloat16 [2, 384, 8, 128, 128], P(None, 'dp', 'mp'), may hold values from -6 to 6
- leaf_cache: bfloat16 [2, 512, 8, 128, 128], P(None, 'dp', 'mp'), may hold values from -6 to 6
- slot_request: int32 [512], replicated, may hold values from 0 to 511, each once
- request_branch: int32 [512], replicated, may hold values from 0 to 31, as said below
- branch_parent: int32 [32], replicated, may hold values from 0 to 7, as said below
- root_owner: int32 [8], replicated, may hold values from 0 to 3, as said below
- branch_owner: int32 [32], replicated, may hold values from 0 to 3, as said below
- root_pages: int32 [8, 32], replicated, may hold values from 0 to 95, as said below
- branch_pages: int32 [32, 4], replicated, may hold values from 0 to 95, as said below
- root_len: int32 [8], replicated, may hold values from 1 to 4096, as said below
- branch_len: int32 [32], replicated, may hold values from 1 to 512
- leaf_len: int32 [512], P('dp'), may hold values from 1 to 128
- routes: int32 [512, 2], P('dp'), may hold values from 0 to 7, all different within a row; in each aligned block of 128 rows (0 to 127, 128 to 255, ...) at most 64 rows name the same one
Outputs:
- layer_out: bfloat16 [512, 4096], P('dp', 'mp')
Inputs may be any that keep to these rules, and one draw needn't show every extreme that they name: `request_branch`: at most 32 requests share a branch, and some branch has exactly 32. `branch_parent`: every root has exactly 4 branches. `root_owner`: every index of dp holds exactly 2 roots. `branch_owner`: every index of dp holds exactly 8 branches. `root_pages`: no slot of an owner's pool serves two pages of its nodes. `branch_pages`: no slot of an owner's pool serves two pages of its nodes. `root_len`: some root has 32 full pages.
All inputs are finite; a program needn't handle non-finite values.
Results may differ from a plain program's by a relative error of at most 0.034.
Values may be sent and summed in bfloat16 or wider, within the bound.
No kernel may reach another device: no remote copies, remote signals or barrier semaphores. Data moves between devices by JAX's collectives and lax.ppermute only.
A program may use at most 576 MiB of HBM per device.

v0:
```python
import jax
import jax.numpy as jnp
from jax import lax
from jax.sharding import PartitionSpec as P

HEADS = 32
KVH = 8
EXPERTS = 8
TOP = 2
PAGE = 128
ROOT_DEV = 2
BR_DEV = 8
BR_CAP = 32
E_CAP = 64


MASKED_SCORE = -1e30
NORM_EPS = 1e-05


def partner(x, axis, apart):
    return lax.ppermute(x, axis, [(i, i ^ 1 << apart) for i in range(lax.axis_size(axis))])


def merge_partials(first_part, second_part):
    first_sum, first_max, first_total = first_part
    second_sum, second_max, second_total = second_part
    common_max = jnp.maximum(first_max, second_max)
    first_factor = jnp.exp(first_max - common_max)
    second_factor = jnp.exp(second_max - common_max)
    merged_sum = first_sum * first_factor[..., None] + second_sum * second_factor[..., None]
    return (merged_sum, common_max, first_total * first_factor + second_total * second_factor)


def weigh_scores(scores, usable, values, pattern):
    masked_scores = jnp.where(usable, scores, MASKED_SCORE)
    row_max = jnp.max(masked_scores, axis=-1)
    weights = jnp.where(usable, jnp.exp(masked_scores - row_max[..., None]), 0.0)
    weight_total = jnp.sum(weights, axis=-1)
    weighted_sum = jnp.einsum(
        pattern, weights.astype(jnp.bfloat16), values, preferred_element_type=jnp.float32
    )
    return (weighted_sum, row_max, weight_total)


def shards(
    queries,
    new_kv,
    residual,
    out_weight,
    norm_gain,
    router,
    expert_in,
    expert_out,
    node_cache,
    leaf_cache,
    slot_request,
    request_branch,
    branch_parent,
    root_owner,
    branch_owner,
    root_pages,
    branch_pages,
    root_len,
    branch_len,
    leaf_len,
    routes,
):
    head_width = node_cache.shape[-1]
    token_width = node_cache.shape[-2]
    part_count = lax.axis_size("mp") // KVH
    group_size = HEADS // KVH
    own_heads = HEADS // lax.axis_size("mp")
    local_rows = queries.shape[0]
    requests = slot_request.shape[0]
    branches = branch_parent.shape[0]
    root_count = root_owner.shape[0]
    mp_index = lax.axis_index("mp")
    dp_index = lax.axis_index("dp")
    kv_head = mp_index // part_count
    part_index = mp_index % part_count
    group_queries = lax.dynamic_slice_in_dim(
        queries, kv_head * group_size * head_width, group_size * head_width, 1
    )
    all_queries = lax.all_gather(group_queries, "dp", axis=0, tiled=True).reshape(
        requests, group_size, head_width
    )
    slot_branch = jnp.sum(
        jnp.where(
            slot_request[:, None] == jnp.arange(requests)[None, :], request_branch[None, :], 0
        ),
        axis=1,
    )
    slot_root = jnp.sum(
        jnp.where(
            slot_branch[:, None] == jnp.arange(branches)[None, :], branch_parent[None, :], 0
        ),
        axis=1,
    )
    local_roots = jnp.nonzero(root_owner == dp_index, size=ROOT_DEV)[0]
    local_branches = jnp.nonzero(branch_owner == dp_index, size=BR_DEV)[0]
    page_pool = node_cache[:, :, 0]
    flat_queries = all_queries.reshape(requests, group_size * head_width)

    def selection(node_of_slot, nodes, cap):
        hit = node_of_slot[None, :] == nodes[:, None]
        rank = jnp.cumsum(hit.astype(jnp.int32), axis=1) - 1
        return hit[:, None, :] & (rank[:, None, :] == jnp.arange(cap)[None, :, None])

    def level_rows(nodes, node_pages, node_len, cap):
        pick = selection(node_of_slot_for[cap], nodes, cap)
        member_queries = jnp.einsum(
            "nks,sx->nkx", pick.astype(jnp.bfloat16), flat_queries,
            preferred_element_type=jnp.float32,
        ).astype(jnp.bfloat16).reshape(nodes.shape[0], cap, group_size, head_width)
        page_list = jnp.take(node_pages, nodes, axis=0)
        blocks = jnp.take(page_pool, page_list.reshape(-1), axis=1).reshape(
            (2,) + page_list.shape + page_pool.shape[2:]
        )
        lengths = jnp.take(node_len, nodes)

        def one_node(queries_of, keys_of, values_of, length):
            page_count = keys_of.shape[0]
            positions = (
                jnp.arange(page_count)[:, None] * PAGE
                + part_index * token_width
                + jnp.arange(token_width)[None, :]
            ).reshape(-1)
            usable = (positions < length)[None, None, :]
            scores = jnp.einsum(
                "sgd,ld->sgl", queries_of, keys_of.reshape(-1, head_width),
                preferred_element_type=jnp.float32,
            ) * head_width ** (-0.5)
            return weigh_scores(scores, usable, values_of.reshape(-1, head_width), "sgl,ld->sgd")

        weighted_sum, row_max, weight_total = jax.vmap(one_node)(
            member_queries, blocks[0], blocks[1], lengths
        )
        stats = jnp.concatenate([row_max, weight_total], axis=2)
        stats = jnp.pad(stats, ((0, 0), (0, 0), (0, head_width - 2 * group_size)))
        rows = jnp.concatenate(
            [weighted_sum.reshape(nodes.shape[0], cap, group_size * head_width), stats], axis=2
        )
        return jnp.einsum(
            "nks,nkc->sc", pick.astype(jnp.float32), rows,
            precision=lax.Precision.HIGHEST, preferred_element_type=jnp.float32,
        )

    root_cap = (branches // root_count) * BR_CAP
    node_of_slot_for = {root_cap: slot_root, BR_CAP: slot_branch}
    root_rows = level_rows(local_roots, root_pages, root_len, root_cap)
    branch_rows = level_rows(local_branches, branch_pages, branch_len, BR_CAP)
    groups = group_size
    dp_count = lax.axis_size("dp")
    packed = jnp.concatenate([root_rows, branch_rows], axis=1)
    exchanged = lax.all_to_all(
        packed.reshape(dp_count, local_rows, (2 * groups + 2) * head_width),
        "dp",
        split_axis=0,
        concat_axis=0,
        tiled=True,
    )
    gathered = jnp.sum(exchanged, axis=0).reshape(local_rows, 2 * groups + 2, head_width)
    root_stats = gathered[:, groups]
    branch_stats = gathered[:, 2 * groups + 1]
    returned = (
        gathered[:, :groups],
        root_stats[:, :groups],
        root_stats[:, groups : 2 * groups],
        gathered[:, groups + 1 : 2 * groups + 1],
        branch_stats[:, :groups],
        branch_stats[:, groups : 2 * groups],
    )
    leaf_block = leaf_cache[:, :, 0]
    mine_queries = group_queries.reshape(local_rows, group_size, head_width)
    leaf_places = part_index * token_width + jnp.arange(token_width)
    leaf_usable = (leaf_places[None, :] < leaf_len[:, None])[:, None, :]
    leaf_scores = jnp.einsum(
        "rgd,rtd->rgt", mine_queries, leaf_block[0], preferred_element_type=jnp.float32
    ) * head_width ** (-0.5)
    leaf_partial = weigh_scores(leaf_scores, leaf_usable, leaf_block[1], "rgt,rtd->rgd")
    running = merge_partials(
        (returned[0], returned[1], returned[2]), (returned[3], returned[4], returned[5])
    )
    running = merge_partials(running, leaf_partial)
    bit_count = part_count.bit_length() - 1
    for bit_index in reversed(range(bit_count)):
        half_heads = running[1].shape[1] // 2
        upper_side = mp_index >> bit_index & 1 == 1
        kept_half = tuple(
            (
                jnp.where(upper_side, component[:, half_heads:], component[:, :half_heads])
                for component in running
            )
        )
        sent_half = tuple(
            (
                jnp.where(upper_side, component[:, :half_heads], component[:, half_heads:])
                for component in running
            )
        )
        received = partner((sent_half[0], sent_half[1], sent_half[2]), "mp", bit_index)
        running = merge_partials(kept_half, received)
    own_queries = lax.dynamic_slice_in_dim(
        queries, mp_index * own_heads * head_width, own_heads * head_width, 1
    ).reshape(local_rows, own_heads, head_width)
    fresh_kv = lax.dynamic_slice_in_dim(new_kv, kv_head * head_width, head_width, 2)
    self_score = jnp.einsum(
        "rhd,rd->rh", own_queries, fresh_kv[0], preferred_element_type=jnp.float32
    ) * head_width ** (-0.5)
    weighted, row_max, weight_total = running
    common_max = jnp.maximum(row_max, self_score)
    old_factor = jnp.exp(row_max - common_max)
    new_factor = jnp.exp(self_score - common_max)
    weighted = (
        weighted * old_factor[..., None]
        + new_factor[..., None] * fresh_kv[1].astype(jnp.float32)[:, None, :]
    )
    weight_total = weight_total * old_factor + new_factor
    attended = (
        (weighted / weight_total[..., None])
        .astype(jnp.bfloat16)
        .reshape(local_rows, own_heads * head_width)
    )
    projected = jnp.dot(attended, out_weight, preferred_element_type=jnp.float32)
    slice_width = residual.shape[1]
    mp_count = lax.axis_size("mp")
    start_col = mp_index * slice_width
    own_cols = lax.dynamic_slice_in_dim(projected, start_col, slice_width, 1) + residual.astype(
        jnp.float32
    )
    projected = lax.dynamic_update_slice_in_dim(projected, own_cols, start_col, 1)
    terms = projected.astype(jnp.bfloat16).reshape(local_rows, mp_count, slice_width)
    terms = jnp.transpose(terms, (1, 0, 2))
    received_terms = lax.all_to_all(terms, "mp", split_axis=0, concat_axis=0, tiled=True)
    kept_cols = jnp.sum(received_terms.astype(jnp.float32), axis=0)
    spread_cols = jnp.broadcast_to(
        kept_cols.astype(jnp.bfloat16)[None], (mp_count, local_rows, slice_width)
    )
    all_cols = lax.all_to_all(spread_cols, "mp", split_axis=0, concat_axis=0, tiled=True)
    hidden = jnp.transpose(all_cols, (1, 0, 2)).reshape(local_rows, -1).astype(jnp.float32)
    inv_rms = lax.rsqrt(jnp.mean(hidden * hidden, axis=1) + NORM_EPS)
    normed = (hidden * inv_rms[:, None] * norm_gain[None, :]).astype(jnp.bfloat16)
    logits = jnp.dot(normed, router, preferred_element_type=jnp.float32)
    route_hits = routes[:, :, None] == jnp.arange(EXPERTS)[None, None, :]
    chosen = jnp.sum(jnp.where(route_hits, logits[:, None, :], 0.0), axis=2)
    gate_weights = jax.nn.softmax(chosen, axis=1)
    pair_experts = routes.reshape(-1)
    pair_onehot = (pair_experts[:, None] == jnp.arange(EXPERTS)[None, :]).astype(jnp.int32)
    pair_rank = jnp.sum((jnp.cumsum(pair_onehot, axis=0) - 1) * pair_onehot, axis=1)
    pair_slot = pair_experts * E_CAP + pair_rank
    slot_source = (
        jnp.full((EXPERTS * E_CAP,), local_rows, jnp.int32)
        .at[pair_slot]
        .set(jnp.arange(pair_experts.shape[0], dtype=jnp.int32) // TOP)
    )
    padded = jnp.concatenate([normed, jnp.zeros((1, normed.shape[1]), jnp.bfloat16)], axis=0)
    local_experts = expert_in.shape[0]
    outgoing = jnp.take(padded, slot_source, axis=0).reshape(
        dp_count, local_experts, E_CAP, normed.shape[1]
    )
    returned_parts = []
    for expert_index in range(local_experts):
        incoming = lax.all_to_all(
            outgoing[:, expert_index], "dp", split_axis=0, concat_axis=0, tiled=True
        )
        gate_up = jnp.einsum(
            "scd,kfd->kscf", incoming, expert_in[expert_index], preferred_element_type=jnp.float32
        )
        expert_hidden = (jax.nn.silu(gate_up[0]) * gate_up[1]).astype(jnp.bfloat16)
        if expert_index == local_experts - 1 and local_experts > 1:
            pieces = jnp.einsum(
                "scf,fmd->mscd", expert_hidden,
                expert_out[expert_index].reshape(-1, mp_count, slice_width),
                preferred_element_type=jnp.float32,
            ).astype(jnp.bfloat16)
            gathered_pieces = lax.all_to_all(pieces, "mp", split_axis=0, concat_axis=0, tiled=True)
            summed = jnp.sum(gathered_pieces.astype(jnp.float32), axis=0).astype(jnp.bfloat16)
        else:
            expert_partial = jnp.einsum(
                "scf,fd->scd", expert_hidden, expert_out[expert_index],
                preferred_element_type=jnp.float32,
            )
            summed = lax.psum_scatter(
                expert_partial.astype(jnp.bfloat16), "mp", scatter_dimension=2, tiled=True
            )
        returned_parts.append(
            lax.all_to_all(summed, "dp", split_axis=0, concat_axis=0, tiled=True)
        )
    returned_rows = jnp.stack(returned_parts, axis=1)
    results = jnp.take(returned_rows.reshape(-1, slice_width), pair_slot, axis=0).reshape(
        local_rows, TOP, slice_width
    )
    layer_out = kept_cols + jnp.sum(gate_weights[:, :, None] * results.astype(jnp.float32), axis=1)
    return layer_out.astype(jnp.bfloat16)


def solution(mesh):
    placed = (
        P("dp", None),
        P(None, "dp", None),
        P("dp", "mp"),
        P("mp", None),
        P(),
        P(),
        P("dp", None, "mp", None),
        P("dp", "mp", None),
        P(None, "dp", "mp", None, None),
        P(None, "dp", "mp", None, None),
        P(),
        P(),
        P(),
        P(),
        P(),
        P(),
        P(),
        P(),
        P(),
        P("dp"),
        P("dp", None),
    )
    return jax.shard_map(
        shards, mesh=mesh, in_specs=placed, out_specs=P("dp", "mp"), check_vma=False
    )
```

profile of v0, /device:TPU:0, one launch (start us, length us, event | category | flops | bytes accessed | tf_op | source)
XLA Modules:
  0.0 351.5 jit_solution(9087854962025036373)
XLA Ops:
  6.5 0.7 fusion.125
  7.3 1.3 fusion.126
  9.2 1.4 fusion.124
  10.9 0.8 scatter_custom_fusion.1
  13.5 0.7 fusion.120
  14.2 1.3 gather_fusion
  15.5 0.7 broadcast_select_fusion.4
  16.2 1.2 gather_fusion.1
  17.7 1.3 gather_fusion.3
  19.7 0.8 copy.180
  21.2 0.9 select_reduce_fusion
  22.2 0.7 select_reduce_fusion.1
  24.2 8.6 %all_gather.3 = bf16[512,512]{1,0:T(8,128)(2,1)S(1)} all-gather(bf16[128,512]{1,0:T(8,128)(2,1)S(1)} %constant_dynamic-slice_fusion), channel_id=1, replica_groups=mesh['dp'=4,'mp'=8] {'dp'}, dimensions={0}, use_global_device_ids=true | all-gather | bytes 655360 | tf_op jit(solution)/shard_map/all_gather | solution.py:85
  32.8 6.0 %gather_fusion.2 = bf16[64,2,128,128]{3,2,1,0:T(8,128)(2,1)} fusion(bf16[2,96,128,128]{3,2,1,0:T(8,128)(2,1)} %bitcast.233, s32[1024]{0:T(1024)S(1)} %pad_clamp_fusion.4), kind=kCustom, calls=%fused_computation.2 | custom fusion | bytes 8388864 | tf_op jit(solution)/shard_map/jit(_take)/gather | solution.py:117
  38.8 2.6 select_bitcast_fusion
  42.0 0.7 fusion.36
  42.8 2.8 fusion.6
  45.6 5.1 %fusion.7 = f32[2,128,4]{1,2,0:T(4,128)S(1)} fusion(f32[2,128,4,4096]{3,1,2,0:T(8,128)S(1)} %get-tuple-element.33, f32[2,128,4]{1,2,0:T(4,128)S(1)} %get-tuple-element.32, pred[2,4096]{1,0:T(4,128)(4,1)S(1)} %broadcast_compare_fusion), kind=kLoop, calls=%fused_computation.20 | loop fusion | flops 20970496 | bytes 16793600 | tf_op jit(solution)/shard_map/vmap()/reduce_sum | solution.py:39
  50.7 4.2 %fusion.12 = f32[2,128,4,128]{1,3,2,0:T(8,128)S(1)} fusion(bf16[2,4096,128,1]{2,1,3,0:T(8,128)(2,1)S(1)} %bitcast.240, f32[2,128,4,4096]{3,1,2,0:T(8,128)S(1)} %get-tuple-element.33, f32[2,128,4]{1,2,0:T(4,128)S(1)} %get-tuple-element.32, pred[2,4096]{1,0:T(4,128)(4,1)S(1)} %broadcast_compare_fusion), kind=kOutput, calls=%fused_computation.25 | convolution fusion | flops 1094713344 | bytes 19410944 | tf_op jit(solution)/shard_map/vmap(sgl,ld->sgd)/dot_general | solution.py:40
  54.9 1.0 copy.178
  56.1 1.1 reduce-window.36
  57.7 3.7 %gather_fusion.5 = bf16[32,2,128,128]{3,2,1,0:T(8,128)(2,1)S(1)} fusion(bf16[2,96,128,128]{3,2,1,0:T(8,128)(2,1)} %bitcast.234, s32[1024]{0:T(1024)S(1)} %pad_clamp_fusion.2), kind=kCustom, calls=%fused_computation.5 | custom fusion | bytes 4194432 | tf_op jit(solution)/shard_map/jit(_take)/gather | solution.py:117
  62.0 0.8 copy-done.6
  63.7 0.7 fusion.34
  65.5 1.0 convolution_bitcast_fusion.1
  66.6 0.9 convolution_bitcast_fusion
  67.5 1.7 pad_maximum_fusion
  69.2 4.9 %all-to-all-start = ((f32[4,128,1280]{2,1,0:T(8,128)}), f32[4,128,1280]{2,1,0:T(8,128)}, u32[]{:S(2)}, u32[]{:S(2)}) async-start(f32[4,128,1280]{2,1,0:T(8,128)} %bitcast.229), calls=%async_computation | async-start | bytes 5242880 | tf_op jit(solution)/shard_map/all_to_all | solution.py:156
  74.2 4.5 %fusion.151 = (f32[128,4]{1,0:T(8,128)S(1)}, f32[128,4,128]{2,1,0:T(4,128)S(1)}) fusion(bf16[128,4,128]{2,1,0:T(4,128)(2,1)S(1)} %reshape.712, bf16[2,128,1,128,128]{4,3,1,2,0:T(8,128)(2,1)} %bitcast.255, pred[128,128]{1,0:T(8,128)(4,1)S(1)} %iota_compare_fusion.7), kind=kOutput, calls=%fused_computation.276 | convolution fusion | flops 16973312 | bytes 4605952 | tf_op jit(solution)/shard_map/rgd,rtd->rgt/dot_general | solution.py:178
  79.3 0.8 fusion.99
  80.5 25.0 %all-to-all-done = f32[4,128,1280]{2,1,0:T(8,128)} async-done(((f32[4,128,1280]{2,1,0:T(8,128)}), f32[4,128,1280]{2,1,0:T(8,128)}, u32[]{:S(2)}, u32[]{:S(2)}) %all-to-all-start) | async-done | bytes 2621472 | tf_op jit(solution)/shard_map/all_to_all | solution.py:156
  105.5 2.0 reduce_sum.148
  108.8 3.2 fusion.53
  112.3 0.7 fusion.91
  113.5 31.2 %all_to_all.40 = bf16[8,128,512]{2,1,0:T(8,128)(2,1)S(1)} all-to-all(bf16[8,128,512]{2,1,0:T(8,128)(2,1)S(1)} %bitcast.236), channel_id=1, replica_groups=mesh['dp'=4,'mp'=8] {'mp'}, dimensions={0} | all-to-all | bytes 2097152 | tf_op jit(solution)/shard_map/all_to_all | solution.py:235
  144.9 1.1 broadcast_in_dim.255
  146.0 3.6 %all-to-all-start.2 = ((bf16[8,128,512]{2,1,0:T(8,128)(2,1)}), bf16[8,128,512]{2,1,0:T(8,128)(2,1)S(1)}, u32[]{:S(2)}, u32[]{:S(2)}) async-start(bf16[8,128,512]{2,1,0:T(8,128)(2,1)} %broadcast_in_dim.255), calls=%async_computation.2 | async-start | bytes 2097152 | tf_op jit(solution)/shard_map/all_to_all | solution.py:240
  151.2 1.4 scatter_custom_fusion.2
  152.7 22.4 %all-to-all-done.2 = bf16[8,128,512]{2,1,0:T(8,128)(2,1)S(1)} async-done(((bf16[8,128,512]{2,1,0:T(8,128)(2,1)}), bf16[8,128,512]{2,1,0:T(8,128)(2,1)S(1)}, u32[]{:S(2)}, u32[]{:S(2)}) %all-to-all-start.2) | async-done | bytes 1048608 | tf_op jit(solution)/shard_map/all_to_all | solution.py:240
  176.5 4.4 %gather_fusion.6 = bf16[512,4096]{1,0:T(8,128)(2,1)} fusion(bf16[129,4096]{1,0:T(8,128)(2,1)S(1)} %concatenate.23, s32[1024]{0:T(1024)S(1)} %pad_clamp_fusion.1), kind=kCustom, calls=%fused_computation.6 | custom fusion | bytes 8390656 | tf_op jit(solution)/shard_map/jit(_take)/gather | solution.py:259
  180.9 2.6 copy_select_fusion
  183.5 2.5 slice_bitcast_fusion.5
  186.0 3.6 %all-to-all-start.3 = ((bf16[4,64,4096]{2,1,0:T(8,128)(2,1)}), bf16[4,64,4096]{2,1,0:T(8,128)(2,1)S(1)}, u32[]{:S(2)}, u32[]{:S(2)}) async-start(bf16[4,64,4096]{2,1,0:T(8,128)(2,1)} %get-tuple-element.18), calls=%async_computation.3 | async-start | bytes 4194304 | tf_op jit(solution)/shard_map/all_to_all | solution.py:264
  189.6 7.7 %slice.133 = bf16[1,1024,4096]{2,1,0:T(8,128)(2,1)} slice(bf16[2,1024,4096]{2,1,0:T(8,128)(2,1)} %param.28), slice={[1:2], [0:1024], [0:4096]} | slice | bytes 16777216 | tf_op jit(solution)/shard_map/slice | solution.py:274
  197.3 12.0 %copy.232 = bf16[1,1024,4096]{1,2,0:T(8,128)(2,1)} copy(bf16[1,1024,4096]{2,1,0:T(8,128)(2,1)} %slice.133) | data formatting | bytes 16777216
  209.2 6.0 %all-to-all-done.3 = bf16[4,64,4096]{2,1,0:T(8,128)(2,1)S(1)} async-done(((bf16[4,64,4096]{2,1,0:T(8,128)(2,1)}), bf16[4,64,4096]{2,1,0:T(8,128)(2,1)S(1)}, u32[]{:S(2)}, u32[]{:S(2)}) %all-to-all-start.3) | async-done | bytes 2097184 | tf_op jit(solution)/shard_map/all_to_all | solution.py:264
  215.3 1.4 copy-done.4
  216.6 3.6 %all-to-all-start.5 = ((bf16[4,64,4096]{2,1,0:T(8,128)(2,1)}), bf16[4,64,4096]{2,1,0:T(8,128)(2,1)S(1)}, u32[]{:S(2)}, u32[]{:S(2)}) async-start(bf16[4,64,4096]{2,1,0:T(8,128)(2,1)} %get-tuple-element.19), calls=%async_computation.6 | async-start | bytes 4194304 | tf_op jit(solution)/shard_map/all_to_all | solution.py:264
  220.6 12.2 %fusion.24 = f32[2,4,64,1024]{3,2,0,1:T(8,128)} fusion(bf16[2,2,1024,4096]{3,2,1,0:T(8,128)(2,1)} %param.27, bf16[4,64,4096]{2,1,0:T(8,128)(2,1)} %copy-done.4), kind=kOutput, calls=%fused_computation.49 | convolution fusion | flops 4294967296 | bytes 20971520 | tf_op jit(solution)/shard_map/scd,kfd->kscf/dot_general | solution.py:267
  232.8 7.8 %fusion.15 = bf16[4,64,4096]{2,1,0:T(8,128)(2,1)} fusion(bf16[2,1024,4096]{2,1,0:T(8,128)(2,1)} %param.28, f32[2,4,64,1024]{3,2,0,1:T(8,128)} %fusion.24), kind=kOutput, calls=%fused_computation.27 | convolution fusion | flops 2150105088 | bytes 12582912 | tf_op jit(solution)/shard_map/scf,fd->scd/dot_general | solution.py:280
  240.6 5.3 %all-to-all-done.5 = bf16[4,64,4096]{2,1,0:T(8,128)(2,1)S(1)} async-done(((bf16[4,64,4096]{2,1,0:T(8,128)(2,1)}), bf16[4,64,4096]{2,1,0:T(8,128)(2,1)S(1)}, u32[]{:S(2)}, u32[]{:S(2)}) %all-to-all-start.5) | async-done | bytes 2097184 | tf_op jit(solution)/shard_map/all_to_all | solution.py:264
  245.9 11.8 %fusion.29 = f32[2,4,64,1024]{3,2,0,1:T(8,128)} fusion(bf16[2,2,1024,4096]{3,2,1,0:T(8,128)(2,1)} %param.27, bf16[4,64,4096]{2,1,0:T(8,128)(2,1)S(1)} %all-to-all-done.5), kind=kOutput, calls=%fused_computation.50 | convolution fusion | flops 4294967296 | bytes 20971520 | tf_op jit(solution)/shard_map/scd,kfd->kscf/dot_general | solution.py:267
  257.7 6.9 %convert_bitcast_fusion.1 = bf16[8,4,64,512]{3,2,0,1:T(8,128)(2,1)S(1)} fusion(bf16[1024,8,512,1]{0,2,1,3:T(8,128)(2,1)} %bitcast.230, f32[2,4,64,1024]{3,2,0,1:T(8,128)} %fusion.29), kind=kOutput, calls=%fused_computation.43 | convolution fusion | flops 2150105088 | bytes 12582912 | tf_op jit(solution)/shard_map/scf,fmd->mscd/dot_general | solution.py:272
  264.6 1.5 copy.214
  266.1 3.7 %all-to-all-start.6 = ((bf16[8,4,64,512]{3,2,1,0:T(8,128)(2,1)}), bf16[8,4,64,512]{3,2,1,0:T(8,128)(2,1)S(1)}, u32[]{:S(2)}, u32[]{:S(2)}) async-start(bf16[8,4,64,512]{3,2,1,0:T(8,128)(2,1)} %copy.214), calls=%async_computation.7 | async-start | bytes 4194304 | tf_op jit(solution)/shard_map/all_to_all | solution.py:277
  270.6 50.7 %all-to-all-done.6 = bf16[8,4,64,512]{3,2,1,0:T(8,128)(2,1)S(1)} async-done(((bf16[8,4,64,512]{3,2,1,0:T(8,128)(2,1)}), bf16[8,4,64,512]{3,2,1,0:T(8,128)(2,1)S(1)}, u32[]{:S(2)}, u32[]{:S(2)}) %all-to-all-start.6) | async-done | bytes 2097184 | tf_op jit(solution)/shard_map/all_to_all | solution.py:277
  321.3 1.1 reduce_sum.157
  322.4 3.4 all-to-all-start.7
  325.8 5.9 %all-to-all-done.7 = bf16[4,64,512]{2,1,0:T(8,128)(2,1)S(1)} async-done(((bf16[4,64,512]{2,1,0:T(8,128)(2,1)}), bf16[4,64,512]{2,1,0:T(8,128)(2,1)S(1)}, u32[]{:S(2)}, u32[]{:S(2)}) %all-to-all-start.7) | async-done | bytes 262176 | tf_op jit(solution)/shard_map/all_to_all | solution.py:288
  331.8 3.4 all-to-all-start.4
  335.3 5.9 %all-to-all-done.4 = bf16[4,64,512]{2,1,0:T(8,128)(2,1)S(1)} async-done(((bf16[4,64,512]{2,1,0:T(8,128)(2,1)}), bf16[4,64,512]{2,1,0:T(8,128)(2,1)S(1)}, u32[]{:S(2)}, u32[]{:S(2)}) %all-to-all-start.4) | async-done | bytes 262176 | tf_op jit(solution)/shard_map/all_to_all | solution.py:288
  341.3 1.2 gather_fusion.7
  342.6 0.8 multiply_reduce_fusion
  343.4 0.7 add_convert_fusion
  (147 shorter events, 17.2 us)
Async XLA Ops:
  6.5 17.6 %copy-start = (bf16[128,4096]{1,0:T(8,128)(2,1)S(1)}, bf16[128,4096]{1,0:T(8,128)(2,1)}, u32[]{:S(2)}) copy-start(bf16[128,4096]{1,0:T(8,128)(2,1)} %param.21) | copy-start | bytes 3145732
  32.8 9.2 %copy-start.5 = (bf16[512,512]{1,0:T(8,128)(2,1)}, bf16[512,512]{1,0:T(8,128)(2,1)S(1)}, u32[]{:S(2)}) copy-start(bf16[512,512]{1,0:T(8,128)(2,1)S(1)} %all_gather.3) | copy-start | bytes 1572868
  61.8 1.0 copy-start.6
  64.5 1.0 copy-start.3
  69.2 4.9 %copy-start.11 = (s32[128]{0:T(128)S(1)}, s32[128]{0:T(128)}, u32[]{:S(2)}) copy-start(s32[128]{0:T(128)} %param.40) | copy-start | bytes 1540
  69.2 36.3 %all-to-all-start = ((f32[4,128,1280]{2,1,0:T(8,128)}), f32[4,128,1280]{2,1,0:T(8,128)}, u32[]{:S(2)}, u32[]{:S(2)}) async-start(f32[4,128,1280]{2,1,0:T(8,128)} %bitcast.229), calls=%async_computation | async-start | bytes 5242880 | tf_op jit(solution)/shard_map/all_to_all | solution.py:156
  108.8 3.5 copy-start.2
  112.3 0.9 copy-start.7
  144.9 4.7 %copy-start.10 = (s32[128,2]{0,1:T(2,128)S(1)}, s32[128,2]{0,1:T(2,128)}, u32[]{:S(2)}) copy-start(s32[128,2]{0,1:T(2,128)} %param.41) | copy-start | bytes 3076
  146.0 29.1 %all-to-all-start.2 = ((bf16[8,128,512]{2,1,0:T(8,128)(2,1)}), bf16[8,128,512]{2,1,0:T(8,128)(2,1)S(1)}, u32[]{:S(2)}, u32[]{:S(2)}) async-start(bf16[8,128,512]{2,1,0:T(8,128)(2,1)} %broadcast_in_dim.255), calls=%async_computation.2 | async-start | bytes 2097152 | tf_op jit(solution)/shard_map/all_to_all | solution.py:240
  175.4 0.7 copy-start.9
  186.0 29.3 %all-to-all-start.3 = ((bf16[4,64,4096]{2,1,0:T(8,128)(2,1)}), bf16[4,64,4096]{2,1,0:T(8,128)(2,1)S(1)}, u32[]{:S(2)}, u32[]{:S(2)}) async-start(bf16[4,64,4096]{2,1,0:T(8,128)(2,1)} %get-tuple-element.18), calls=%async_computation.3 | async-start | bytes 4194304 | tf_op jit(solution)/shard_map/all_to_all | solution.py:264
  215.2 1.4 copy-start.4
  216.6 29.3 %all-to-all-start.5 = ((bf16[4,64,4096]{2,1,0:T(8,128)(2,1)}), bf16[4,64,4096]{2,1,0:T(8,128)(2,1)S(1)}, u32[]{:S(2)}, u32[]{:S(2)}) async-start(bf16[4,64,4096]{2,1,0:T(8,128)(2,1)} %get-tuple-element.19), calls=%async_computation.6 | async-start | bytes 4194304 | tf_op jit(solution)/shard_map/all_to_all | solution.py:264
  220.3 111.5 %reduce-scatter.2.cloned.1.call-start = ((), (), s32[]{:S(2)}) async-start(), calls=%async_computation.9 | async-start | bytes 2359296 | tf_op jit(solution)/shard_map/reduce_scatter | solution.py:284
  266.1 4.1 %copy-start.8 = (bf16[4096,8]{0,1:T(8,128)(2,1)S(1)}, bf16[4096,8]{0,1:T(8,128)(2,1)}, u32[]{:S(2)}) copy-start(bf16[4096,8]{0,1:T(8,128)(2,1)} %param.26) | copy-start | bytes 196612
  266.1 55.2 %all-to-all-start.6 = ((bf16[8,4,64,512]{3,2,1,0:T(8,128)(2,1)}), bf16[8,4,64,512]{3,2,1,0:T(8,128)(2,1)S(1)}, u32[]{:S(2)}, u32[]{:S(2)}) async-start(bf16[8,4,64,512]{3,2,1,0:T(8,128)(2,1)} %copy.214), calls=%async_computation.7 | async-start | bytes 4194304 | tf_op jit(solution)/shard_map/all_to_all | solution.py:277
  322.4 9.4 %all-to-all-start.7 = ((bf16[4,64,512]{2,1,0:T(8,128)(2,1)}), bf16[4,64,512]{2,1,0:T(8,128)(2,1)S(1)}, u32[]{:S(2)}, u32[]{:S(2)}) async-start(bf16[4,64,512]{2,1,0:T(8,128)(2,1)} %reduce_sum.157), calls=%async_computation.8 | async-start | bytes 524288 | tf_op jit(solution)/shard_map/all_to_all | solution.py:288
  331.8 9.4 %all-to-all-start.4 = ((bf16[4,64,512]{2,1,0:T(8,128)(2,1)}), bf16[4,64,512]{2,1,0:T(8,128)(2,1)S(1)}, u32[]{:S(2)}, u32[]{:S(2)}) async-start(bf16[4,64,512]{2,1,0:T(8,128)(2,1)} %reduce-scatter.2.cloned.1.call-done), calls=%async_computation.5 | async-start | bytes 524288 | tf_op jit(solution)/shard_map/all_to_all | solution.py:288
  341.3 2.9 copy-start.1
Sparse Core Ops, SparseCore 0:
  240.7 89.3 reduce-scatter.1
where the time goes:
time: 358 us; the launch traced here: 351 us
  waiting for transfers between devices  121 us (34%)
  matrix products  58.9 us (16%)
  local copies, waits for them, and re-layouts  55.8 us (16%)
  blocking collectives  39.9 us (11%)
  other arithmetic  34.6 us (10%)
  starting transfers between devices  26.5 us (7%)
  between operations  14.5 us (4%)
    all_to_all x1, waiting for transfers between devices, shards(): lax.all_to_all(pieces, 'mp', split_axis=0, concat_axis=0, tiled=True)  50.7 us
    all_to_all x1, blocking collectives, shards(): lax.all_to_all(terms, 'mp', split_axis=0, concat_axis=0, tiled=True)  31.2 us
    all_to_all x1, waiting for transfers between devices, shards(): lax.all_to_all(packed.reshape(dp_count, local_rows, (2 * groups + 2) * he...  25 us
    dot_general x2, matrix products, shards(): jnp.einsum('scd,kfd->kscf', incoming, expert_in[expert_index], preferred_...  24 us
    all_to_all x1, waiting for transfers between devices, shards(): lax.all_to_all(spread_cols, 'mp', split_axis=0, concat_axis=0, tiled=True)  22.4 us
    unnamed x30, local copies, waits for them, and re-layouts  16.1 us
    all_to_all x2, waiting for transfers between devices, shards(): lax.all_to_all(summed, 'dp', split_axis=0, concat_axis=0, tiled=True)  11.8 us
    all_to_all x2, waiting for transfers between devices, shards(): lax.all_to_all(outgoing[:, expert_index], 'dp', split_axis=0, concat_axis...  11.3 us
  transfers between devices with their start and end apart: 8, of which 7 were waited for; matrix products, arithmetic and copies ran while one was open for 20% of the time, Pallas kernels for 0%

commit v1 on v0

--- a/solution.py
+++ b/solution.py
@@ -264,26 +264,33 @@
         incoming = lax.all_to_all(
             outgoing[:, expert_index], "dp", split_axis=0, concat_axis=0, tiled=True
         )
-        gate_up = jnp.einsum(
-            "scd,kfd->kscf", incoming, expert_in[expert_index], preferred_element_type=jnp.float32
-        )
-        expert_hidden = (jax.nn.silu(gate_up[0]) * gate_up[1]).astype(jnp.bfloat16)
-        if expert_index == local_experts - 1 and local_experts > 1:
-            pieces = jnp.einsum(
-                "scf,fmd->mscd", expert_hidden,
-                expert_out[expert_index].reshape(-1, mp_count, slice_width),
-                preferred_element_type=jnp.float32,
-            ).astype(jnp.bfloat16)
-            gathered_pieces = lax.all_to_all(pieces, "mp", split_axis=0, concat_axis=0, tiled=True)
-            summed = jnp.sum(gathered_pieces.astype(jnp.float32), axis=0).astype(jnp.bfloat16)
-        else:
+        by_mesh = expert_index == local_experts - 1 and local_experts > 1 and dp_count % 2 == 0
+        halves = 2 if by_mesh else 1
+        pieces_summed = []
+        for half in range(halves):
+            sources = dp_count // halves
+            chunk = incoming[half * sources : (half + 1) * sources]
+            gate_up = jnp.einsum(
+                "scd,kfd->kscf", chunk, expert_in[expert_index], preferred_element_type=jnp.float32
+            )
+            expert_hidden = (jax.nn.silu(gate_up[0]) * gate_up[1]).astype(jnp.bfloat16)
             expert_partial = jnp.einsum(
                 "scf,fd->scd", expert_hidden, expert_out[expert_index],
                 preferred_element_type=jnp.float32,
-            )
-            summed = lax.psum_scatter(
-                expert_partial.astype(jnp.bfloat16), "mp", scatter_dimension=2, tiled=True
-            )
+            ).astype(jnp.bfloat16)
+            if by_mesh:
+                pieces = expert_partial.reshape(sources, E_CAP, mp_count, slice_width)
+                gathered_pieces = lax.all_to_all(
+                    pieces, "mp", split_axis=2, concat_axis=2, tiled=True
+                )
+                pieces_summed.append(
+                    jnp.sum(gathered_pieces.astype(jnp.float32), axis=2).astype(jnp.bfloat16)
+                )
+            else:
+                pieces_summed.append(
+                    lax.psum_scatter(expert_partial, "mp", scatter_dimension=2, tiled=True)
+                )
+        summed = jnp.concatenate(pieces_summed, axis=0)
         returned_parts.append(
             lax.all_to_all(summed, "dp", split_axis=0, concat_axis=0, tiled=True)
         )

time: 358 us -> 366 us (1.022)
  blocking collectives: 39.9 us -> 68.8 us
  local copies, waits for them, and re-layouts: 55.8 us -> 34.7 us
  matrix products: 58.9 us -> 74.3 us
  waiting for transfers between devices: 121 us -> 106 us
    all_to_all x0 -> x1, blocking collectives: none -> 28.9 us  [shards(): lax.all_to_all(outgoing[:, expert_index], 'dp', split_axis=0, concat_axis...]
    unnamed x30 -> x29, local copies, waits for them, and re-layouts: 16.1 us -> 2.79 us
    dot_general x1 -> x3, matrix products: 7.81 us -> 18 us  [shards(): jnp.einsum('scf,fd->scd', expert_hidden, expert_out[expert_index], prefer...]
    all_to_all x1 -> x2, waiting for transfers between devices: 50.7 us -> 41.4 us  [shards(): lax.all_to_all(pieces, 'mp', split_axis=2, concat_axis=2, tiled=True)]
    slice x2 -> x1, local copies, waits for them, and re-layouts: 7.92 us -> 0.21 us  [the longest x1 7.7 us: shards(): expert_out[expert_index].reshape(-1, mp_count, slice_width)]
    all_to_all x2 -> x1, waiting for transfers between devices: 11.3 us -> 5.35 us  [shards(): lax.all_to_all(outgoing[:, expert_index], 'dp', split_axis=0, concat_axis...]
    dot_general x3, matrix products: 30.9 us -> 36.1 us  [shards(): jnp.einsum('scd,kfd->kscf', chunk, expert_in[expert_index], preferred_ele...]
    all_to_all x1 -> x2, starting transfers between devices: 3.74 us -> 7.51 us  [shards(): lax.all_to_all(pieces, 'mp', split_axis=2, concat_axis=2, tiled=True)]
  transfers between devices with their start and end apart: 8 -> 8, of which waited for: 7 -> 7; matrix products, arithmetic and copies ran while one was open for 20% -> 19% of each run, Pallas kernels for 0% -> 0%
where the time goes in v1:
time: 366 us; the launch traced here: 360 us
  waiting for transfers between devices  106 us (29%)
  matrix products  74.3 us (20%)
  blocking collectives  68.8 us (19%)
  other arithmetic  35 us (10%)
  local copies, waits for them, and re-layouts  34.7 us (9%)
  starting transfers between devices  26.6 us (7%)
  between operations  14.3 us (4%)
    all_to_all x2, waiting for transfers between devices, shards(): lax.all_to_all(pieces, 'mp', split_axis=2, concat_axis=2, tiled=True)  41.4 us
    dot_general x3, matrix products, shards(): jnp.einsum('scd,kfd->kscf', chunk, expert_in[expert_index], preferred_ele...  36.1 us
    all_to_all x1, blocking collectives, shards(): lax.all_to_all(terms, 'mp', split_axis=0, concat_axis=0, tiled=True)  31.2 us
    all_to_all x1, blocking collectives, shards(): lax.all_to_all(outgoing[:, expert_index], 'dp', split_axis=0, concat_axis...  28.9 us
    all_to_all x1, waiting for transfers between devices, shards(): lax.all_to_all(packed.reshape(dp_count, local_rows, (2 * groups + 2) * he...  25 us
    all_to_all x1, waiting for transfers between devices, shards(): lax.all_to_all(spread_cols, 'mp', split_axis=0, concat_axis=0, tiled=True)  22.4 us
    dot_general x3, matrix products, shards(): jnp.einsum('scf,fd->scd', expert_hidden, expert_out[expert_index], prefer...  18 us
    all_to_all x2, waiting for transfers between devices, shards(): lax.all_to_all(summed, 'dp', split_axis=0, concat_axis=0, tiled=True)  11.8 us
  transfers between devices with their start and end apart: 8, of which 7 were waited for; matrix products, arithmetic and copies ran while one was open for 19% of the time, Pallas kernels for 0%

profile of v1, /device:TPU:0, one launch (start us, length us, event | category | flops | bytes accessed | tf_op | source)
XLA Modules:
  0.0 359.7 jit_solution(15637508156191548270)
XLA Ops:
  6.5 0.7 fusion.143
  7.3 1.3 fusion.144
  9.2 1.4 fusion.142
  10.9 0.8 scatter_custom_fusion.1
  13.5 0.7 fusion.138
  14.2 1.3 gather_fusion
  15.5 0.7 broadcast_select_fusion.4
  16.2 1.2 gather_fusion.1
  17.7 1.3 gather_fusion.3
  19.7 0.8 copy.174
  21.2 0.9 select_reduce_fusion
  22.2 0.7 select_reduce_fusion.1
  24.2 8.6 %all_gather.3 = bf16[512,512]{1,0:T(8,128)(2,1)S(1)} all-gather(bf16[128,512]{1,0:T(8,128)(2,1)S(1)} %constant_dynamic-slice_fusion), channel_id=1, replica_groups=mesh['dp'=4,'mp'=8] {'dp'}, dimensions={0}, use_global_device_ids=true | all-gather | bytes 655360 | tf_op jit(solution)/shard_map/all_gather | solution.py:85
  32.8 6.0 %gather_fusion.2 = bf16[64,2,128,128]{3,2,1,0:T(8,128)(2,1)} fusion(bf16[2,96,128,128]{3,2,1,0:T(8,128)(2,1)} %bitcast.253, s32[1024]{0:T(1024)S(1)} %pad_clamp_fusion.4), kind=kCustom, calls=%fused_computation.2 | custom fusion | bytes 8388864 | tf_op jit(solution)/shard_map/jit(_take)/gather | solution.py:117
  38.8 2.6 select_bitcast_fusion
  42.1 0.7 fusion.51
  42.9 2.8 fusion.7
  45.6 5.5 %fusion.10 = f32[2,128,4]{1,2,0:T(4,128)S(1)} fusion(f32[2,128,4,4096]{3,1,2,0:T(8,128)S(1)} %get-tuple-element.33, f32[2,128,4]{1,2,0:T(4,128)S(1)} %get-tuple-element.32, pred[2,4096]{1,0:T(4,128)(4,1)S(1)} %broadcast_compare_fusion), kind=kLoop, calls=%fused_computation.23 | loop fusion | flops 20970496 | bytes 16793600 | tf_op jit(solution)/shard_map/vmap()/reduce_sum | solution.py:39
  51.1 4.2 %fusion.19 = f32[2,128,4,128]{1,3,2,0:T(8,128)S(1)} fusion(bf16[2,4096,128,1]{2,1,3,0:T(8,128)(2,1)S(1)} %bitcast.260, f32[2,128,4,4096]{3,1,2,0:T(8,128)S(1)} %get-tuple-element.33, f32[2,128,4]{1,2,0:T(4,128)S(1)} %get-tuple-element.32, pred[2,4096]{1,0:T(4,128)(4,1)S(1)} %broadcast_compare_fusion), kind=kOutput, calls=%fused_computation.32 | convolution fusion | flops 1094713344 | bytes 19410944 | tf_op jit(solution)/shard_map/vmap(sgl,ld->sgd)/dot_general | solution.py:40
  55.3 1.0 copy.172
  56.6 1.1 reduce-window.36
  58.2 3.7 %gather_fusion.5 = bf16[32,2,128,128]{3,2,1,0:T(8,128)(2,1)S(1)} fusion(bf16[2,96,128,128]{3,2,1,0:T(8,128)(2,1)} %bitcast.254, s32[1024]{0:T(1024)S(1)} %pad_clamp_fusion.2), kind=kCustom, calls=%fused_computation.5 | custom fusion | bytes 4194432 | tf_op jit(solution)/shard_map/jit(_take)/gather | solution.py:117
  62.5 0.8 copy-done.6
  64.2 0.7 fusion.43
  66.0 1.0 convolution_bitcast_fusion.1
  67.0 0.9 convolution_bitcast_fusion
  67.9 1.7 pad_maximum_fusion
  69.6 4.8 %all-to-all-start = ((f32[4,128,1280]{2,1,0:T(8,128)}), f32[4,128,1280]{2,1,0:T(8,128)}, u32[]{:S(2)}, u32[]{:S(2)}) async-start(f32[4,128,1280]{2,1,0:T(8,128)} %bitcast.250), calls=%async_computation | async-start | bytes 5242880 | tf_op jit(solution)/shard_map/all_to_all | solution.py:156
  74.6 4.5 %fusion.170 = (f32[128,4]{1,0:T(8,128)S(1)}, f32[128,4,128]{2,1,0:T(4,128)S(1)}) fusion(bf16[128,4,128]{2,1,0:T(4,128)(2,1)S(1)} %reshape.719, bf16[2,128,1,128,128]{4,3,1,2,0:T(8,128)(2,1)} %bitcast.277, pred[128,128]{1,0:T(8,128)(4,1)S(1)} %iota_compare_fusion.7), kind=kOutput, calls=%fused_computation.295 | convolution fusion | flops 16973312 | bytes 4605952 | tf_op jit(solution)/shard_map/rgd,rtd->rgt/dot_general | solution.py:178
  79.7 0.8 fusion.117
  80.9 25.0 %all-to-all-done = f32[4,128,1280]{2,1,0:T(8,128)} async-done(((f32[4,128,1280]{2,1,0:T(8,128)}), f32[4,128,1280]{2,1,0:T(8,128)}, u32[]{:S(2)}, u32[]{:S(2)}) %all-to-all-start) | async-done | bytes 2621472 | tf_op jit(solution)/shard_map/all_to_all | solution.py:156
  105.9 2.0 reduce_sum.160
  109.2 3.2 fusion.67
  112.7 0.7 fusion.109
  113.9 31.2 %all_to_all.45 = bf16[8,128,512]{2,1,0:T(8,128)(2,1)S(1)} all-to-all(bf16[8,128,512]{2,1,0:T(8,128)(2,1)S(1)} %bitcast.256), channel_id=1, replica_groups=mesh['dp'=4,'mp'=8] {'mp'}, dimensions={0} | all-to-all | bytes 2097152 | tf_op jit(solution)/shard_map/all_to_all | solution.py:235
  145.3 1.1 broadcast_in_dim.255
  146.4 3.6 all-to-all-start.2
  151.6 1.4 scatter_custom_fusion.2
  153.1 22.4 %all-to-all-done.2 = bf16[8,128,512]{2,1,0:T(8,128)(2,1)S(1)} async-done(((bf16[8,128,512]{2,1,0:T(8,128)(2,1)}), bf16[8,128,512]{2,1,0:T(8,128)(2,1)S(1)}, u32[]{:S(2)}, u32[]{:S(2)}) %all-to-all-start.2) | async-done | bytes 1048608 | tf_op jit(solution)/shard_map/all_to_all | solution.py:240
  176.9 4.4 %gather_fusion.6 = bf16[512,4096]{1,0:T(8,128)(2,1)} fusion(bf16[129,4096]{1,0:T(8,128)(2,1)S(1)} %concatenate.26, s32[1024]{0:T(1024)S(1)} %pad_clamp_fusion.1), kind=kCustom, calls=%fused_computation.6 | custom fusion | bytes 8390656 | tf_op jit(solution)/shard_map/jit(_take)/gather | solution.py:259
  181.2 2.6 copy_select_fusion
  183.9 1.7 slice_bitcast_fusion.5
  185.5 28.9 %all_to_all.46 = bf16[4,64,4096]{2,1,0:T(8,128)(2,1)} all-to-all(bf16[4,64,4096]{2,1,0:T(8,128)(2,1)S(1)} %get-tuple-element.18), channel_id=1, replica_groups=mesh['dp'=4,'mp'=8] {'dp'}, dimensions={0} | all-to-all | bytes 4194304 | tf_op jit(solution)/shard_map/all_to_all | solution.py:264
  214.4 3.6 %all-to-all-start.5 = ((bf16[4,64,4096]{2,1,0:T(8,128)(2,1)}), bf16[4,64,4096]{2,1,0:T(8,128)(2,1)S(1)}, u32[]{:S(2)}, u32[]{:S(2)}) async-start(bf16[4,64,4096]{2,1,0:T(8,128)(2,1)} %get-tuple-element.19), calls=%async_computation.6 | async-start | bytes 4194304 | tf_op jit(solution)/shard_map/all_to_all | solution.py:264
  218.3 12.3 %fusion.38 = f32[2,4,64,1024]{3,2,0,1:T(8,128)} fusion(bf16[2,2,1024,4096]{3,2,1,0:T(8,128)(2,1)} %param.27, bf16[4,64,4096]{2,1,0:T(8,128)(2,1)} %all_to_all.46), kind=kOutput, calls=%fused_computation.58 | convolution fusion | flops 4294967296 | bytes 20971520 | tf_op jit(solution)/shard_map/scd,kfd->kscf/dot_general | solution.py:273
  230.6 7.8 %fusion.24 = bf16[4,64,4096]{2,1,0:T(8,128)(2,1)} fusion(bf16[2,1024,4096]{2,1,0:T(8,128)(2,1)} %param.28, f32[2,4,64,1024]{3,2,0,1:T(8,128)} %fusion.38), kind=kOutput, calls=%fused_computation.36 | convolution fusion | flops 2150105088 | bytes 12582912 | tf_op jit(solution)/shard_map/scf,fd->scd/dot_general | solution.py:277
  238.4 5.3 %all-to-all-done.5 = bf16[4,64,4096]{2,1,0:T(8,128)(2,1)S(1)} async-done(((bf16[4,64,4096]{2,1,0:T(8,128)(2,1)}), bf16[4,64,4096]{2,1,0:T(8,128)(2,1)S(1)}, u32[]{:S(2)}, u32[]{:S(2)}) %all-to-all-start.5) | async-done | bytes 2097184 | tf_op jit(solution)/shard_map/all_to_all | solution.py:264
  243.7 10.9 %fusion.45 = f32[2,2,64,1024]{3,2,0,1:T(8,128)} fusion(bf16[2,2,1024,4096]{3,2,1,0:T(8,128)(2,1)} %param.27, bf16[4,64,4096]{2,1,0:T(8,128)(2,1)S(1)} %all-to-all-done.5), kind=kOutput, calls=%fused_computation.63 | convolution fusion | flops 2147483648 | bytes 18874368 | tf_op jit(solution)/shard_map/scd,kfd->kscf/dot_general | solution.py:273
  254.7 5.1 %fusion.27 = bf16[2,64,4096]{2,1,0:T(8,128)(2,1)S(1)} fusion(bf16[2,1024,4096]{2,1,0:T(8,128)(2,1)} %param.28, f32[2,2,64,1024]{3,2,0,1:T(8,128)} %fusion.45), kind=kOutput, calls=%fused_computation.37 | convolution fusion | flops 1075052544 | bytes 10485760 | tf_op jit(solution)/shard_map/scf,fd->scd/dot_general | solution.py:277
  259.8 1.1 copy.257
  260.9 3.8 %all-to-all-start.6 = ((bf16[2,64,8,512]{3,1,0,2:T(8,128)(2,1)}), bf16[2,64,8,512]{3,1,0,2:T(8,128)(2,1)S(1)}, u32[]{:S(2)}, u32[]{:S(2)}) async-start(bf16[2,64,8,512]{3,1,0,2:T(8,128)(2,1)} %bitcast.242), calls=%async_computation.7 | async-start | bytes 2097152 | tf_op jit(solution)/shard_map/all_to_all | solution.py:283
  264.7 12.9 %fusion.48 = f32[2,2,64,1024]{3,2,0,1:T(8,128)} fusion(bf16[2,2,1024,4096]{3,2,1,0:T(8,128)(2,1)} %param.27, bf16[4,64,4096]{2,1,0:T(8,128)(2,1)} %copy-done.4), kind=kOutput, calls=%fused_computation.64 | convolution fusion | flops 2147483648 | bytes 18874368 | tf_op jit(solution)/shard_map/scd,kfd->kscf/dot_general | solution.py:273
  277.7 5.1 %fusion.30 = bf16[2,64,4096]{2,1,0:T(8,128)(2,1)S(1)} fusion(bf16[2,1024,4096]{2,1,0:T(8,128)(2,1)} %param.28, f32[2,2,64,1024]{3,2,0,1:T(8,128)} %fusion.48), kind=kOutput, calls=%fused_computation.38 | convolution fusion | flops 1075052544 | bytes 10485760 | tf_op jit(solution)/shard_map/scf,fd->scd/dot_general | solution.py:277
  282.8 1.1 copy.256
  283.9 8.0 %all-to-all-done.6 = bf16[2,64,8,512]{3,1,0,2:T(8,128)(2,1)S(1)} async-done(((bf16[2,64,8,512]{3,1,0,2:T(8,128)(2,1)}), bf16[2,64,8,512]{3,1,0,2:T(8,128)(2,1)S(1)}, u32[]{:S(2)}, u32[]{:S(2)}) %all-to-all-start.6) | async-done | bytes 1048608 | tf_op jit(solution)/shard_map/all_to_all | solution.py:283
  291.8 3.7 %all-to-all-start.7 = ((bf16[2,64,8,512]{3,1,0,2:T(8,128)(2,1)}), bf16[2,64,8,512]{3,1,0,2:T(8,128)(2,1)S(1)}, u32[]{:S(2)}, u32[]{:S(2)}) async-start(bf16[2,64,8,512]{3,1,0,2:T(8,128)(2,1)} %bitcast.241), calls=%async_computation.8 | async-start | bytes 2097152 | tf_op jit(solution)/shard_map/all_to_all | solution.py:283
  296.5 33.4 %all-to-all-done.7 = bf16[2,64,8,512]{3,1,0,2:T(8,128)(2,1)S(1)} async-done(((bf16[2,64,8,512]{3,1,0,2:T(8,128)(2,1)}), bf16[2,64,8,512]{3,1,0,2:T(8,128)(2,1)S(1)}, u32[]{:S(2)}, u32[]{:S(2)}) %all-to-all-start.7) | async-done | bytes 1048608 | tf_op jit(solution)/shard_map/all_to_all | solution.py:283
  330.1 0.8 pad_maximum_fusion.2
  330.8 3.4 all-to-all-start.8
  334.3 5.9 %all-to-all-done.8 = bf16[4,64,512]{2,1,0:T(8,128)(2,1)S(1)} async-done(((bf16[4,64,512]{2,1,0:T(8,128)(2,1)}), bf16[4,64,512]{2,1,0:T(8,128)(2,1)S(1)}, u32[]{:S(2)}, u32[]{:S(2)}) %all-to-all-start.8) | async-done | bytes 262176 | tf_op jit(solution)/shard_map/all_to_all | solution.py:295
  340.2 3.4 all-to-all-start.4
  343.8 5.9 %all-to-all-done.4 = bf16[4,64,512]{2,1,0:T(8,128)(2,1)S(1)} async-done(((bf16[4,64,512]{2,1,0:T(8,128)(2,1)}), bf16[4,64,512]{2,1,0:T(8,128)(2,1)S(1)}, u32[]{:S(2)}, u32[]{:S(2)}) %all-to-all-start.4) | async-done | bytes 262176 | tf_op jit(solution)/shard_map/all_to_all | solution.py:295
  349.7 1.2 gather_fusion.7
  351.0 0.8 multiply_reduce_fusion
  (151 shorter events, 18.2 us)
Async XLA Ops:
  6.5 17.6 %copy-start = (bf16[128,4096]{1,0:T(8,128)(2,1)S(1)}, bf16[128,4096]{1,0:T(8,128)(2,1)}, u32[]{:S(2)}) copy-start(bf16[128,4096]{1,0:T(8,128)(2,1)} %param.21) | copy-start | bytes 3145732
  32.8 9.3 %copy-start.5 = (bf16[512,512]{1,0:T(8,128)(2,1)}, bf16[512,512]{1,0:T(8,128)(2,1)S(1)}, u32[]{:S(2)}) copy-start(bf16[512,512]{1,0:T(8,128)(2,1)S(1)} %all_gather.3) | copy-start | bytes 1572868
  62.2 1.0 copy-start.6
  64.9 1.0 copy-start.3
  69.6 4.9 %copy-start.11 = (s32[128]{0:T(128)S(1)}, s32[128]{0:T(128)}, u32[]{:S(2)}) copy-start(s32[128]{0:T(128)} %param.40) | copy-start | bytes 1540
  69.6 36.2 %all-to-all-start = ((f32[4,128,1280]{2,1,0:T(8,128)}), f32[4,128,1280]{2,1,0:T(8,128)}, u32[]{:S(2)}, u32[]{:S(2)}) async-start(f32[4,128,1280]{2,1,0:T(8,128)} %bitcast.250), calls=%async_computation | async-start | bytes 5242880 | tf_op jit(solution)/shard_map/all_to_all | solution.py:156
  109.2 3.5 copy-start.2
  112.7 0.9 copy-start.7
  145.1 4.8 %copy-start.10 = (s32[128,2]{0,1:T(2,128)S(1)}, s32[128,2]{0,1:T(2,128)}, u32[]{:S(2)}) copy-start(s32[128,2]{0,1:T(2,128)} %param.41) | copy-start | bytes 3076
  146.4 29.1 %all-to-all-start.2 = ((bf16[8,128,512]{2,1,0:T(8,128)(2,1)}), bf16[8,128,512]{2,1,0:T(8,128)(2,1)S(1)}, u32[]{:S(2)}, u32[]{:S(2)}) async-start(bf16[8,128,512]{2,1,0:T(8,128)(2,1)} %broadcast_in_dim.255), calls=%async_computation.2 | async-start | bytes 2097152 | tf_op jit(solution)/shard_map/all_to_all | solution.py:240
  175.8 0.7 copy-start.9
  214.4 29.3 %all-to-all-start.5 = ((bf16[4,64,4096]{2,1,0:T(8,128)(2,1)}), bf16[4,64,4096]{2,1,0:T(8,128)(2,1)S(1)}, u32[]{:S(2)}, u32[]{:S(2)}) async-start(bf16[4,64,4096]{2,1,0:T(8,128)(2,1)} %get-tuple-element.19), calls=%async_computation.6 | async-start | bytes 4194304 | tf_op jit(solution)/shard_map/all_to_all | solution.py:264
  218.1 122.2 %reduce-scatter.2.cloned.1.call-start = ((), (), s32[]{:S(2)}) async-start(), calls=%async_computation.10 | async-start | bytes 2359296 | tf_op jit(solution)/shard_map/reduce_scatter | solution.py:291
  243.7 10.9 %copy-start.4 = (bf16[4,64,4096]{2,1,0:T(8,128)(2,1)}, bf16[4,64,4096]{2,1,0:T(8,128)(2,1)S(1)}, u32[]{:S(2)}) copy-start(bf16[4,64,4096]{2,1,0:T(8,128)(2,1)S(1)} %all-to-all-done.5) | copy-start | bytes 6291460
  260.9 31.0 %all-to-all-start.6 = ((bf16[2,64,8,512]{3,1,0,2:T(8,128)(2,1)}), bf16[2,64,8,512]{3,1,0,2:T(8,128)(2,1)S(1)}, u32[]{:S(2)}, u32[]{:S(2)}) async-start(bf16[2,64,8,512]{3,1,0,2:T(8,128)(2,1)} %bitcast.242), calls=%async_computation.7 | async-start | bytes 2097152 | tf_op jit(solution)/shard_map/all_to_all | solution.py:283
  282.8 13.1 %copy-start.8 = (bf16[4096,8]{0,1:T(8,128)(2,1)S(1)}, bf16[4096,8]{0,1:T(8,128)(2,1)}, u32[]{:S(2)}) copy-start(bf16[4096,8]{0,1:T(8,128)(2,1)} %param.26) | copy-start | bytes 196612
  291.8 38.1 %all-to-all-start.7 = ((bf16[2,64,8,512]{3,1,0,2:T(8,128)(2,1)}), bf16[2,64,8,512]{3,1,0,2:T(8,128)(2,1)S(1)}, u32[]{:S(2)}, u32[]{:S(2)}) async-start(bf16[2,64,8,512]{3,1,0,2:T(8,128)(2,1)} %bitcast.241), calls=%async_computation.8 | async-start | bytes 2097152 | tf_op jit(solution)/shard_map/all_to_all | solution.py:283
  330.8 9.4 %all-to-all-start.8 = ((bf16[4,64,512]{2,1,0:T(8,128)(2,1)}), bf16[4,64,512]{2,1,0:T(8,128)(2,1)S(1)}, u32[]{:S(2)}, u32[]{:S(2)}) async-start(bf16[4,64,512]{2,1,0:T(8,128)(2,1)} %pad_maximum_fusion.2), calls=%async_computation.9 | async-start | bytes 524288 | tf_op jit(solution)/shard_map/all_to_all | solution.py:295
  340.2 9.4 %all-to-all-start.4 = ((bf16[4,64,512]{2,1,0:T(8,128)(2,1)}), bf16[4,64,512]{2,1,0:T(8,128)(2,1)S(1)}, u32[]{:S(2)}, u32[]{:S(2)}) async-start(bf16[4,64,512]{2,1,0:T(8,128)(2,1)} %reduce-scatter.2.cloned.1.call-done), calls=%async_computation.5 | async-start | bytes 524288 | tf_op jit(solution)/shard_map/all_to_all | solution.py:295
  349.6 2.9 copy-start.1
Sparse Core Ops, SparseCore 0:
  238.5 89.7 reduce-scatter.1

commit v2 on v0

--- a/solution.py
+++ b/solution.py
@@ -152,24 +152,44 @@
     branch_rows = level_rows(local_branches, branch_pages, branch_len, BR_CAP)
     groups = group_size
     dp_count = lax.axis_size("dp")
-    packed = jnp.concatenate([root_rows, branch_rows], axis=1)
+    stats = jnp.concatenate(
+        [root_rows[:, groups * head_width : (groups * head_width + 2 * groups)],
+         branch_rows[:, groups * head_width : (groups * head_width + 2 * groups)]],
+        axis=1,
+    )
+    stats_high = lax.reduce_precision(stats, exponent_bits=8, mantissa_bits=7)
+    stats_rest = stats - stats_high
+    stats_mid = lax.reduce_precision(stats_rest, exponent_bits=8, mantissa_bits=7)
+    stats_low = stats_rest - stats_mid
+    stat_block = jnp.concatenate([stats_high, stats_mid, stats_low], axis=1).astype(jnp.bfloat16)
+    stat_block = jnp.pad(stat_block, ((0, 0), (0, head_width - stat_block.shape[1])))
+    packed = jnp.concatenate(
+        [root_rows[:, : groups * head_width].astype(jnp.bfloat16),
+         branch_rows[:, : groups * head_width].astype(jnp.bfloat16),
+         stat_block],
+        axis=1,
+    )
     exchanged = lax.all_to_all(
-        packed.reshape(dp_count, local_rows, (2 * groups + 2) * head_width),
+        packed.reshape(dp_count, local_rows, packed.shape[1]),
         "dp",
         split_axis=0,
         concat_axis=0,
         tiled=True,
     )
-    gathered = jnp.sum(exchanged, axis=0).reshape(local_rows, 2 * groups + 2, head_width)
-    root_stats = gathered[:, groups]
-    branch_stats = gathered[:, 2 * groups + 1]
+    gathered = jnp.sum(exchanged.astype(jnp.float32), axis=0)
+    sum_width = groups * head_width
+    stat_width = 4 * groups
+    stat_parts = gathered[:, 2 * sum_width :]
+    joined = (
+        stat_parts[:, :stat_width] + stat_parts[:, stat_width : 2 * stat_width]
+    ) + stat_parts[:, 2 * stat_width : 3 * stat_width]
     returned = (
-        gathered[:, :groups],
-        root_stats[:, :groups],
-        root_stats[:, groups : 2 * groups],
-        gathered[:, groups + 1 : 2 * groups + 1],
-        branch_stats[:, :groups],
-        branch_stats[:, groups : 2 * groups],
+        gathered[:, :sum_width].reshape(local_rows, groups, head_width),
+        joined[:, :groups],
+        joined[:, groups : 2 * groups],
+        gathered[:, sum_width : 2 * sum_width].reshape(local_rows, groups, head_width),
+        joined[:, 2 * groups : 3 * groups],
+        joined[:, 3 * groups : 4 * groups],
     )
     leaf_block = leaf_cache[:, :, 0]
     mine_queries = group_queries.reshape(local_rows, group_size, head_width)

time: 358 us -> 340 us (0.950)
  waiting for transfers between devices: 121 us -> 106 us
    all_to_all x1, waiting for transfers between devices: 25 us -> 9.45 us  [shards(): lax.all_to_all(packed.reshape(dp_count, local_rows, packed.shape[1]), 'dp...]
    unnamed x30 -> x41, local copies, waits for them, and re-layouts: 16.1 us -> 15.7 us
  transfers between devices with their start and end apart: 8 -> 8, of which waited for: 7 -> 7; matrix products, arithmetic and copies ran while one was open for 20% -> 21% of each run, Pallas kernels for 0% -> 0%
where the time goes in v2:
time: 340 us; the launch traced here: 334 us
  waiting for transfers between devices  106 us (31%)
  matrix products  58.9 us (17%)
  local copies, waits for them, and re-layouts  55.2 us (16%)
  blocking collectives  39.9 us (12%)
  other arithmetic  33.9 us (10%)
  starting transfers between devices  25.3 us (7%)
  between operations  14.7 us (4%)
    all_to_all x1, waiting for transfers between devices, shards(): lax.all_to_all(pieces, 'mp', split_axis=0, concat_axis=0, tiled=True)  50.7 us
    all_to_all x1, blocking collectives, shards(): lax.all_to_all(terms, 'mp', split_axis=0, concat_axis=0, tiled=True)  31.2 us
    dot_general x2, matrix products, shards(): jnp.einsum('scd,kfd->kscf', incoming, expert_in[expert_index], preferred_...  24 us
    all_to_all x1, waiting for transfers between devices, shards(): lax.all_to_all(spread_cols, 'mp', split_axis=0, concat_axis=0, tiled=True)  22.4 us
    unnamed x41, local copies, waits for them, and re-layouts  15.7 us
    all_to_all x2, waiting for transfers between devices, shards(): lax.all_to_all(summed, 'dp', split_axis=0, concat_axis=0, tiled=True)  11.8 us
    all_to_all x2, waiting for transfers between devices, shards(): lax.all_to_all(outgoing[:, expert_index], 'dp', split_axis=0, concat_axis...  11.3 us
    gather x2, local copies, waits for them, and re-layouts, level_rows(): jnp.take(page_pool, page_list.reshape(-1), axis=1)  9.71 us
  transfers between devices with their start and end apart: 8, of which 7 were waited for; matrix products, arithmetic and copies ran while one was open for 21% of the time, Pallas kernels for 0%

profile of v2, /device:TPU:0, one launch (start us, length us, event | category | flops | bytes accessed | tf_op | source)
XLA Modules:
  0.0 333.6 jit_solution(5277343488953882324)
XLA Ops:
  6.5 0.7 fusion.128
  7.3 1.3 fusion.129
  8.6 0.7 fusion.126
  9.2 1.4 fusion.127
  10.9 0.8 scatter_custom_fusion.1
  12.0 0.7 fusion.122
  13.5 0.7 fusion.123
  14.2 1.3 gather_fusion
  15.5 0.7 broadcast_select_fusion.4
  16.2 1.2 gather_fusion.1
  17.7 0.9 select_reduce_fusion
  18.6 0.7 select_reduce_fusion.1
  20.6 8.6 %all_gather.3 = bf16[512,512]{1,0:T(8,128)(2,1)S(1)} all-gather(bf16[128,512]{1,0:T(8,128)(2,1)S(1)} %constant_dynamic-slice_fusion), channel_id=1, replica_groups=mesh['dp'=4,'mp'=8] {'dp'}, dimensions={0}, use_global_device_ids=true | all-gather | bytes 655360 | tf_op jit(solution)/shard_map/all_gather | solution.py:85
  29.3 6.0 %gather_fusion.2 = bf16[64,2,128,128]{3,2,1,0:T(8,128)(2,1)} fusion(bf16[2,96,128,128]{3,2,1,0:T(8,128)(2,1)} %bitcast.227, s32[1024]{0:T(1024)S(1)} %pad_clamp_fusion.4), kind=kCustom, calls=%fused_computation.2 | custom fusion | bytes 8388864 | tf_op jit(solution)/shard_map/jit(_take)/gather | solution.py:117
  35.3 2.6 select_bitcast_fusion
  38.5 0.7 fusion.38
  39.2 2.8 fusion.6
  42.0 5.1 %fusion.7 = f32[2,128,4]{1,2,0:T(4,128)S(1)} fusion(f32[2,128,4,4096]{3,1,2,0:T(8,128)S(1)} %get-tuple-element.37, f32[2,128,4]{1,2,0:T(4,128)S(1)} %get-tuple-element.36, pred[2,4096]{1,0:T(4,128)(4,1)S(1)} %broadcast_compare_fusion), kind=kLoop, calls=%fused_computation.20 | loop fusion | flops 20970496 | bytes 16793600 | tf_op jit(solution)/shard_map/vmap()/reduce_sum | solution.py:39
  47.1 4.2 %fusion.12 = f32[2,128,4,128]{1,3,2,0:T(8,128)S(1)} fusion(bf16[2,4096,128,1]{2,1,3,0:T(8,128)(2,1)S(1)} %bitcast.232, f32[2,128,4,4096]{3,1,2,0:T(8,128)S(1)} %get-tuple-element.37, f32[2,128,4]{1,2,0:T(4,128)S(1)} %get-tuple-element.36, pred[2,4096]{1,0:T(4,128)(4,1)S(1)} %broadcast_compare_fusion), kind=kOutput, calls=%fused_computation.25 | convolution fusion | flops 1094713344 | bytes 19410944 | tf_op jit(solution)/shard_map/vmap(sgl,ld->sgd)/dot_general | solution.py:40
  51.7 1.0 convolution_bitcast_fusion.1
  52.7 0.8 slice.288
  54.3 1.3 broadcast_select_fusion.3
  56.9 0.7 broadcast_compare_fusion.2
  57.6 1.1 reduce-window.36
  59.2 3.7 %gather_fusion.5 = bf16[32,2,128,128]{3,2,1,0:T(8,128)(2,1)S(1)} fusion(bf16[2,96,128,128]{3,2,1,0:T(8,128)(2,1)} %bitcast.228, s32[1024]{0:T(1024)S(1)} %pad_clamp_fusion.2), kind=kCustom, calls=%fused_computation.5 | custom fusion | bytes 4194432 | tf_op jit(solution)/shard_map/jit(_take)/gather | solution.py:117
  65.3 0.7 fusion.35
  66.8 0.9 convolution_bitcast_fusion
  68.8 1.1 fusion.37
  69.9 3.7 %all-to-all-start = ((bf16[4,128,1152]{2,1,0:T(8,128)(2,1)}), bf16[4,128,1152]{2,1,0:T(8,128)(2,1)S(1)}, u32[]{:S(2)}, u32[]{:S(2)}) async-start(bf16[4,128,1152]{2,1,0:T(8,128)(2,1)} %bitcast.33), calls=%async_computation | async-start | bytes 2359296 | tf_op jit(solution)/shard_map/all_to_all | solution.py:172
  73.8 4.5 %fusion.155 = (f32[128,4]{1,0:T(8,128)S(1)}, f32[128,4,128]{2,1,0:T(4,128)S(1)}) fusion(bf16[128,4,128]{2,1,0:T(4,128)(2,1)S(1)} %reshape.716, bf16[2,128,1,128,128]{4,3,1,2,0:T(8,128)(2,1)} %bitcast.247, pred[128,128]{1,0:T(8,128)(4,1)S(1)} %iota_compare_fusion.8), kind=kOutput, calls=%fused_computation.288 | convolution fusion | flops 16973312 | bytes 4605952 | tf_op jit(solution)/shard_map/rgd,rtd->rgt/dot_general | solution.py:198
  78.8 0.8 fusion.102
  80.0 9.5 %all-to-all-done = bf16[4,128,1152]{2,1,0:T(8,128)(2,1)S(1)} async-done(((bf16[4,128,1152]{2,1,0:T(8,128)(2,1)}), bf16[4,128,1152]{2,1,0:T(8,128)(2,1)S(1)}, u32[]{:S(2)}, u32[]{:S(2)}) %all-to-all-start) | async-done | bytes 1179680 | tf_op jit(solution)/shard_map/all_to_all | solution.py:172
  91.0 3.2 fusion.55
  94.4 0.7 fusion.93
  95.6 31.2 %all_to_all.40 = bf16[8,128,512]{2,1,0:T(8,128)(2,1)S(1)} all-to-all(bf16[8,128,512]{2,1,0:T(8,128)(2,1)S(1)} %bitcast.230), channel_id=1, replica_groups=mesh['dp'=4,'mp'=8] {'mp'}, dimensions={0} | all-to-all | bytes 2097152 | tf_op jit(solution)/shard_map/all_to_all | solution.py:255
  127.1 1.1 broadcast_in_dim.255
  128.1 3.6 %all-to-all-start.2 = ((bf16[8,128,512]{2,1,0:T(8,128)(2,1)}), bf16[8,128,512]{2,1,0:T(8,128)(2,1)S(1)}, u32[]{:S(2)}, u32[]{:S(2)}) async-start(bf16[8,128,512]{2,1,0:T(8,128)(2,1)} %broadcast_in_dim.255), calls=%async_computation.2 | async-start | bytes 2097152 | tf_op jit(solution)/shard_map/all_to_all | solution.py:260
  133.3 1.4 scatter_custom_fusion.2
  134.9 22.4 %all-to-all-done.2 = bf16[8,128,512]{2,1,0:T(8,128)(2,1)S(1)} async-done(((bf16[8,128,512]{2,1,0:T(8,128)(2,1)}), bf16[8,128,512]{2,1,0:T(8,128)(2,1)S(1)}, u32[]{:S(2)}, u32[]{:S(2)}) %all-to-all-start.2) | async-done | bytes 1048608 | tf_op jit(solution)/shard_map/all_to_all | solution.py:260
  158.7 4.4 %gather_fusion.6 = bf16[512,4096]{1,0:T(8,128)(2,1)} fusion(bf16[129,4096]{1,0:T(8,128)(2,1)S(1)} %concatenate.32, s32[1024]{0:T(1024)S(1)} %pad_clamp_fusion.1), kind=kCustom, calls=%fused_computation.6 | custom fusion | bytes 8390656 | tf_op jit(solution)/shard_map/jit(_take)/gather | solution.py:279
  163.0 2.6 copy_select_fusion
  165.6 2.5 slice_bitcast_fusion.5
  168.1 3.6 %all-to-all-start.3 = ((bf16[4,64,4096]{2,1,0:T(8,128)(2,1)}), bf16[4,64,4096]{2,1,0:T(8,128)(2,1)S(1)}, u32[]{:S(2)}, u32[]{:S(2)}) async-start(bf16[4,64,4096]{2,1,0:T(8,128)(2,1)} %get-tuple-element.18), calls=%async_computation.3 | async-start | bytes 4194304 | tf_op jit(solution)/shard_map/all_to_all | solution.py:284
  171.7 7.7 %slice.159 = bf16[1,1024,4096]{2,1,0:T(8,128)(2,1)} slice(bf16[2,1024,4096]{2,1,0:T(8,128)(2,1)} %param.28), slice={[1:2], [0:1024], [0:4096]} | slice | bytes 16777216 | tf_op jit(solution)/shard_map/slice | solution.py:294
  179.4 12.0 %copy.253 = bf16[1,1024,4096]{1,2,0:T(8,128)(2,1)} copy(bf16[1,1024,4096]{2,1,0:T(8,128)(2,1)} %slice.159) | data formatting | bytes 16777216
  191.4 6.0 %all-to-all-done.3 = bf16[4,64,4096]{2,1,0:T(8,128)(2,1)S(1)} async-done(((bf16[4,64,4096]{2,1,0:T(8,128)(2,1)}), bf16[4,64,4096]{2,1,0:T(8,128)(2,1)S(1)}, u32[]{:S(2)}, u32[]{:S(2)}) %all-to-all-start.3) | async-done | bytes 2097184 | tf_op jit(solution)/shard_map/all_to_all | solution.py:284
  197.4 1.4 copy-done.4
  198.8 3.6 %all-to-all-start.5 = ((bf16[4,64,4096]{2,1,0:T(8,128)(2,1)}), bf16[4,64,4096]{2,1,0:T(8,128)(2,1)S(1)}, u32[]{:S(2)}, u32[]{:S(2)}) async-start(bf16[4,64,4096]{2,1,0:T(8,128)(2,1)} %get-tuple-element.19), calls=%async_computation.6 | async-start | bytes 4194304 | tf_op jit(solution)/shard_map/all_to_all | solution.py:284
  202.7 12.2 %fusion.25 = f32[2,4,64,1024]{3,2,0,1:T(8,128)} fusion(bf16[2,2,1024,4096]{3,2,1,0:T(8,128)(2,1)} %param.27, bf16[4,64,4096]{2,1,0:T(8,128)(2,1)} %copy-done.4), kind=kOutput, calls=%fused_computation.51 | convolution fusion | flops 4294967296 | bytes 20971520 | tf_op jit(solution)/shard_map/scd,kfd->kscf/dot_general | solution.py:287
  214.9 7.8 %fusion.15 = bf16[4,64,4096]{2,1,0:T(8,128)(2,1)} fusion(bf16[2,1024,4096]{2,1,0:T(8,128)(2,1)} %param.28, f32[2,4,64,1024]{3,2,0,1:T(8,128)} %fusion.25), kind=kOutput, calls=%fused_computation.27 | convolution fusion | flops 2150105088 | bytes 12582912 | tf_op jit(solution)/shard_map/scf,fd->scd/dot_general | solution.py:300
  222.8 5.3 %all-to-all-done.5 = bf16[4,64,4096]{2,1,0:T(8,128)(2,1)S(1)} async-done(((bf16[4,64,4096]{2,1,0:T(8,128)(2,1)}), bf16[4,64,4096]{2,1,0:T(8,128)(2,1)S(1)}, u32[]{:S(2)}, u32[]{:S(2)}) %all-to-all-start.5) | async-done | bytes 2097184 | tf_op jit(solution)/shard_map/all_to_all | solution.py:284
  228.1 11.8 %fusion.30 = f32[2,4,64,1024]{3,2,0,1:T(8,128)} fusion(bf16[2,2,1024,4096]{3,2,1,0:T(8,128)(2,1)} %param.27, bf16[4,64,4096]{2,1,0:T(8,128)(2,1)S(1)} %all-to-all-done.5), kind=kOutput, calls=%fused_computation.52 | convolution fusion | flops 4294967296 | bytes 20971520 | tf_op jit(solution)/shard_map/scd,kfd->kscf/dot_general | solution.py:287
  239.8 6.8 %convert_bitcast_fusion.1 = bf16[8,4,64,512]{3,2,0,1:T(8,128)(2,1)S(1)} fusion(bf16[1024,8,512,1]{0,2,1,3:T(8,128)(2,1)} %bitcast.224, f32[2,4,64,1024]{3,2,0,1:T(8,128)} %fusion.30), kind=kOutput, calls=%fused_computation.45 | convolution fusion | flops 2150105088 | bytes 12582912 | tf_op jit(solution)/shard_map/scf,fmd->mscd/dot_general | solution.py:292
  246.7 1.5 copy.234
  248.2 3.7 %all-to-all-start.6 = ((bf16[8,4,64,512]{3,2,1,0:T(8,128)(2,1)}), bf16[8,4,64,512]{3,2,1,0:T(8,128)(2,1)S(1)}, u32[]{:S(2)}, u32[]{:S(2)}) async-start(bf16[8,4,64,512]{3,2,1,0:T(8,128)(2,1)} %copy.234), calls=%async_computation.7 | async-start | bytes 4194304 | tf_op jit(solution)/shard_map/all_to_all | solution.py:297
  252.7 50.7 %all-to-all-done.6 = bf16[8,4,64,512]{3,2,1,0:T(8,128)(2,1)S(1)} async-done(((bf16[8,4,64,512]{3,2,1,0:T(8,128)(2,1)}), bf16[8,4,64,512]{3,2,1,0:T(8,128)(2,1)S(1)}, u32[]{:S(2)}, u32[]{:S(2)}) %all-to-all-start.6) | async-done | bytes 2097184 | tf_op jit(solution)/shard_map/all_to_all | solution.py:297
  303.5 1.1 reduce_sum.157
  304.5 3.4 %all-to-all-start.7 = ((bf16[4,64,512]{2,1,0:T(8,128)(2,1)}), bf16[4,64,512]{2,1,0:T(8,128)(2,1)S(1)}, u32[]{:S(2)}, u32[]{:S(2)}) async-start(bf16[4,64,512]{2,1,0:T(8,128)(2,1)} %reduce_sum.157), calls=%async_computation.8 | async-start | bytes 524288 | tf_op jit(solution)/shard_map/all_to_all | solution.py:308
  308.0 5.9 %all-to-all-done.7 = bf16[4,64,512]{2,1,0:T(8,128)(2,1)S(1)} async-done(((bf16[4,64,512]{2,1,0:T(8,128)(2,1)}), bf16[4,64,512]{2,1,0:T(8,128)(2,1)S(1)}, u32[]{:S(2)}, u32[]{:S(2)}) %all-to-all-start.7) | async-done | bytes 262176 | tf_op jit(solution)/shard_map/all_to_all | solution.py:308
  313.9 3.4 %all-to-all-start.4 = ((bf16[4,64,512]{2,1,0:T(8,128)(2,1)}), bf16[4,64,512]{2,1,0:T(8,128)(2,1)S(1)}, u32[]{:S(2)}, u32[]{:S(2)}) async-start(bf16[4,64,512]{2,1,0:T(8,128)(2,1)} %reduce-scatter.2.cloned.1.call-done), calls=%async_computation.5 | async-start | bytes 524288 | tf_op jit(solution)/shard_map/all_to_all | solution.py:308
  317.5 5.9 %all-to-all-done.4 = bf16[4,64,512]{2,1,0:T(8,128)(2,1)S(1)} async-done(((bf16[4,64,512]{2,1,0:T(8,128)(2,1)}), bf16[4,64,512]{2,1,0:T(8,128)(2,1)S(1)}, u32[]{:S(2)}, u32[]{:S(2)}) %all-to-all-start.4) | async-done | bytes 262176 | tf_op jit(solution)/shard_map/all_to_all | solution.py:308
  323.5 1.2 gather_fusion.7
  324.7 0.8 multiply_reduce_fusion
  325.6 0.7 add_convert_fusion
  (169 shorter events, 18.2 us)
Async XLA Ops:
  6.5 14.1 %copy-start = (bf16[128,4096]{1,0:T(8,128)(2,1)S(1)}, bf16[128,4096]{1,0:T(8,128)(2,1)}, u32[]{:S(2)}) copy-start(bf16[128,4096]{1,0:T(8,128)(2,1)} %param.21) | copy-start | bytes 3145732
  29.3 9.2 %copy-start.6 = (bf16[512,512]{1,0:T(8,128)(2,1)}, bf16[512,512]{1,0:T(8,128)(2,1)S(1)}, u32[]{:S(2)}) copy-start(bf16[512,512]{1,0:T(8,128)(2,1)S(1)} %all_gather.3) | copy-start | bytes 1572868
  51.5 2.1 copy-start.2
  51.6 4.0 %copy-start.13 = (s32[32,4]{0,1:T(4,128)S(1)}, s32[32,4]{0,1:T(4,128)}, u32[]{:S(2)}) copy-start(s32[32,4]{0,1:T(4,128)} %param.37) | copy-start | bytes 1540
  63.3 0.6 copy-start.16
  63.3 1.0 copy-start.7
  63.3 1.0 copy-start.12
  63.3 1.3 copy-start.14
  67.7 1.0 copy-start.5
  68.8 4.8 %copy-start.15 = (s32[128]{0:T(128)S(1)}, s32[128]{0:T(128)}, u32[]{:S(2)}) copy-start(s32[128]{0:T(128)} %param.40) | copy-start | bytes 1540
  69.9 19.6 %all-to-all-start = ((bf16[4,128,1152]{2,1,0:T(8,128)(2,1)}), bf16[4,128,1152]{2,1,0:T(8,128)(2,1)S(1)}, u32[]{:S(2)}, u32[]{:S(2)}) async-start(bf16[4,128,1152]{2,1,0:T(8,128)(2,1)} %bitcast.33), calls=%async_computation | async-start | bytes 2359296 | tf_op jit(solution)/shard_map/all_to_all | solution.py:172
  91.0 3.5 %copy-start.3 = (bf16[512,4096]{1,0:T(8,128)(2,1)S(1)}, bf16[512,4096]{1,0:T(8,128)(2,1)}, u32[]{:S(2)}) copy-start(bf16[512,4096]{1,0:T(8,128)(2,1)} %param.24) | copy-start | bytes 12582916
  94.4 0.9 copy-start.8
  127.0 4.7 %copy-start.11 = (s32[128,2]{0,1:T(2,128)S(1)}, s32[128,2]{0,1:T(2,128)}, u32[]{:S(2)}) copy-start(s32[128,2]{0,1:T(2,128)} %param.41) | copy-start | bytes 3076
  128.1 29.1 %all-to-all-start.2 = ((bf16[8,128,512]{2,1,0:T(8,128)(2,1)}), bf16[8,128,512]{2,1,0:T(8,128)(2,1)S(1)}, u32[]{:S(2)}, u32[]{:S(2)}) async-start(bf16[8,128,512]{2,1,0:T(8,128)(2,1)} %broadcast_in_dim.255), calls=%async_computation.2 | async-start | bytes 2097152 | tf_op jit(solution)/shard_map/all_to_all | solution.py:260
  157.5 0.7 copy-start.10
  168.1 29.3 %all-to-all-start.3 = ((bf16[4,64,4096]{2,1,0:T(8,128)(2,1)}), bf16[4,64,4096]{2,1,0:T(8,128)(2,1)S(1)}, u32[]{:S(2)}, u32[]{:S(2)}) async-start(bf16[4,64,4096]{2,1,0:T(8,128)(2,1)} %get-tuple-element.18), calls=%async_computation.3 | async-start | bytes 4194304 | tf_op jit(solution)/shard_map/all_to_all | solution.py:284
  197.4 1.4 copy-start.4
  198.8 29.3 %all-to-all-start.5 = ((bf16[4,64,4096]{2,1,0:T(8,128)(2,1)}), bf16[4,64,4096]{2,1,0:T(8,128)(2,1)S(1)}, u32[]{:S(2)}, u32[]{:S(2)}) async-start(bf16[4,64,4096]{2,1,0:T(8,128)(2,1)} %get-tuple-element.19), calls=%async_computation.6 | async-start | bytes 4194304 | tf_op jit(solution)/shard_map/all_to_all | solution.py:284
  202.4 111.5 %reduce-scatter.2.cloned.1.call-start = ((), (), s32[]{:S(2)}) async-start(), calls=%async_computation.9 | async-start | bytes 2359296 | tf_op jit(solution)/shard_map/reduce_scatter | solution.py:304
  248.2 4.1 %copy-start.9 = (bf16[4096,8]{0,1:T(8,128)(2,1)S(1)}, bf16[4096,8]{0,1:T(8,128)(2,1)}, u32[]{:S(2)}) copy-start(bf16[4096,8]{0,1:T(8,128)(2,1)} %param.26) | copy-start | bytes 196612
  248.2 55.3 %all-to-all-start.6 = ((bf16[8,4,64,512]{3,2,1,0:T(8,128)(2,1)}), bf16[8,4,64,512]{3,2,1,0:T(8,128)(2,1)S(1)}, u32[]{:S(2)}, u32[]{:S(2)}) async-start(bf16[8,4,64,512]{3,2,1,0:T(8,128)(2,1)} %copy.234), calls=%async_computation.7 | async-start | bytes 4194304 | tf_op jit(solution)/shard_map/all_to_all | solution.py:297
  304.5 9.4 %all-to-all-start.7 = ((bf16[4,64,512]{2,1,0:T(8,128)(2,1)}), bf16[4,64,512]{2,1,0:T(8,128)(2,1)S(1)}, u32[]{:S(2)}, u32[]{:S(2)}) async-start(bf16[4,64,512]{2,1,0:T(8,128)(2,1)} %reduce_sum.157), calls=%async_computation.8 | async-start | bytes 524288 | tf_op jit(solution)/shard_map/all_to_all | solution.py:308
  313.9 9.4 %all-to-all-start.4 = ((bf16[4,64,512]{2,1,0:T(8,128)(2,1)}), bf16[4,64,512]{2,1,0:T(8,128)(2,1)S(1)}, u32[]{:S(2)}, u32[]{:S(2)}) async-start(bf16[4,64,512]{2,1,0:T(8,128)(2,1)} %reduce-scatter.2.cloned.1.call-done), calls=%async_computation.5 | async-start | bytes 524288 | tf_op jit(solution)/shard_map/all_to_all | solution.py:308
  323.4 2.9 copy-start.1
Sparse Core Ops, SparseCore 0:
  222.9 89.3 reduce-scatter.1

commit v3 on v2

--- a/solution.py
+++ b/solution.py
@@ -41,6 +41,23 @@
         pattern, weights.astype(jnp.bfloat16), values, preferred_element_type=jnp.float32
     )
     return (weighted_sum, row_max, weight_total)
+
+
+def halving_scatter(held, axis, block_axis):
+    size = lax.axis_size(axis)
+    me = lax.axis_index(axis)
+    for bit in range(size.bit_length() - 1):
+        shape = held.shape
+        split = shape[:block_axis] + (shape[block_axis] // 2, 2) + shape[block_axis + 1 :]
+        pairs = held.reshape(split)
+        even = lax.index_in_dim(pairs, 0, block_axis + 1, keepdims=False)
+        odd = lax.index_in_dim(pairs, 1, block_axis + 1, keepdims=False)
+        upper = (me >> bit) & 1 == 1
+        kept = jnp.where(upper, odd, even)
+        sent = jnp.where(upper, even, odd).astype(jnp.bfloat16)
+        received = lax.ppermute(sent, axis, [(i, i ^ (1 << bit)) for i in range(size)])
+        held = kept + received.astype(jnp.float32)
+    return lax.index_in_dim(held, 0, block_axis, keepdims=False)
 
 
 def shards(
@@ -288,19 +305,15 @@
             "scd,kfd->kscf", incoming, expert_in[expert_index], preferred_element_type=jnp.float32
         )
         expert_hidden = (jax.nn.silu(gate_up[0]) * gate_up[1]).astype(jnp.bfloat16)
+        expert_partial = jnp.einsum(
+            "scf,fd->scd", expert_hidden, expert_out[expert_index],
+            preferred_element_type=jnp.float32,
+        )
         if expert_index == local_experts - 1 and local_experts > 1:
-            pieces = jnp.einsum(
-                "scf,fmd->mscd", expert_hidden,
-                expert_out[expert_index].reshape(-1, mp_count, slice_width),
-                preferred_element_type=jnp.float32,
+            summed = halving_scatter(
+                expert_partial.reshape(dp_count, E_CAP, mp_count, slice_width), "mp", 2
             ).astype(jnp.bfloat16)
-            gathered_pieces = lax.all_to_all(pieces, "mp", split_axis=0, concat_axis=0, tiled=True)
-            summed = jnp.sum(gathered_pieces.astype(jnp.float32), axis=0).astype(jnp.bfloat16)
         else:
-            expert_partial = jnp.einsum(
-                "scf,fd->scd", expert_hidden, expert_out[expert_index],
-                preferred_element_type=jnp.float32,
-            )
             summed = lax.psum_scatter(
                 expert_partial.astype(jnp.bfloat16), "mp", scatter_dimension=2, tiled=True
             )

time: 340 us -> 354 us (1.041)
  waiting for transfers between devices: 106 us -> 118 us
  other arithmetic: 33.9 us -> 40.5 us
  matrix products: 58.9 us -> 54.6 us
    ppermute x0 -> x3, waiting for transfers between devices: none -> 62.2 us  [halving_scatter(): lax.ppermute(sent, axis, [(i, i ^ 1 << bit) for i in range(size)])]
    all_to_all x1 -> x0, waiting for transfers between devices: 50.7 us -> none  [shards(): lax.all_to_all(pieces, 'mp', split_axis=0, concat_axis=0, tiled=True)]
    dot_general x0 -> x2, local copies, waits for them, and re-layouts: none -> 19.7 us  [shards(): jnp.einsum('scf,fd->scd', expert_hidden, expert_out[expert_index], prefer...]
    unnamed x41 -> x42, local copies, waits for them, and re-layouts: 15.7 us -> 5.27 us
    slice x2, local copies, waits for them, and re-layouts: 7.92 us -> 0.43 us  [the longest x1 0.22 us: halving_scatter(): even = lax.index_in_dim(pairs, 0, block_axis + 1, keepdims=False)]
    dot_general x1 -> x0, matrix products: 6.85 us -> none  [shards(): jnp.einsum('scf,fmd->mscd', expert_hidden, expert_out[expert_index].resha...]
    dot_general x1 -> x2, matrix products: 7.81 us -> 13.6 us  [shards(): jnp.einsum('scf,fd->scd', expert_hidden, expert_out[expert_index], prefer...]
    all_to_all x1 -> x0, starting transfers between devices: 3.73 us -> none  [shards(): lax.all_to_all(pieces, 'mp', split_axis=0, concat_axis=0, tiled=True)]
  transfers between devices with their start and end apart: 8 -> 10, of which waited for: 7 -> 9; matrix products, arithmetic and copies ran while one was open for 21% -> 21% of each run, Pallas kernels for 0% -> 0%
where the time goes in v3:
time: 354 us; the launch traced here: 348 us
  waiting for transfers between devices  118 us (33%)
  local copies, waits for them, and re-layouts  55.4 us (16%)
  matrix products  54.6 us (15%)
  other arithmetic  40.5 us (11%)
  blocking collectives  39.9 us (11%)
  starting transfers between devices  24.8 us (7%)
  between operations  14.5 us (4%)
    ppermute x3, waiting for transfers between devices, halving_scatter(): lax.ppermute(sent, axis, [(i, i ^ 1 << bit) for i in range(size)])  62.2 us
    all_to_all x1, blocking collectives, shards(): lax.all_to_all(terms, 'mp', split_axis=0, concat_axis=0, tiled=True)  31.2 us
    all_to_all x1, waiting for transfers between devices, shards(): lax.all_to_all(spread_cols, 'mp', split_axis=0, concat_axis=0, tiled=True)  22.4 us
    dot_general x2, matrix products, shards(): jnp.einsum('scd,kfd->kscf', incoming, expert_in[expert_index], preferred_...  20.7 us
    dot_general x2, local copies, waits for them, and re-layouts, shards(): jnp.einsum('scf,fd->scd', expert_hidden, expert_out[expert_index], prefer...  19.7 us
    dot_general x2, matrix products, shards(): jnp.einsum('scf,fd->scd', expert_hidden, expert_out[expert_index], prefer...  13.6 us
    all_to_all x2, waiting for transfers between devices, shards(): lax.all_to_all(outgoing[:, expert_index], 'dp', split_axis=0, concat_axis...  12 us
    all_to_all x2, waiting for transfers between devices, shards(): lax.all_to_all(summed, 'dp', split_axis=0, concat_axis=0, tiled=True)  11.8 us
  transfers between devices with their start and end apart: 10, of which 9 were waited for; matrix products, arithmetic and copies ran while one was open for 21% of the time, Pallas kernels for 0%

profile of v3, /device:TPU:0, one launch (start us, length us, event | category | flops | bytes accessed | tf_op | source)
XLA Modules:
  0.0 347.5 jit_solution(1521120330103869567)
XLA Ops:
  6.5 0.7 fusion.137
  7.3 1.3 fusion.138
  9.2 1.4 fusion.136
  10.9 0.8 scatter_custom_fusion.1
  14.2 1.3 gather_fusion
  16.2 1.2 gather_fusion.1
  17.7 0.9 select_reduce_fusion
  18.6 0.7 select_reduce_fusion.1
  20.6 8.6 %all_gather.3 = bf16[512,512]{1,0:T(8,128)(2,1)S(1)} all-gather(bf16[128,512]{1,0:T(8,128)(2,1)S(1)} %constant_dynamic-slice_fusion), channel_id=1, replica_groups=mesh['dp'=4,'mp'=8] {'dp'}, dimensions={0}, use_global_device_ids=true | all-gather | bytes 655360 | tf_op jit(solution)/shard_map/all_gather | solution.py:102
  29.3 6.0 %gather_fusion.2 = bf16[64,2,128,128]{3,2,1,0:T(8,128)(2,1)} fusion(bf16[2,96,128,128]{3,2,1,0:T(8,128)(2,1)} %bitcast.270, s32[1024]{0:T(1024)S(1)} %pad_clamp_fusion.4), kind=kCustom, calls=%fused_computation.2 | custom fusion | bytes 8388864 | tf_op jit(solution)/shard_map/jit(_take)/gather | solution.py:134
  35.3 2.6 select_bitcast_fusion
  38.5 0.7 fusion.40
  39.2 2.8 fusion.6
  42.0 5.5 %fusion.7 = f32[2,128,4]{1,2,0:T(4,128)S(1)} fusion(f32[2,128,4,4096]{3,1,2,0:T(8,128)S(1)} %get-tuple-element.39, f32[2,128,4]{1,2,0:T(4,128)S(1)} %get-tuple-element.38, pred[2,4096]{1,0:T(4,128)(4,1)S(1)} %broadcast_compare_fusion), kind=kLoop, calls=%fused_computation.20 | loop fusion | flops 20970496 | bytes 16793600 | tf_op jit(solution)/shard_map/vmap()/reduce_sum | solution.py:39
  47.5 4.2 %fusion.12 = f32[2,128,4,128]{1,3,2,0:T(8,128)S(1)} fusion(bf16[2,4096,128,1]{2,1,3,0:T(8,128)(2,1)S(1)} %bitcast.275, f32[2,128,4,4096]{3,1,2,0:T(8,128)S(1)} %get-tuple-element.39, f32[2,128,4]{1,2,0:T(4,128)S(1)} %get-tuple-element.38, pred[2,4096]{1,0:T(4,128)(4,1)S(1)} %broadcast_compare_fusion), kind=kOutput, calls=%fused_computation.26 | convolution fusion | flops 1094713344 | bytes 19410944 | tf_op jit(solution)/shard_map/vmap(sgl,ld->sgd)/dot_general | solution.py:40
  52.0 1.0 convolution_bitcast_fusion.1
  53.1 0.8 slice.339
  54.6 1.3 broadcast_select_fusion.3
  58.0 1.1 reduce-window.36
  59.6 3.7 %gather_fusion.5 = bf16[32,2,128,128]{3,2,1,0:T(8,128)(2,1)S(1)} fusion(bf16[2,96,128,128]{3,2,1,0:T(8,128)(2,1)} %bitcast.271, s32[1024]{0:T(1024)S(1)} %pad_clamp_fusion.2), kind=kCustom, calls=%fused_computation.5 | custom fusion | bytes 4194432 | tf_op jit(solution)/shard_map/jit(_take)/gather | solution.py:134
  65.6 0.7 fusion.37
  67.2 0.9 convolution_bitcast_fusion
  69.1 1.1 fusion.39
  70.2 3.7 %all-to-all-start = ((bf16[4,128,1152]{2,1,0:T(8,128)(2,1)}), bf16[4,128,1152]{2,1,0:T(8,128)(2,1)S(1)}, u32[]{:S(2)}, u32[]{:S(2)}) async-start(bf16[4,128,1152]{2,1,0:T(8,128)(2,1)} %bitcast.33), calls=%async_computation | async-start | bytes 2359296 | tf_op jit(solution)/shard_map/all_to_all | solution.py:189
  74.1 4.5 %fusion.165 = (f32[128,4]{1,0:T(8,128)S(1)}, f32[128,4,128]{2,1,0:T(4,128)S(1)}) fusion(bf16[128,4,128]{2,1,0:T(4,128)(2,1)S(1)} %reshape.783, bf16[2,128,1,128,128]{4,3,1,2,0:T(8,128)(2,1)} %bitcast.290, pred[128,128]{1,0:T(8,128)(4,1)S(1)} %iota_compare_fusion.8), kind=kOutput, calls=%fused_computation.304 | convolution fusion | flops 16973312 | bytes 4605952 | tf_op jit(solution)/shard_map/rgd,rtd->rgt/dot_general | solution.py:215
  79.1 0.8 fusion.111
  80.3 9.5 %all-to-all-done = bf16[4,128,1152]{2,1,0:T(8,128)(2,1)S(1)} async-done(((bf16[4,128,1152]{2,1,0:T(8,128)(2,1)}), bf16[4,128,1152]{2,1,0:T(8,128)(2,1)S(1)}, u32[]{:S(2)}, u32[]{:S(2)}) %all-to-all-start) | async-done | bytes 1179680 | tf_op jit(solution)/shard_map/all_to_all | solution.py:189
  91.3 3.2 fusion.59
  94.8 0.7 fusion.102
  95.9 31.2 %all_to_all.35 = bf16[8,128,512]{2,1,0:T(8,128)(2,1)S(1)} all-to-all(bf16[8,128,512]{2,1,0:T(8,128)(2,1)S(1)} %bitcast.273), channel_id=1, replica_groups=mesh['dp'=4,'mp'=8] {'mp'}, dimensions={0} | all-to-all | bytes 2097152 | tf_op jit(solution)/shard_map/all_to_all | solution.py:272
  127.4 1.1 broadcast_in_dim.255
  128.4 3.6 %all-to-all-start.2 = ((bf16[8,128,512]{2,1,0:T(8,128)(2,1)}), bf16[8,128,512]{2,1,0:T(8,128)(2,1)S(1)}, u32[]{:S(2)}, u32[]{:S(2)}) async-start(bf16[8,128,512]{2,1,0:T(8,128)(2,1)} %broadcast_in_dim.255), calls=%async_computation.2 | async-start | bytes 2097152 | tf_op jit(solution)/shard_map/all_to_all | solution.py:277
  133.6 1.4 scatter_custom_fusion.2
  135.2 22.4 %all-to-all-done.2 = bf16[8,128,512]{2,1,0:T(8,128)(2,1)S(1)} async-done(((bf16[8,128,512]{2,1,0:T(8,128)(2,1)}), bf16[8,128,512]{2,1,0:T(8,128)(2,1)S(1)}, u32[]{:S(2)}, u32[]{:S(2)}) %all-to-all-start.2) | async-done | bytes 1048608 | tf_op jit(solution)/shard_map/all_to_all | solution.py:277
  159.0 4.4 %gather_fusion.6 = bf16[512,4096]{1,0:T(8,128)(2,1)} fusion(bf16[129,4096]{1,0:T(8,128)(2,1)S(1)} %concatenate.32, s32[1024]{0:T(1024)S(1)} %pad_clamp_fusion.1), kind=kCustom, calls=%fused_computation.6 | custom fusion | bytes 8390656 | tf_op jit(solution)/shard_map/jit(_take)/gather | solution.py:296
  163.3 2.6 copy_select_fusion
  166.0 2.5 slice_bitcast_fusion.6
  168.4 3.6 %all-to-all-start.3 = ((bf16[4,64,4096]{2,1,0:T(8,128)(2,1)}), bf16[4,64,4096]{2,1,0:T(8,128)(2,1)S(1)}, u32[]{:S(2)}, u32[]{:S(2)}) async-start(bf16[4,64,4096]{2,1,0:T(8,128)(2,1)} %get-tuple-element.18), calls=%async_computation.3 | async-start | bytes 4194304 | tf_op jit(solution)/shard_map/all_to_all | solution.py:301
  172.0 7.7 %slice_bitcast_fusion = bf16[4096,1024]{0,1:T(8,128)(2,1)} fusion(bf16[2,1024,4096]{2,1,0:T(8,128)(2,1)} %param.28), kind=kLoop, calls=%fused_computation.24 | loop fusion | bytes 16777216 | tf_op jit(solution)/shard_map/scf,fd->scd/dot_general | solution.py:308
  179.8 12.0 %copy.259 = bf16[4096,1024]{1,0:T(8,128)(2,1)} copy(bf16[4096,1024]{0,1:T(8,128)(2,1)} %slice_bitcast_fusion) | data formatting | bytes 16777216 | tf_op jit(solution)/shard_map/scf,fd->scd/dot_general | solution.py:308
  191.7 6.0 %all-to-all-done.3 = bf16[4,64,4096]{2,1,0:T(8,128)(2,1)S(1)} async-done(((bf16[4,64,4096]{2,1,0:T(8,128)(2,1)}), bf16[4,64,4096]{2,1,0:T(8,128)(2,1)S(1)}, u32[]{:S(2)}, u32[]{:S(2)}) %all-to-all-start.3) | async-done | bytes 2097184 | tf_op jit(solution)/shard_map/all_to_all | solution.py:301
  197.7 4.5 %all-to-all-start.5 = ((bf16[4,64,4096]{2,1,0:T(8,128)(2,1)}), bf16[4,64,4096]{2,1,0:T(8,128)(2,1)}, u32[]{:S(2)}, u32[]{:S(2)}) async-start(bf16[4,64,4096]{2,1,0:T(8,128)(2,1)} %get-tuple-element.19), calls=%async_computation.6 | async-start | bytes 4194304 | tf_op jit(solution)/shard_map/all_to_all | solution.py:301
  202.5 11.7 %fusion.27 = f32[2,4,64,1024]{3,2,0,1:T(8,128)} fusion(bf16[2,2,1024,4096]{3,2,1,0:T(8,128)(2,1)} %param.27, bf16[4,64,4096]{2,1,0:T(8,128)(2,1)S(1)} %all-to-all-done.3), kind=kOutput, calls=%fused_computation.55 | convolution fusion | flops 4294967296 | bytes 20971520 | tf_op jit(solution)/shard_map/scd,kfd->kscf/dot_general | solution.py:304
  214.1 7.8 %fusion.15 = bf16[4,64,4096]{2,1,0:T(8,128)(2,1)} fusion(bf16[2,1024,4096]{2,1,0:T(8,128)(2,1)} %param.28, f32[2,4,64,1024]{3,2,0,1:T(8,128)} %fusion.27), kind=kOutput, calls=%fused_computation.28 | convolution fusion | flops 2150105088 | bytes 12582912 | tf_op jit(solution)/shard_map/scf,fd->scd/dot_general | solution.py:308
  221.9 6.0 %all-to-all-done.5 = bf16[4,64,4096]{2,1,0:T(8,128)(2,1)} async-done(((bf16[4,64,4096]{2,1,0:T(8,128)(2,1)}), bf16[4,64,4096]{2,1,0:T(8,128)(2,1)}, u32[]{:S(2)}, u32[]{:S(2)}) %all-to-all-start.5) | async-done | bytes 2097184 | tf_op jit(solution)/shard_map/all_to_all | solution.py:301
  228.0 9.0 %fusion.32 = f32[2,4,64,1024]{3,2,0,1:T(8,128)S(1)} fusion(bf16[2,2,1024,4096]{3,2,1,0:T(8,128)(2,1)} %param.27, bf16[4,64,4096]{2,1,0:T(8,128)(2,1)} %all-to-all-done.5), kind=kOutput, calls=%fused_computation.56 | convolution fusion | flops 4294967296 | bytes 20971520 | tf_op jit(solution)/shard_map/scd,kfd->kscf/dot_general | solution.py:304
  237.0 5.8 %fusion.65 = f32[4,64,4,2,512]{4,1,3,2,0:T(8,128)S(1)} fusion(bf16[4,2,512,1024,1]{3,2,1,0,4:T(8,128)(2,1)} %bitcast.266, f32[2,4,64,1024]{3,2,0,1:T(8,128)S(1)} %fusion.32), kind=kOutput, calls=%fused_computation.104 | convolution fusion | flops 2149056512 | bytes 14680064 | tf_op jit(solution)/shard_map/scf,fd->scd/dot_general | solution.py:308
  242.9 1.9 copy-done.3
  245.0 1.5 collective-permute-start
  246.4 29.1 %collective-permute-done = bf16[4,64,4,512]{3,1,2,0:T(8,128)(2,1)S(1)} collective-permute-done((bf16[4,64,4,512]{3,1,2,0:T(8,128)(2,1)S(1)}, bf16[4,64,4,512]{3,1,2,0:T(8,128)(2,1)S(1)}, u32[]{:S(2)}, u32[]{:S(2)}) %collective-permute-start) | collective-permute-done | bytes 1048608 | tf_op jit(solution)/shard_map/ppermute | solution.py:58
  275.5 2.8 fusion.23
  278.6 0.9 fusion.64
  279.7 20.6 %collective-permute-done.1 = bf16[4,64,2,512]{3,1,0,2:T(8,128)(2,1)} collective-permute-done((bf16[4,64,2,512]{3,1,0,2:T(8,128)(2,1)}, bf16[4,64,2,512]{3,1,0,2:T(8,128)(2,1)}, u32[]{:S(2)}, u32[]{:S(2)}) %collective-permute-start.1) | collective-permute-done | bytes 524320 | tf_op jit(solution)/shard_map/ppermute | solution.py:58
  300.3 1.3 fusion.52
  301.6 1.0 copy-done.4
  302.6 0.9 collective-permute-start.2
  304.1 12.5 %collective-permute-done.2 = bf16[4,64,1,512]{3,1,0,2:T(8,128)(2,1)S(1)} collective-permute-done((bf16[4,64,1,512]{3,1,0,2:T(8,128)(2,1)S(1)}, bf16[4,64,1,512]{3,1,0,2:T(8,128)(2,1)S(1)}, u32[]{:S(2)}, u32[]{:S(2)}) %collective-permute-start.2) | collective-permute-done | bytes 262176 | tf_op jit(solution)/shard_map/ppermute | solution.py:58
  316.6 2.1 fusion.84
  318.6 3.4 all-to-all-start.6
  322.1 5.9 %all-to-all-done.6 = bf16[4,64,512]{2,1,0:T(8,128)(2,1)S(1)} async-done(((bf16[4,64,512]{2,1,0:T(8,128)(2,1)}), bf16[4,64,512]{2,1,0:T(8,128)(2,1)S(1)}, u32[]{:S(2)}, u32[]{:S(2)}) %all-to-all-start.6) | async-done | bytes 262176 | tf_op jit(solution)/shard_map/all_to_all | solution.py:321
  328.1 3.4 all-to-all-start.4
  331.6 5.9 %all-to-all-done.4 = bf16[4,64,512]{2,1,0:T(8,128)(2,1)S(1)} async-done(((bf16[4,64,512]{2,1,0:T(8,128)(2,1)}), bf16[4,64,512]{2,1,0:T(8,128)(2,1)S(1)}, u32[]{:S(2)}, u32[]{:S(2)}) %all-to-all-start.4) | async-done | bytes 262176 | tf_op jit(solution)/shard_map/all_to_all | solution.py:321
  337.6 1.2 gather_fusion.7
  338.8 0.8 multiply_reduce_fusion
  (180 shorter events, 22.7 us)
Async XLA Ops:
  6.5 14.1 %copy-start = (bf16[128,4096]{1,0:T(8,128)(2,1)S(1)}, bf16[128,4096]{1,0:T(8,128)(2,1)}, u32[]{:S(2)}) copy-start(bf16[128,4096]{1,0:T(8,128)(2,1)} %param.21) | copy-start | bytes 3145732
  29.3 9.2 %copy-start.7 = (bf16[512,512]{1,0:T(8,128)(2,1)}, bf16[512,512]{1,0:T(8,128)(2,1)S(1)}, u32[]{:S(2)}) copy-start(bf16[512,512]{1,0:T(8,128)(2,1)S(1)} %all_gather.3) | copy-start | bytes 1572868
  51.9 2.1 copy-start.2
  51.9 4.0 %copy-start.14 = (s32[32,4]{0,1:T(4,128)S(1)}, s32[32,4]{0,1:T(4,128)}, u32[]{:S(2)}) copy-start(s32[32,4]{0,1:T(4,128)} %param.37) | copy-start | bytes 1540
  63.6 0.6 copy-start.17
  63.6 1.0 copy-start.8
  63.6 1.0 copy-start.13
  63.6 1.3 copy-start.15
  68.1 1.0 copy-start.6
  69.1 4.8 %copy-start.16 = (s32[128]{0:T(128)S(1)}, s32[128]{0:T(128)}, u32[]{:S(2)}) copy-start(s32[128]{0:T(128)} %param.40) | copy-start | bytes 1540
  70.2 19.5 %all-to-all-start = ((bf16[4,128,1152]{2,1,0:T(8,128)(2,1)}), bf16[4,128,1152]{2,1,0:T(8,128)(2,1)S(1)}, u32[]{:S(2)}, u32[]{:S(2)}) async-start(bf16[4,128,1152]{2,1,0:T(8,128)(2,1)} %bitcast.33), calls=%async_computation | async-start | bytes 2359296 | tf_op jit(solution)/shard_map/all_to_all | solution.py:189
  91.3 3.5 copy-start.5
  94.8 0.9 copy-start.9
  127.3 4.7 %copy-start.12 = (s32[128,2]{0,1:T(2,128)S(1)}, s32[128,2]{0,1:T(2,128)}, u32[]{:S(2)}) copy-start(s32[128,2]{0,1:T(2,128)} %param.41) | copy-start | bytes 3076
  128.4 29.1 %all-to-all-start.2 = ((bf16[8,128,512]{2,1,0:T(8,128)(2,1)}), bf16[8,128,512]{2,1,0:T(8,128)(2,1)S(1)}, u32[]{:S(2)}, u32[]{:S(2)}) async-start(bf16[8,128,512]{2,1,0:T(8,128)(2,1)} %broadcast_in_dim.255), calls=%async_computation.2 | async-start | bytes 2097152 | tf_op jit(solution)/shard_map/all_to_all | solution.py:277
  157.9 0.7 copy-start.11
  168.4 29.3 %all-to-all-start.3 = ((bf16[4,64,4096]{2,1,0:T(8,128)(2,1)}), bf16[4,64,4096]{2,1,0:T(8,128)(2,1)S(1)}, u32[]{:S(2)}, u32[]{:S(2)}) async-start(bf16[4,64,4096]{2,1,0:T(8,128)(2,1)} %get-tuple-element.18), calls=%async_computation.3 | async-start | bytes 4194304 | tf_op jit(solution)/shard_map/all_to_all | solution.py:301
  197.7 30.2 %all-to-all-start.5 = ((bf16[4,64,4096]{2,1,0:T(8,128)(2,1)}), bf16[4,64,4096]{2,1,0:T(8,128)(2,1)}, u32[]{:S(2)}, u32[]{:S(2)}) async-start(bf16[4,64,4096]{2,1,0:T(8,128)(2,1)} %get-tuple-element.19), calls=%async_computation.6 | async-start | bytes 4194304 | tf_op jit(solution)/shard_map/all_to_all | solution.py:301
  202.2 125.9 %reduce-scatter.2.cloned.1.call-start = ((), (), s32[]{:S(2)}) async-start(), calls=%async_computation.8 | async-start | bytes 2359296 | tf_op jit(solution)/shard_map/reduce_scatter | solution.py:317
  242.8 1.9 copy-start.3
  245.0 30.6 %collective-permute-start = (bf16[4,64,4,512]{3,1,2,0:T(8,128)(2,1)S(1)}, bf16[4,64,4,512]{3,1,2,0:T(8,128)(2,1)S(1)}, u32[]{:S(2)}, u32[]{:S(2)}) collective-permute-start(bf16[4,64,4,512]{3,1,2,0:T(8,128)(2,1)S(1)} %fusion.49), channel_id=1, source_target_pairs={{0,1},{1,0},{2,3},{3,2},{4,5},{5,4},{6,7},{7,6},{8,9},{9,8},{10,11... | collective-permute-start | bytes 3145736 | tf_op jit(solution)/shard_map/ppermute | solution.py:58
  279.4 20.8 %collective-permute-start.1 = (bf16[4,64,2,512]{3,1,0,2:T(8,128)(2,1)}, bf16[4,64,2,512]{3,1,0,2:T(8,128)(2,1)}, u32[]{:S(2)}, u32[]{:S(2)}) collective-permute-start(bf16[4,64,2,512]{3,1,0,2:T(8,128)(2,1)} %fusion.64), channel_id=1, source_target_pairs={{0,2},{1,3},{2,0},{3,1},{4,6},{5,7},{6,4},{7,5},{8,10},{9,11},{10,... | collective-permute-start | bytes 1572872 | tf_op jit(solution)/shard_map/ppermute | solution.py:58
  279.7 24.0 %copy-start.10 = (bf16[4096,8]{0,1:T(8,128)(2,1)S(1)}, bf16[4096,8]{0,1:T(8,128)(2,1)}, u32[]{:S(2)}) copy-start(bf16[4096,8]{0,1:T(8,128)(2,1)} %param.26) | copy-start | bytes 196612
  301.6 1.0 copy-start.4
  302.6 14.0 %collective-permute-start.2 = (bf16[4,64,1,512]{3,1,0,2:T(8,128)(2,1)S(1)}, bf16[4,64,1,512]{3,1,0,2:T(8,128)(2,1)S(1)}, u32[]{:S(2)}, u32[]{:S(2)}) collective-permute-start(bf16[4,64,1,512]{3,1,0,2:T(8,128)(2,1)S(1)} %fusion.83), channel_id=1, source_target_pairs={{0,4},{1,5},{2,6},{3,7},{4,0},{5,1},{6,2},{7,3},{8,12},{9,13},{10,... | collective-permute-start | bytes 786440 | tf_op jit(solution)/shard_map/ppermute | solution.py:58
  318.6 9.4 %all-to-all-start.6 = ((bf16[4,64,512]{2,1,0:T(8,128)(2,1)}), bf16[4,64,512]{2,1,0:T(8,128)(2,1)S(1)}, u32[]{:S(2)}, u32[]{:S(2)}) async-start(bf16[4,64,512]{2,1,0:T(8,128)(2,1)} %fusion.84), calls=%async_computation.7 | async-start | bytes 524288 | tf_op jit(solution)/shard_map/all_to_all | solution.py:321
  328.1 9.4 %all-to-all-start.4 = ((bf16[4,64,512]{2,1,0:T(8,128)(2,1)}), bf16[4,64,512]{2,1,0:T(8,128)(2,1)S(1)}, u32[]{:S(2)}, u32[]{:S(2)}) async-start(bf16[4,64,512]{2,1,0:T(8,128)(2,1)} %reduce-scatter.2.cloned.1.call-done), calls=%async_computation.5 | async-start | bytes 524288 | tf_op jit(solution)/shard_map/all_to_all | solution.py:321
  337.5 2.9 copy-start.1
Sparse Core Ops, SparseCore 0:
  222.1 75.0 reduce-scatter.1

commit v4 on v2

--- a/solution.py
+++ b/solution.py
@@ -82,9 +82,14 @@
     group_queries = lax.dynamic_slice_in_dim(
         queries, kv_head * group_size * head_width, group_size * head_width, 1
     )
-    all_queries = lax.all_gather(group_queries, "dp", axis=0, tiled=True).reshape(
-        requests, group_size, head_width
-    )
+    dp_count = lax.axis_size("dp")
+    all_queries = lax.all_to_all(
+        jnp.broadcast_to(group_queries[None], (dp_count,) + group_queries.shape),
+        "dp",
+        split_axis=0,
+        concat_axis=0,
+        tiled=True,
+    ).reshape(requests, group_size, head_width)
     slot_branch = jnp.sum(
         jnp.where(
             slot_request[:, None] == jnp.arange(requests)[None, :], request_branch[None, :], 0
@@ -304,10 +309,10 @@
             summed = lax.psum_scatter(
                 expert_partial.astype(jnp.bfloat16), "mp", scatter_dimension=2, tiled=True
             )
-        returned_parts.append(
-            lax.all_to_all(summed, "dp", split_axis=0, concat_axis=0, tiled=True)
-        )
-    returned_rows = jnp.stack(returned_parts, axis=1)
+        returned_parts.append(summed)
+    returned_rows = lax.all_to_all(
+        jnp.stack(returned_parts, axis=1), "dp", split_axis=0, concat_axis=0, tiled=True
+    )
     results = jnp.take(returned_rows.reshape(-1, slice_width), pair_slot, axis=0).reshape(
         local_rows, TOP, slice_width
     )

time: 340 us -> 349 us (1.026); the launches traced: 334 us -> 347 us
  waiting for transfers between devices: 106 us -> 118 us
  starting transfers between devices: 25.3 us -> 35.1 us
  blocking collectives: 39.9 us -> 32 us
  other arithmetic: 33.9 us -> 28.7 us
    reduce_scatter x1, waiting for transfers between devices: 0.01 us -> 20.6 us  [shards(): lax.psum_scatter(expert_partial.astype(jnp.bfloat16), 'mp', scatter_dimen...]
    all_gather x1 -> x0, blocking collectives: 8.62 us -> none  [shards(): lax.all_gather(group_queries, 'dp', axis=0, tiled=True)]
    reduce_scatter x1, starting transfers between devices: 0.29 us -> 8.79 us  [shards(): lax.psum_scatter(expert_partial.astype(jnp.bfloat16), 'mp', scatter_dimen...]
    all_to_all x2, waiting for transfers between devices: 11.3 us -> 6.01 us  [shards(): lax.all_to_all(outgoing[:, expert_index], 'dp', split_axis=0, concat_axis...]
    unnamed x41 -> x47, local copies, waits for them, and re-layouts: 15.7 us -> 16.9 us
  transfers between devices with their start and end apart: 8 -> 8, of which waited for: 7 -> 6; matrix products, arithmetic and copies ran while one was open for 21% -> 28% of each run, Pallas kernels for 0% -> 0%
where the time goes in v4:
time: 349 us; the launch traced here: 347 us
  waiting for transfers between devices  118 us (34%)
  matrix products  61.3 us (18%)
  local copies, waits for them, and re-layouts  58 us (17%)
  starting transfers between devices  35.1 us (10%)
  blocking collectives  32 us (9%)
  other arithmetic  28.7 us (8%)
  between operations  14.4 us (4%)
    all_to_all x1, waiting for transfers between devices, shards(): lax.all_to_all(pieces, 'mp', split_axis=0, concat_axis=0, tiled=True)  50.4 us
    all_to_all x1, blocking collectives, shards(): lax.all_to_all(terms, 'mp', split_axis=0, concat_axis=0, tiled=True)  32 us
    dot_general x2, matrix products, shards(): jnp.einsum('scd,kfd->kscf', incoming, expert_in[expert_index], preferred_...  23.8 us
    all_to_all x1, waiting for transfers between devices, shards(): lax.all_to_all(spread_cols, 'mp', split_axis=0, concat_axis=0, tiled=True)  22.4 us
    reduce_scatter x1, waiting for transfers between devices, shards(): lax.psum_scatter(expert_partial.astype(jnp.bfloat16), 'mp', scatter_dimen...  20.6 us
    unnamed x47, local copies, waits for them, and re-layouts  16.9 us
    gather x2, local copies, waits for them, and re-layouts, level_rows(): jnp.take(page_pool, page_list.reshape(-1), axis=1)  9.53 us
    all_to_all x1, waiting for transfers between devices, shards(): lax.all_to_all(packed.reshape(dp_count, local_rows, packed.shape[1]), 'dp...  9.51 us
  transfers between devices with their start and end apart: 8, of which 6 were waited for; matrix products, arithmetic and copies ran while one was open for 28% of the time, Pallas kernels for 0%

profile of v4, /device:TPU:0, one launch (start us, length us, event | category | flops | bytes accessed | tf_op | source)
XLA Modules:
  0.0 347.0 jit_solution(15742058655420201985)
XLA Ops:
  6.6 1.2 copy-done
  7.8 0.9 broadcast_in_dim.244
  8.6 4.2 %all-to-all-start = ((bf16[4,128,512]{2,1,0:T(8,128)(2,1)}), bf16[4,128,512]{2,1,0:T(8,128)(2,1)}, u32[]{:S(2)}, u32[]{:S(2)}) async-start(bf16[4,128,512]{2,1,0:T(8,128)(2,1)} %broadcast_in_dim.244), calls=%async_computation | async-start | bytes 1048576 | tf_op jit(solution)/shard_map/all_to_all | solution.py:86
  12.8 0.7 fusion.126
  13.5 1.3 fusion.127
  14.8 0.7 fusion.124
  15.4 1.4 fusion.125
  17.1 0.8 scatter_custom_fusion.1
  18.2 0.7 fusion.120
  19.7 0.7 fusion.121
  21.0 0.7 broadcast_select_fusion.4
  22.6 0.6 gather_fusion.3
  23.2 0.7 broadcast_select_fusion.3
  26.5 1.1 reduce-window.36
  28.1 5.8 %gather_fusion.2 = bf16[64,2,128,128]{3,2,1,0:T(8,128)(2,1)} fusion(bf16[2,96,128,128]{3,2,1,0:T(8,128)(2,1)} %bitcast.227, s32[1024]{0:T(1024)S(1)} %pad_clamp_fusion.4), kind=kCustom, calls=%fused_computation.2 | custom fusion | bytes 8388864 | tf_op jit(solution)/shard_map/jit(_take)/gather | solution.py:122
  33.9 3.7 %gather_fusion.5 = bf16[32,2,128,128]{3,2,1,0:T(8,128)(2,1)S(1)} fusion(bf16[2,96,128,128]{3,2,1,0:T(8,128)(2,1)} %bitcast.228, s32[1024]{0:T(1024)S(1)} %pad_clamp_fusion.2), kind=kCustom, calls=%fused_computation.5 | custom fusion | bytes 4194432 | tf_op jit(solution)/shard_map/jit(_take)/gather | solution.py:122
  38.0 1.1 fusion.150
  39.2 1.4 copy-done.4
  41.2 1.8 fusion.149
  43.0 1.8 fusion.38
  44.8 2.8 fusion.6
  47.6 4.9 %fusion.7 = f32[2,128,4]{1,2,0:T(4,128)S(1)} fusion(f32[2,128,4,4096]{3,1,2,0:T(8,128)S(1)} %get-tuple-element.37, f32[2,128,4]{1,2,0:T(4,128)S(1)} %get-tuple-element.36, pred[2,4096]{1,0:T(4,128)(4,1)S(1)} %broadcast_compare_fusion), kind=kLoop, calls=%fused_computation.20 | loop fusion | flops 20970496 | bytes 16793600 | tf_op jit(solution)/shard_map/vmap()/reduce_sum | solution.py:39
  52.5 4.4 %fusion.12 = f32[2,128,4,128]{1,3,2,0:T(8,128)S(1)} fusion(bf16[2,4096,128,1]{2,1,3,0:T(8,128)(2,1)S(1)} %bitcast.232, f32[2,128,4,4096]{3,1,2,0:T(8,128)S(1)} %get-tuple-element.37, f32[2,128,4]{1,2,0:T(4,128)S(1)} %get-tuple-element.36, pred[2,4096]{1,0:T(4,128)(4,1)S(1)} %broadcast_compare_fusion), kind=kOutput, calls=%fused_computation.25 | convolution fusion | flops 1094713344 | bytes 19410944 | tf_op jit(solution)/shard_map/vmap(sgl,ld->sgd)/dot_general | solution.py:40
  57.3 1.0 convolution_bitcast_fusion.1
  58.4 1.7 fusion.39
  60.7 0.7 fusion.35
  62.3 0.9 convolution_bitcast_fusion
  63.7 1.1 fusion.37
  64.8 4.2 %all-to-all-start.1 = ((bf16[4,128,1152]{2,1,0:T(8,128)(2,1)}), bf16[4,128,1152]{2,1,0:T(8,128)(2,1)S(1)}, u32[]{:S(2)}, u32[]{:S(2)}) async-start(bf16[4,128,1152]{2,1,0:T(8,128)(2,1)} %bitcast.35), calls=%async_computation.1 | async-start | bytes 2359296 | tf_op jit(solution)/shard_map/all_to_all | solution.py:177
  69.1 4.5 %fusion.153 = (f32[128,4]{1,0:T(8,128)S(1)}, f32[128,4,128]{2,1,0:T(4,128)S(1)}) fusion(bf16[128,4,128]{2,1,0:T(4,128)(2,1)S(1)} %reshape.717, bf16[2,128,1,128,128]{4,3,1,2,0:T(8,128)(2,1)} %bitcast.247, pred[128,128]{1,0:T(8,128)(4,1)S(1)} %iota_compare_fusion.8), kind=kOutput, calls=%fused_computation.286 | convolution fusion | flops 16973312 | bytes 4605952 | tf_op jit(solution)/shard_map/rgd,rtd->rgt/dot_general | solution.py:203
  74.2 0.8 fusion.100
  75.3 9.5 %all-to-all-done.1 = bf16[4,128,1152]{2,1,0:T(8,128)(2,1)S(1)} async-done(((bf16[4,128,1152]{2,1,0:T(8,128)(2,1)}), bf16[4,128,1152]{2,1,0:T(8,128)(2,1)S(1)}, u32[]{:S(2)}, u32[]{:S(2)}) %all-to-all-start.1) | async-done | bytes 1179680 | tf_op jit(solution)/shard_map/all_to_all | solution.py:177
  86.4 3.2 fusion.55
  89.8 0.7 fusion.91
  91.0 32.0 %all_to_all.40 = bf16[8,128,512]{2,1,0:T(8,128)(2,1)S(1)} all-to-all(bf16[8,128,512]{2,1,0:T(8,128)(2,1)S(1)} %bitcast.230), channel_id=1, replica_groups=mesh['dp'=4,'mp'=8] {'mp'}, dimensions={0} | all-to-all | bytes 2097152 | tf_op jit(solution)/shard_map/all_to_all | solution.py:260
  123.2 1.1 broadcast_in_dim.262
  124.2 3.6 %all-to-all-start.3 = ((bf16[8,128,512]{2,1,0:T(8,128)(2,1)}), bf16[8,128,512]{2,1,0:T(8,128)(2,1)S(1)}, u32[]{:S(2)}, u32[]{:S(2)}) async-start(bf16[8,128,512]{2,1,0:T(8,128)(2,1)} %broadcast_in_dim.262), calls=%async_computation.3 | async-start | bytes 2097152 | tf_op jit(solution)/shard_map/all_to_all | solution.py:265
  129.4 1.4 scatter_custom_fusion.2
  131.0 22.4 %all-to-all-done.3 = bf16[8,128,512]{2,1,0:T(8,128)(2,1)S(1)} async-done(((bf16[8,128,512]{2,1,0:T(8,128)(2,1)}), bf16[8,128,512]{2,1,0:T(8,128)(2,1)S(1)}, u32[]{:S(2)}, u32[]{:S(2)}) %all-to-all-start.3) | async-done | bytes 1048608 | tf_op jit(solution)/shard_map/all_to_all | solution.py:265
  154.8 4.4 %gather_fusion.6 = bf16[512,4096]{1,0:T(8,128)(2,1)} fusion(bf16[129,4096]{1,0:T(8,128)(2,1)S(1)} %concatenate.32, s32[1024]{0:T(1024)S(1)} %pad_clamp_fusion.1), kind=kCustom, calls=%fused_computation.6 | custom fusion | bytes 8390656 | tf_op jit(solution)/shard_map/jit(_take)/gather | solution.py:284
  159.1 2.6 copy_select_fusion
  161.8 2.5 slice_bitcast_fusion.5
  164.2 3.6 %all-to-all-start.4 = ((bf16[4,64,4096]{2,1,0:T(8,128)(2,1)}), bf16[4,64,4096]{2,1,0:T(8,128)(2,1)S(1)}, u32[]{:S(2)}, u32[]{:S(2)}) async-start(bf16[4,64,4096]{2,1,0:T(8,128)(2,1)} %get-tuple-element.18), calls=%async_computation.4 | async-start | bytes 4194304 | tf_op jit(solution)/shard_map/all_to_all | solution.py:289
  167.8 7.7 %slice.159 = bf16[1,1024,4096]{2,1,0:T(8,128)(2,1)} slice(bf16[2,1024,4096]{2,1,0:T(8,128)(2,1)} %param.28), slice={[1:2], [0:1024], [0:4096]} | slice | bytes 16777216 | tf_op jit(solution)/shard_map/slice | solution.py:299
  175.6 12.0 %copy.253 = bf16[1,1024,4096]{1,2,0:T(8,128)(2,1)} copy(bf16[1,1024,4096]{2,1,0:T(8,128)(2,1)} %slice.159) | data formatting | bytes 16777216
  187.5 6.0 %all-to-all-done.4 = bf16[4,64,4096]{2,1,0:T(8,128)(2,1)S(1)} async-done(((bf16[4,64,4096]{2,1,0:T(8,128)(2,1)}), bf16[4,64,4096]{2,1,0:T(8,128)(2,1)S(1)}, u32[]{:S(2)}, u32[]{:S(2)}) %all-to-all-start.4) | async-done | bytes 2097184 | tf_op jit(solution)/shard_map/all_to_all | solution.py:289
  193.5 1.4 copy-done.7
  194.9 3.6 %all-to-all-start.5 = ((bf16[4,64,4096]{2,1,0:T(8,128)(2,1)}), bf16[4,64,4096]{2,1,0:T(8,128)(2,1)S(1)}, u32[]{:S(2)}, u32[]{:S(2)}) async-start(bf16[4,64,4096]{2,1,0:T(8,128)(2,1)} %get-tuple-element.19), calls=%async_computation.6 | async-start | bytes 4194304 | tf_op jit(solution)/shard_map/all_to_all | solution.py:289
  198.5 8.8 %reduce-scatter.2.cloned.1.call-start = ((), (), s32[]{:S(2)}) async-start(), calls=%async_computation.9 | async-start | bytes 2359296 | tf_op jit(solution)/shard_map/reduce_scatter | solution.py:309
  207.3 12.2 %fusion.25 = f32[2,4,64,1024]{3,2,0,1:T(8,128)} fusion(bf16[2,2,1024,4096]{3,2,1,0:T(8,128)(2,1)} %param.27, bf16[4,64,4096]{2,1,0:T(8,128)(2,1)} %copy-done.7), kind=kOutput, calls=%fused_computation.51 | convolution fusion | flops 4294967296 | bytes 20971520 | tf_op jit(solution)/shard_map/scd,kfd->kscf/dot_general | solution.py:292
  219.5 7.8 %fusion.15 = bf16[4,64,4096]{2,1,0:T(8,128)(2,1)} fusion(bf16[2,1024,4096]{2,1,0:T(8,128)(2,1)} %param.28, f32[2,4,64,1024]{3,2,0,1:T(8,128)} %fusion.25), kind=kOutput, calls=%fused_computation.27 | convolution fusion | flops 2150105088 | bytes 12582912 | tf_op jit(solution)/shard_map/scf,fd->scd/dot_general | solution.py:305
  227.4 11.6 %fusion.30 = f32[2,4,64,1024]{3,2,0,1:T(8,128)} fusion(bf16[2,2,1024,4096]{3,2,1,0:T(8,128)(2,1)} %param.27, bf16[4,64,4096]{2,1,0:T(8,128)(2,1)S(1)} %all-to-all-done.5), kind=kOutput, calls=%fused_computation.52 | convolution fusion | flops 4294967296 | bytes 20971520 | tf_op jit(solution)/shard_map/scd,kfd->kscf/dot_general | solution.py:292
  239.0 6.7 %convert_bitcast_fusion.1 = bf16[8,4,64,512]{3,2,0,1:T(8,128)(2,1)S(1)} fusion(bf16[1024,8,512,1]{0,2,1,3:T(8,128)(2,1)} %bitcast.224, f32[2,4,64,1024]{3,2,0,1:T(8,128)} %fusion.30), kind=kOutput, calls=%fused_computation.45 | convolution fusion | flops 2150105088 | bytes 12582912 | tf_op jit(solution)/shard_map/scf,fmd->mscd/dot_general | solution.py:297
  245.7 1.5 copy.234
  247.1 3.7 %all-to-all-start.6 = ((bf16[8,4,64,512]{3,2,1,0:T(8,128)(2,1)}), bf16[8,4,64,512]{3,2,1,0:T(8,128)(2,1)S(1)}, u32[]{:S(2)}, u32[]{:S(2)}) async-start(bf16[8,4,64,512]{3,2,1,0:T(8,128)(2,1)} %copy.234), calls=%async_computation.7 | async-start | bytes 4194304 | tf_op jit(solution)/shard_map/all_to_all | solution.py:302
  251.7 50.4 %all-to-all-done.6 = bf16[8,4,64,512]{3,2,1,0:T(8,128)(2,1)S(1)} async-done(((bf16[8,4,64,512]{3,2,1,0:T(8,128)(2,1)}), bf16[8,4,64,512]{3,2,1,0:T(8,128)(2,1)S(1)}, u32[]{:S(2)}, u32[]{:S(2)}) %all-to-all-start.6) | async-done | bytes 2097184 | tf_op jit(solution)/shard_map/all_to_all | solution.py:302
  302.4 20.6 %reduce-scatter.2.cloned.1.call-done = bf16[4,64,512]{2,1,0:T(8,128)(2,1)} async-done(((bf16[4,64,4096]{2,1,0:T(8,128)(2,1)}), bf16[4,64,512]{2,1,0:T(8,128)(2,1)}) %reduce-scatter.2.cloned.1.call-update) | async-done | bytes 262160 | tf_op jit(solution)/shard_map/reduce_scatter | solution.py:309
  323.0 1.0 pad_maximum_fusion
  324.0 0.8 copy.235
  324.8 3.5 all-to-all-start.7
  328.5 8.6 %all-to-all-done.7 = bf16[4,2,64,512]{3,2,1,0:T(8,128)(2,1)S(1)} async-done(((bf16[4,2,64,512]{3,2,1,0:T(8,128)(2,1)}), bf16[4,2,64,512]{3,2,1,0:T(8,128)(2,1)S(1)}, u32[]{:S(2)}, u32[]{:S(2)}) %all-to-all-start.7) | async-done | bytes 524320 | tf_op jit(solution)/shard_map/all_to_all | solution.py:313
  337.1 1.2 gather_fusion.7
  338.4 0.8 multiply_reduce_fusion
  339.2 0.7 add_convert_fusion
  (176 shorter events, 16.9 us)
Async XLA Ops:
  6.5 1.2 copy-start
  6.5 13.9 %copy-start.2 = (s32[8]{0:T(128)S(1)}, s32[8]{0:T(128)}, u32[]{:S(2)}) copy-start(s32[8]{0:T(128)} %param.38) | copy-start | bytes 100
  6.5 15.2 %copy-start.14 = (s32[8,32]{1,0:T(8,128)S(1)}, s32[8,32]{1,0:T(8,128)}, u32[]{:S(2)}) copy-start(s32[8,32]{1,0:T(8,128)} %param.36) | copy-start | bytes 3076
  6.5 16.0 %copy-start.3 = (s32[32]{0:T(128)S(1)}, s32[32]{0:T(128)}, u32[]{:S(2)}) copy-start(s32[32]{0:T(128)} %param.39) | copy-start | bytes 388
  6.5 17.3 %copy-start.15 = (s32[32,4]{0,1:T(4,128)S(1)}, s32[32,4]{0,1:T(4,128)}, u32[]{:S(2)}) copy-start(s32[32,4]{0,1:T(4,128)} %param.37) | copy-start | bytes 1540
  6.5 18.2 %copy-start.17 = (s32[512]{0:T(512)S(1)}, s32[512]{0:T(512)}, u32[]{:S(2)}) copy-start(s32[512]{0:T(512)} %param.31) | copy-start | bytes 6148
  6.6 18.2 %copy-start.16 = (s32[512]{0:T(512)S(1)}, s32[512]{0:T(512)}, u32[]{:S(2)}) copy-start(s32[512]{0:T(512)} %param.32) | copy-start | bytes 6148
  6.6 18.5 %copy-start.18 = (s32[32]{0:T(128)S(1)}, s32[32]{0:T(128)}, u32[]{:S(2)}) copy-start(s32[32]{0:T(128)} %param.33) | copy-start | bytes 388
  8.6 34.4 %all-to-all-start = ((bf16[4,128,512]{2,1,0:T(8,128)(2,1)}), bf16[4,128,512]{2,1,0:T(8,128)(2,1)}, u32[]{:S(2)}, u32[]{:S(2)}) async-start(bf16[4,128,512]{2,1,0:T(8,128)(2,1)} %broadcast_in_dim.244), calls=%async_computation | async-start | bytes 1048576 | tf_op jit(solution)/shard_map/all_to_all | solution.py:86
  38.0 2.6 copy-start.4
  47.6 4.9 %copy-start.8 = (bf16[1,64,128,128]{3,2,0,1:T(8,128)(2,1)S(1)}, bf16[1,64,128,128]{3,2,0,1:T(8,128)(2,1)}, u32[]{:S(2)}) copy-start(bf16[1,64,128,128]{3,2,0,1:T(8,128)(2,1)} %get-tuple-element.20) | copy-start | bytes 6291460
  58.4 2.4 copy-start.6
  60.2 1.3 copy-start.9
  62.3 1.0 slice-start
  63.7 5.3 %copy-start.19 = (s32[128]{0:T(128)S(1)}, s32[128]{0:T(128)}, u32[]{:S(2)}) copy-start(s32[128]{0:T(128)} %param.40) | copy-start | bytes 1540
  64.8 20.0 %all-to-all-start.1 = ((bf16[4,128,1152]{2,1,0:T(8,128)(2,1)}), bf16[4,128,1152]{2,1,0:T(8,128)(2,1)S(1)}, u32[]{:S(2)}, u32[]{:S(2)}) async-start(bf16[4,128,1152]{2,1,0:T(8,128)(2,1)} %bitcast.35), calls=%async_computation.1 | async-start | bytes 2359296 | tf_op jit(solution)/shard_map/all_to_all | solution.py:177
  86.4 3.5 copy-start.5
  89.8 0.9 copy-start.10
  123.1 4.7 %copy-start.13 = (s32[128,2]{0,1:T(2,128)S(1)}, s32[128,2]{0,1:T(2,128)}, u32[]{:S(2)}) copy-start(s32[128,2]{0,1:T(2,128)} %param.41) | copy-start | bytes 3076
  124.2 29.1 %all-to-all-start.3 = ((bf16[8,128,512]{2,1,0:T(8,128)(2,1)}), bf16[8,128,512]{2,1,0:T(8,128)(2,1)S(1)}, u32[]{:S(2)}, u32[]{:S(2)}) async-start(bf16[8,128,512]{2,1,0:T(8,128)(2,1)} %broadcast_in_dim.262), calls=%async_computation.3 | async-start | bytes 2097152 | tf_op jit(solution)/shard_map/all_to_all | solution.py:265
  153.7 0.7 copy-start.12
  164.2 29.3 %all-to-all-start.4 = ((bf16[4,64,4096]{2,1,0:T(8,128)(2,1)}), bf16[4,64,4096]{2,1,0:T(8,128)(2,1)S(1)}, u32[]{:S(2)}, u32[]{:S(2)}) async-start(bf16[4,64,4096]{2,1,0:T(8,128)(2,1)} %get-tuple-element.18), calls=%async_computation.4 | async-start | bytes 4194304 | tf_op jit(solution)/shard_map/all_to_all | solution.py:289
  193.5 1.4 copy-start.7
  194.9 32.5 %all-to-all-start.5 = ((bf16[4,64,4096]{2,1,0:T(8,128)(2,1)}), bf16[4,64,4096]{2,1,0:T(8,128)(2,1)S(1)}, u32[]{:S(2)}, u32[]{:S(2)}) async-start(bf16[4,64,4096]{2,1,0:T(8,128)(2,1)} %get-tuple-element.19), calls=%async_computation.6 | async-start | bytes 4194304 | tf_op jit(solution)/shard_map/all_to_all | solution.py:289
  198.5 124.5 %reduce-scatter.2.cloned.1.call-start = ((), (), s32[]{:S(2)}) async-start(), calls=%async_computation.9 | async-start | bytes 2359296 | tf_op jit(solution)/shard_map/reduce_scatter | solution.py:309
  247.1 4.1 %copy-start.11 = (bf16[4096,8]{0,1:T(8,128)(2,1)S(1)}, bf16[4096,8]{0,1:T(8,128)(2,1)}, u32[]{:S(2)}) copy-start(bf16[4096,8]{0,1:T(8,128)(2,1)} %param.26) | copy-start | bytes 196612
  247.1 54.9 %all-to-all-start.6 = ((bf16[8,4,64,512]{3,2,1,0:T(8,128)(2,1)}), bf16[8,4,64,512]{3,2,1,0:T(8,128)(2,1)S(1)}, u32[]{:S(2)}, u32[]{:S(2)}) async-start(bf16[8,4,64,512]{3,2,1,0:T(8,128)(2,1)} %copy.234), calls=%async_computation.7 | async-start | bytes 4194304 | tf_op jit(solution)/shard_map/all_to_all | solution.py:302
  324.8 12.3 %all-to-all-start.7 = ((bf16[4,2,64,512]{3,2,1,0:T(8,128)(2,1)}), bf16[4,2,64,512]{3,2,1,0:T(8,128)(2,1)S(1)}, u32[]{:S(2)}, u32[]{:S(2)}) async-start(bf16[4,2,64,512]{3,2,1,0:T(8,128)(2,1)} %copy.235), calls=%async_computation.8 | async-start | bytes 1048576 | tf_op jit(solution)/shard_map/all_to_all | solution.py:313
  328.4 11.6 %copy-start.1 = (bf16[128,4096]{1,0:T(8,128)(2,1)S(1)}, bf16[128,4096]{1,0:T(8,128)(2,1)}, u32[]{:S(2)}) copy-start(bf16[128,4096]{1,0:T(8,128)(2,1)} %param.21) | copy-start | bytes 3145732
Sparse Core Ops, SparseCore 0:
  227.5 95.4 reduce-scatter.1

commit v5 on v4

--- a/solution.py
+++ b/solution.py
@@ -309,10 +309,10 @@
             summed = lax.psum_scatter(
                 expert_partial.astype(jnp.bfloat16), "mp", scatter_dimension=2, tiled=True
             )
-        returned_parts.append(summed)
-    returned_rows = lax.all_to_all(
-        jnp.stack(returned_parts, axis=1), "dp", split_axis=0, concat_axis=0, tiled=True
-    )
+        returned_parts.append(
+            lax.all_to_all(summed, "dp", split_axis=0, concat_axis=0, tiled=True)
+        )
+    returned_rows = jnp.stack(returned_parts, axis=1)
     results = jnp.take(returned_rows.reshape(-1, slice_width), pair_slot, axis=0).reshape(
         local_rows, TOP, slice_width
     )

time: 349 us -> 345 us (0.989)
  waiting for transfers between devices: 118 us -> 111 us
    reduce_scatter x1, waiting for transfers between devices: 20.6 us -> 10.4 us  [shards(): lax.psum_scatter(expert_partial.astype(jnp.bfloat16), 'mp', scatter_dimen...]
    all_to_all x1 -> x2, waiting for transfers between devices: 8.61 us -> 11.8 us  [shards(): lax.all_to_all(summed, 'dp', split_axis=0, concat_axis=0, tiled=True)]
  transfers between devices with their start and end apart: 8 -> 9, of which waited for: 6 -> 7; matrix products, arithmetic and copies ran while one was open for 28% -> 29% of each run, Pallas kernels for 0% -> 0%
where the time goes in v5:
time: 345 us; the launch traced here: 342 us
  waiting for transfers between devices  111 us (32%)
  matrix products  61.3 us (18%)
  local copies, waits for them, and re-layouts  57.2 us (17%)
  starting transfers between devices  38.5 us (11%)
  blocking collectives  32 us (9%)
  other arithmetic  28.5 us (8%)
  between operations  14.4 us (4%)
    all_to_all x1, waiting for transfers between devices, shards(): lax.all_to_all(pieces, 'mp', split_axis=0, concat_axis=0, tiled=True)  50.4 us
    all_to_all x1, blocking collectives, shards(): lax.all_to_all(terms, 'mp', split_axis=0, concat_axis=0, tiled=True)  32 us
    dot_general x2, matrix products, shards(): jnp.einsum('scd,kfd->kscf', incoming, expert_in[expert_index], preferred_...  23.8 us
    all_to_all x1, waiting for transfers between devices, shards(): lax.all_to_all(spread_cols, 'mp', split_axis=0, concat_axis=0, tiled=True)  22.4 us
    unnamed x47, local copies, waits for them, and re-layouts  16.9 us
    all_to_all x2, waiting for transfers between devices, shards(): lax.all_to_all(summed, 'dp', split_axis=0, concat_axis=0, tiled=True)  11.8 us
    reduce_scatter x1, waiting for transfers between devices, shards(): lax.psum_scatter(expert_partial.astype(jnp.bfloat16), 'mp', scatter_dimen...  10.4 us
    gather x2, local copies, waits for them, and re-layouts, level_rows(): jnp.take(page_pool, page_list.reshape(-1), axis=1)  9.53 us
  transfers between devices with their start and end apart: 9, of which 7 were waited for; matrix products, arithmetic and copies ran while one was open for 29% of the time, Pallas kernels for 0%

profile of v5, /device:TPU:0, one launch (start us, length us, event | category | flops | bytes accessed | tf_op | source)
XLA Modules:
  0.0 342.4 jit_solution(3263161001967208952)
XLA Ops:
  6.6 1.2 copy-done
  7.8 0.9 broadcast_in_dim.244
  8.6 4.2 %all-to-all-start = ((bf16[4,128,512]{2,1,0:T(8,128)(2,1)}), bf16[4,128,512]{2,1,0:T(8,128)(2,1)}, u32[]{:S(2)}, u32[]{:S(2)}) async-start(bf16[4,128,512]{2,1,0:T(8,128)(2,1)} %broadcast_in_dim.244), calls=%async_computation | async-start | bytes 1048576 | tf_op jit(solution)/shard_map/all_to_all | solution.py:86
  12.8 0.7 fusion.126
  13.5 1.3 fusion.127
  14.8 0.7 fusion.124
  15.4 1.4 fusion.125
  17.1 0.8 scatter_custom_fusion.1
  18.2 0.7 fusion.120
  19.7 0.7 fusion.121
  21.0 0.7 broadcast_select_fusion.4
  23.2 0.7 broadcast_select_fusion.3
  26.5 1.1 reduce-window.36
  28.1 5.8 %gather_fusion.2 = bf16[64,2,128,128]{3,2,1,0:T(8,128)(2,1)} fusion(bf16[2,96,128,128]{3,2,1,0:T(8,128)(2,1)} %bitcast.227, s32[1024]{0:T(1024)S(1)} %pad_clamp_fusion.4), kind=kCustom, calls=%fused_computation.2 | custom fusion | bytes 8388864 | tf_op jit(solution)/shard_map/jit(_take)/gather | solution.py:122
  33.9 3.7 %gather_fusion.5 = bf16[32,2,128,128]{3,2,1,0:T(8,128)(2,1)S(1)} fusion(bf16[2,96,128,128]{3,2,1,0:T(8,128)(2,1)} %bitcast.228, s32[1024]{0:T(1024)S(1)} %pad_clamp_fusion.2), kind=kCustom, calls=%fused_computation.5 | custom fusion | bytes 4194432 | tf_op jit(solution)/shard_map/jit(_take)/gather | solution.py:122
  38.0 1.1 fusion.150
  39.2 1.4 copy-done.4
  41.2 1.8 fusion.149
  43.0 1.8 fusion.38
  44.8 2.8 fusion.6
  47.6 4.9 %fusion.7 = f32[2,128,4]{1,2,0:T(4,128)S(1)} fusion(f32[2,128,4,4096]{3,1,2,0:T(8,128)S(1)} %get-tuple-element.37, f32[2,128,4]{1,2,0:T(4,128)S(1)} %get-tuple-element.36, pred[2,4096]{1,0:T(4,128)(4,1)S(1)} %broadcast_compare_fusion), kind=kLoop, calls=%fused_computation.20 | loop fusion | flops 20970496 | bytes 16793600 | tf_op jit(solution)/shard_map/vmap()/reduce_sum | solution.py:39
  52.5 4.4 %fusion.12 = f32[2,128,4,128]{1,3,2,0:T(8,128)S(1)} fusion(bf16[2,4096,128,1]{2,1,3,0:T(8,128)(2,1)S(1)} %bitcast.232, f32[2,128,4,4096]{3,1,2,0:T(8,128)S(1)} %get-tuple-element.37, f32[2,128,4]{1,2,0:T(4,128)S(1)} %get-tuple-element.36, pred[2,4096]{1,0:T(4,128)(4,1)S(1)} %broadcast_compare_fusion), kind=kOutput, calls=%fused_computation.25 | convolution fusion | flops 1094713344 | bytes 19410944 | tf_op jit(solution)/shard_map/vmap(sgl,ld->sgd)/dot_general | solution.py:40
  57.3 1.0 convolution_bitcast_fusion.1
  58.4 1.7 fusion.39
  60.7 0.7 fusion.35
  62.3 0.9 convolution_bitcast_fusion
  63.7 1.1 fusion.37
  64.8 4.2 %all-to-all-start.1 = ((bf16[4,128,1152]{2,1,0:T(8,128)(2,1)}), bf16[4,128,1152]{2,1,0:T(8,128)(2,1)S(1)}, u32[]{:S(2)}, u32[]{:S(2)}) async-start(bf16[4,128,1152]{2,1,0:T(8,128)(2,1)} %bitcast.35), calls=%async_computation.1 | async-start | bytes 2359296 | tf_op jit(solution)/shard_map/all_to_all | solution.py:177
  69.1 4.5 %fusion.153 = (f32[128,4]{1,0:T(8,128)S(1)}, f32[128,4,128]{2,1,0:T(4,128)S(1)}) fusion(bf16[128,4,128]{2,1,0:T(4,128)(2,1)S(1)} %reshape.717, bf16[2,128,1,128,128]{4,3,1,2,0:T(8,128)(2,1)} %bitcast.247, pred[128,128]{1,0:T(8,128)(4,1)S(1)} %iota_compare_fusion.8), kind=kOutput, calls=%fused_computation.286 | convolution fusion | flops 16973312 | bytes 4605952 | tf_op jit(solution)/shard_map/rgd,rtd->rgt/dot_general | solution.py:203
  74.2 0.8 fusion.100
  75.3 9.5 %all-to-all-done.1 = bf16[4,128,1152]{2,1,0:T(8,128)(2,1)S(1)} async-done(((bf16[4,128,1152]{2,1,0:T(8,128)(2,1)}), bf16[4,128,1152]{2,1,0:T(8,128)(2,1)S(1)}, u32[]{:S(2)}, u32[]{:S(2)}) %all-to-all-start.1) | async-done | bytes 1179680 | tf_op jit(solution)/shard_map/all_to_all | solution.py:177
  86.4 3.2 fusion.55
  89.8 0.7 fusion.91
  91.0 32.0 %all_to_all.45 = bf16[8,128,512]{2,1,0:T(8,128)(2,1)S(1)} all-to-all(bf16[8,128,512]{2,1,0:T(8,128)(2,1)S(1)} %bitcast.230), channel_id=1, replica_groups=mesh['dp'=4,'mp'=8] {'mp'}, dimensions={0} | all-to-all | bytes 2097152 | tf_op jit(solution)/shard_map/all_to_all | solution.py:260
  123.2 1.1 broadcast_in_dim.262
  124.2 3.6 %all-to-all-start.3 = ((bf16[8,128,512]{2,1,0:T(8,128)(2,1)}), bf16[8,128,512]{2,1,0:T(8,128)(2,1)S(1)}, u32[]{:S(2)}, u32[]{:S(2)}) async-start(bf16[8,128,512]{2,1,0:T(8,128)(2,1)} %broadcast_in_dim.262), calls=%async_computation.3 | async-start | bytes 2097152 | tf_op jit(solution)/shard_map/all_to_all | solution.py:265
  129.4 1.4 scatter_custom_fusion.2
  131.0 22.4 %all-to-all-done.3 = bf16[8,128,512]{2,1,0:T(8,128)(2,1)S(1)} async-done(((bf16[8,128,512]{2,1,0:T(8,128)(2,1)}), bf16[8,128,512]{2,1,0:T(8,128)(2,1)S(1)}, u32[]{:S(2)}, u32[]{:S(2)}) %all-to-all-start.3) | async-done | bytes 1048608 | tf_op jit(solution)/shard_map/all_to_all | solution.py:265
  154.8 4.4 %gather_fusion.6 = bf16[512,4096]{1,0:T(8,128)(2,1)} fusion(bf16[129,4096]{1,0:T(8,128)(2,1)S(1)} %concatenate.32, s32[1024]{0:T(1024)S(1)} %pad_clamp_fusion.1), kind=kCustom, calls=%fused_computation.6 | custom fusion | bytes 8390656 | tf_op jit(solution)/shard_map/jit(_take)/gather | solution.py:284
  159.1 2.6 copy_select_fusion
  161.8 2.5 slice_bitcast_fusion.5
  164.2 3.6 %all-to-all-start.4 = ((bf16[4,64,4096]{2,1,0:T(8,128)(2,1)}), bf16[4,64,4096]{2,1,0:T(8,128)(2,1)S(1)}, u32[]{:S(2)}, u32[]{:S(2)}) async-start(bf16[4,64,4096]{2,1,0:T(8,128)(2,1)} %get-tuple-element.18), calls=%async_computation.4 | async-start | bytes 4194304 | tf_op jit(solution)/shard_map/all_to_all | solution.py:289
  167.8 7.7 %slice.159 = bf16[1,1024,4096]{2,1,0:T(8,128)(2,1)} slice(bf16[2,1024,4096]{2,1,0:T(8,128)(2,1)} %param.28), slice={[1:2], [0:1024], [0:4096]} | slice | bytes 16777216 | tf_op jit(solution)/shard_map/slice | solution.py:299
  175.6 12.0 %copy.253 = bf16[1,1024,4096]{1,2,0:T(8,128)(2,1)} copy(bf16[1,1024,4096]{2,1,0:T(8,128)(2,1)} %slice.159) | data formatting | bytes 16777216
  187.5 6.0 %all-to-all-done.4 = bf16[4,64,4096]{2,1,0:T(8,128)(2,1)S(1)} async-done(((bf16[4,64,4096]{2,1,0:T(8,128)(2,1)}), bf16[4,64,4096]{2,1,0:T(8,128)(2,1)S(1)}, u32[]{:S(2)}, u32[]{:S(2)}) %all-to-all-start.4) | async-done | bytes 2097184 | tf_op jit(solution)/shard_map/all_to_all | solution.py:289
  193.5 1.4 copy-done.7
  194.9 3.6 %all-to-all-start.6 = ((bf16[4,64,4096]{2,1,0:T(8,128)(2,1)}), bf16[4,64,4096]{2,1,0:T(8,128)(2,1)S(1)}, u32[]{:S(2)}, u32[]{:S(2)}) async-start(bf16[4,64,4096]{2,1,0:T(8,128)(2,1)} %get-tuple-element.19), calls=%async_computation.7 | async-start | bytes 4194304 | tf_op jit(solution)/shard_map/all_to_all | solution.py:289
  198.5 8.8 %reduce-scatter.2.cloned.1.call-start = ((), (), s32[]{:S(2)}) async-start(), calls=%async_computation.10 | async-start | bytes 2359296 | tf_op jit(solution)/shard_map/reduce_scatter | solution.py:309
  207.3 12.2 %fusion.25 = f32[2,4,64,1024]{3,2,0,1:T(8,128)} fusion(bf16[2,2,1024,4096]{3,2,1,0:T(8,128)(2,1)} %param.27, bf16[4,64,4096]{2,1,0:T(8,128)(2,1)} %copy-done.7), kind=kOutput, calls=%fused_computation.51 | convolution fusion | flops 4294967296 | bytes 20971520 | tf_op jit(solution)/shard_map/scd,kfd->kscf/dot_general | solution.py:292
  219.5 7.8 %fusion.15 = bf16[4,64,4096]{2,1,0:T(8,128)(2,1)} fusion(bf16[2,1024,4096]{2,1,0:T(8,128)(2,1)} %param.28, f32[2,4,64,1024]{3,2,0,1:T(8,128)} %fusion.25), kind=kOutput, calls=%fused_computation.27 | convolution fusion | flops 2150105088 | bytes 12582912 | tf_op jit(solution)/shard_map/scf,fd->scd/dot_general | solution.py:305
  227.4 11.6 %fusion.30 = f32[2,4,64,1024]{3,2,0,1:T(8,128)} fusion(bf16[2,2,1024,4096]{3,2,1,0:T(8,128)(2,1)} %param.27, bf16[4,64,4096]{2,1,0:T(8,128)(2,1)S(1)} %all-to-all-done.6), kind=kOutput, calls=%fused_computation.52 | convolution fusion | flops 4294967296 | bytes 20971520 | tf_op jit(solution)/shard_map/scd,kfd->kscf/dot_general | solution.py:292
  239.0 6.7 %convert_bitcast_fusion.1 = bf16[8,4,64,512]{3,2,0,1:T(8,128)(2,1)S(1)} fusion(bf16[1024,8,512,1]{0,2,1,3:T(8,128)(2,1)} %bitcast.224, f32[2,4,64,1024]{3,2,0,1:T(8,128)} %fusion.30), kind=kOutput, calls=%fused_computation.45 | convolution fusion | flops 2150105088 | bytes 12582912 | tf_op jit(solution)/shard_map/scf,fmd->mscd/dot_general | solution.py:297
  245.7 1.5 copy.234
  247.1 3.7 %all-to-all-start.7 = ((bf16[8,4,64,512]{3,2,1,0:T(8,128)(2,1)}), bf16[8,4,64,512]{3,2,1,0:T(8,128)(2,1)S(1)}, u32[]{:S(2)}, u32[]{:S(2)}) async-start(bf16[8,4,64,512]{3,2,1,0:T(8,128)(2,1)} %copy.234), calls=%async_computation.8 | async-start | bytes 4194304 | tf_op jit(solution)/shard_map/all_to_all | solution.py:302
  251.7 50.4 %all-to-all-done.7 = bf16[8,4,64,512]{3,2,1,0:T(8,128)(2,1)S(1)} async-done(((bf16[8,4,64,512]{3,2,1,0:T(8,128)(2,1)}), bf16[8,4,64,512]{3,2,1,0:T(8,128)(2,1)S(1)}, u32[]{:S(2)}, u32[]{:S(2)}) %all-to-all-start.7) | async-done | bytes 2097184 | tf_op jit(solution)/shard_map/all_to_all | solution.py:302
  302.1 1.1 reduce_sum.157
  303.2 3.4 all-to-all-start.8
  306.6 5.9 %all-to-all-done.8 = bf16[4,64,512]{2,1,0:T(8,128)(2,1)S(1)} async-done(((bf16[4,64,512]{2,1,0:T(8,128)(2,1)}), bf16[4,64,512]{2,1,0:T(8,128)(2,1)S(1)}, u32[]{:S(2)}, u32[]{:S(2)}) %all-to-all-start.8) | async-done | bytes 262176 | tf_op jit(solution)/shard_map/all_to_all | solution.py:313
  312.6 10.4 %reduce-scatter.2.cloned.1.call-done = bf16[4,64,512]{2,1,0:T(8,128)(2,1)} async-done(((bf16[4,64,4096]{2,1,0:T(8,128)(2,1)}), bf16[4,64,512]{2,1,0:T(8,128)(2,1)}) %reduce-scatter.2.cloned.1.call-update) | async-done | bytes 262160 | tf_op jit(solution)/shard_map/reduce_scatter | solution.py:309
  323.0 3.4 all-to-all-start.5
  326.5 5.9 %all-to-all-done.5 = bf16[4,64,512]{2,1,0:T(8,128)(2,1)S(1)} async-done(((bf16[4,64,512]{2,1,0:T(8,128)(2,1)}), bf16[4,64,512]{2,1,0:T(8,128)(2,1)S(1)}, u32[]{:S(2)}, u32[]{:S(2)}) %all-to-all-start.5) | async-done | bytes 262176 | tf_op jit(solution)/shard_map/all_to_all | solution.py:313
  332.5 1.2 gather_fusion.7
  333.8 0.8 multiply_reduce_fusion
  334.6 0.7 add_convert_fusion
  (178 shorter events, 17.3 us)
Async XLA Ops:
  6.5 1.2 copy-start
  6.5 13.9 %copy-start.2 = (s32[8]{0:T(128)S(1)}, s32[8]{0:T(128)}, u32[]{:S(2)}) copy-start(s32[8]{0:T(128)} %param.38) | copy-start | bytes 100
  6.5 15.2 %copy-start.14 = (s32[8,32]{1,0:T(8,128)S(1)}, s32[8,32]{1,0:T(8,128)}, u32[]{:S(2)}) copy-start(s32[8,32]{1,0:T(8,128)} %param.36) | copy-start | bytes 3076
  6.5 16.0 %copy-start.3 = (s32[32]{0:T(128)S(1)}, s32[32]{0:T(128)}, u32[]{:S(2)}) copy-start(s32[32]{0:T(128)} %param.39) | copy-start | bytes 388
  6.5 17.3 %copy-start.15 = (s32[32,4]{0,1:T(4,128)S(1)}, s32[32,4]{0,1:T(4,128)}, u32[]{:S(2)}) copy-start(s32[32,4]{0,1:T(4,128)} %param.37) | copy-start | bytes 1540
  6.5 18.2 %copy-start.17 = (s32[512]{0:T(512)S(1)}, s32[512]{0:T(512)}, u32[]{:S(2)}) copy-start(s32[512]{0:T(512)} %param.31) | copy-start | bytes 6148
  6.6 18.2 %copy-start.16 = (s32[512]{0:T(512)S(1)}, s32[512]{0:T(512)}, u32[]{:S(2)}) copy-start(s32[512]{0:T(512)} %param.32) | copy-start | bytes 6148
  6.6 18.5 %copy-start.18 = (s32[32]{0:T(128)S(1)}, s32[32]{0:T(128)}, u32[]{:S(2)}) copy-start(s32[32]{0:T(128)} %param.33) | copy-start | bytes 388
  8.6 34.4 %all-to-all-start = ((bf16[4,128,512]{2,1,0:T(8,128)(2,1)}), bf16[4,128,512]{2,1,0:T(8,128)(2,1)}, u32[]{:S(2)}, u32[]{:S(2)}) async-start(bf16[4,128,512]{2,1,0:T(8,128)(2,1)} %broadcast_in_dim.244), calls=%async_computation | async-start | bytes 1048576 | tf_op jit(solution)/shard_map/all_to_all | solution.py:86
  38.0 2.6 copy-start.4
  47.6 4.9 %copy-start.8 = (bf16[1,64,128,128]{3,2,0,1:T(8,128)(2,1)S(1)}, bf16[1,64,128,128]{3,2,0,1:T(8,128)(2,1)}, u32[]{:S(2)}) copy-start(bf16[1,64,128,128]{3,2,0,1:T(8,128)(2,1)} %get-tuple-element.20) | copy-start | bytes 6291460
  58.4 2.4 copy-start.6
  60.2 1.3 copy-start.9
  62.3 1.0 slice-start
  63.7 5.3 %copy-start.19 = (s32[128]{0:T(128)S(1)}, s32[128]{0:T(128)}, u32[]{:S(2)}) copy-start(s32[128]{0:T(128)} %param.40) | copy-start | bytes 1540
  64.8 20.0 %all-to-all-start.1 = ((bf16[4,128,1152]{2,1,0:T(8,128)(2,1)}), bf16[4,128,1152]{2,1,0:T(8,128)(2,1)S(1)}, u32[]{:S(2)}, u32[]{:S(2)}) async-start(bf16[4,128,1152]{2,1,0:T(8,128)(2,1)} %bitcast.35), calls=%async_computation.1 | async-start | bytes 2359296 | tf_op jit(solution)/shard_map/all_to_all | solution.py:177
  86.4 3.5 %copy-start.5 = (bf16[512,4096]{1,0:T(8,128)(2,1)S(1)}, bf16[512,4096]{1,0:T(8,128)(2,1)}, u32[]{:S(2)}) copy-start(bf16[512,4096]{1,0:T(8,128)(2,1)} %param.24) | copy-start | bytes 12582916
  89.8 0.9 copy-start.10
  123.1 4.7 %copy-start.13 = (s32[128,2]{0,1:T(2,128)S(1)}, s32[128,2]{0,1:T(2,128)}, u32[]{:S(2)}) copy-start(s32[128,2]{0,1:T(2,128)} %param.41) | copy-start | bytes 3076
  124.2 29.1 %all-to-all-start.3 = ((bf16[8,128,512]{2,1,0:T(8,128)(2,1)}), bf16[8,128,512]{2,1,0:T(8,128)(2,1)S(1)}, u32[]{:S(2)}, u32[]{:S(2)}) async-start(bf16[8,128,512]{2,1,0:T(8,128)(2,1)} %broadcast_in_dim.262), calls=%async_computation.3 | async-start | bytes 2097152 | tf_op jit(solution)/shard_map/all_to_all | solution.py:265
  153.7 0.7 copy-start.12
  164.2 29.3 %all-to-all-start.4 = ((bf16[4,64,4096]{2,1,0:T(8,128)(2,1)}), bf16[4,64,4096]{2,1,0:T(8,128)(2,1)S(1)}, u32[]{:S(2)}, u32[]{:S(2)}) async-start(bf16[4,64,4096]{2,1,0:T(8,128)(2,1)} %get-tuple-element.18), calls=%async_computation.4 | async-start | bytes 4194304 | tf_op jit(solution)/shard_map/all_to_all | solution.py:289
  193.5 1.4 copy-start.7
  194.9 32.5 %all-to-all-start.6 = ((bf16[4,64,4096]{2,1,0:T(8,128)(2,1)}), bf16[4,64,4096]{2,1,0:T(8,128)(2,1)S(1)}, u32[]{:S(2)}, u32[]{:S(2)}) async-start(bf16[4,64,4096]{2,1,0:T(8,128)(2,1)} %get-tuple-element.19), calls=%async_computation.7 | async-start | bytes 4194304 | tf_op jit(solution)/shard_map/all_to_all | solution.py:289
  198.5 124.5 %reduce-scatter.2.cloned.1.call-start = ((), (), s32[]{:S(2)}) async-start(), calls=%async_computation.10 | async-start | bytes 2359296 | tf_op jit(solution)/shard_map/reduce_scatter | solution.py:309
  247.1 4.1 %copy-start.11 = (bf16[4096,8]{0,1:T(8,128)(2,1)S(1)}, bf16[4096,8]{0,1:T(8,128)(2,1)}, u32[]{:S(2)}) copy-start(bf16[4096,8]{0,1:T(8,128)(2,1)} %param.26) | copy-start | bytes 196612
  247.1 54.9 %all-to-all-start.7 = ((bf16[8,4,64,512]{3,2,1,0:T(8,128)(2,1)}), bf16[8,4,64,512]{3,2,1,0:T(8,128)(2,1)S(1)}, u32[]{:S(2)}, u32[]{:S(2)}) async-start(bf16[8,4,64,512]{3,2,1,0:T(8,128)(2,1)} %copy.234), calls=%async_computation.8 | async-start | bytes 4194304 | tf_op jit(solution)/shard_map/all_to_all | solution.py:302
  303.2 9.4 %all-to-all-start.8 = ((bf16[4,64,512]{2,1,0:T(8,128)(2,1)}), bf16[4,64,512]{2,1,0:T(8,128)(2,1)S(1)}, u32[]{:S(2)}, u32[]{:S(2)}) async-start(bf16[4,64,512]{2,1,0:T(8,128)(2,1)} %reduce_sum.157), calls=%async_computation.9 | async-start | bytes 524288 | tf_op jit(solution)/shard_map/all_to_all | solution.py:313
  323.0 9.4 %all-to-all-start.5 = ((bf16[4,64,512]{2,1,0:T(8,128)(2,1)}), bf16[4,64,512]{2,1,0:T(8,128)(2,1)S(1)}, u32[]{:S(2)}, u32[]{:S(2)}) async-start(bf16[4,64,512]{2,1,0:T(8,128)(2,1)} %reduce-scatter.2.cloned.1.call-done), calls=%async_computation.6 | async-start | bytes 524288 | tf_op jit(solution)/shard_map/all_to_all | solution.py:313
  332.5 2.9 copy-start.1
Sparse Core Ops, SparseCore 0:
  227.5 95.4 reduce-scatter.1

commit v6 on v2

--- a/solution.py
+++ b/solution.py
@@ -274,16 +274,15 @@
         .at[pair_slot]
         .set(jnp.arange(pair_experts.shape[0], dtype=jnp.int32) // TOP)
     )
-    padded = jnp.concatenate([normed, jnp.zeros((1, normed.shape[1]), jnp.bfloat16)], axis=0)
     local_experts = expert_in.shape[0]
-    outgoing = jnp.take(padded, slot_source, axis=0).reshape(
-        dp_count, local_experts, E_CAP, normed.shape[1]
-    )
+    slot_pick = (slot_source[:, None] == jnp.arange(local_rows)[None, :]).astype(jnp.bfloat16)
+    slot_pick = slot_pick.reshape(dp_count, local_experts, E_CAP, local_rows)
     returned_parts = []
     for expert_index in range(local_experts):
-        incoming = lax.all_to_all(
-            outgoing[:, expert_index], "dp", split_axis=0, concat_axis=0, tiled=True
-        )
+        outgoing = jnp.einsum(
+            "scr,rd->scd", slot_pick[:, expert_index], normed, preferred_element_type=jnp.float32
+        ).astype(jnp.bfloat16)
+        incoming = lax.all_to_all(outgoing, "dp", split_axis=0, concat_axis=0, tiled=True)
         gate_up = jnp.einsum(
             "scd,kfd->kscf", incoming, expert_in[expert_index], preferred_element_type=jnp.float32
         )

time: 340 us -> 339 us (level)
  local copies, waits for them, and re-layouts: 55.2 us -> 47.9 us
  matrix products: 58.9 us -> 62.9 us
    reduce_scatter x1, waiting for transfers between devices: 0.01 us -> 10.1 us  [shards(): lax.psum_scatter(expert_partial.astype(jnp.bfloat16), 'mp', scatter_dimen...]
    all_to_all x1, waiting for transfers between devices: 50.7 us -> 43.8 us  [shards(): lax.all_to_all(pieces, 'mp', split_axis=0, concat_axis=0, tiled=True)]
    gather x1 -> x0, local copies, waits for them, and re-layouts: 4.35 us -> none  [shards(): jnp.take(padded, slot_source, axis=0)]
    dot_general x0 -> x2, matrix products: none -> 4.01 us  [shards(): jnp.einsum('scr,rd->scd', slot_pick[:, expert_index], normed, preferred_e...]
    unnamed x41 -> x47, local copies, waits for them, and re-layouts: 15.7 us -> 14.2 us
  transfers between devices with their start and end apart: 8 -> 8, of which waited for: 7 -> 8; matrix products, arithmetic and copies ran while one was open for 21% -> 23% of each run, Pallas kernels for 0% -> 0%
where the time goes in v6:
time: 339 us; the launch traced here: 333 us
  waiting for transfers between devices  107 us (32%)
  matrix products  62.9 us (19%)
  local copies, waits for them, and re-layouts  47.9 us (14%)
  blocking collectives  39.9 us (12%)
  other arithmetic  34.5 us (10%)
  starting transfers between devices  26.1 us (8%)
  between operations  14.7 us (4%)
    all_to_all x1, waiting for transfers between devices, shards(): lax.all_to_all(pieces, 'mp', split_axis=0, concat_axis=0, tiled=True)  43.8 us
    all_to_all x1, blocking collectives, shards(): lax.all_to_all(terms, 'mp', split_axis=0, concat_axis=0, tiled=True)  31.2 us
    dot_general x2, matrix products, shards(): jnp.einsum('scd,kfd->kscf', incoming, expert_in[expert_index], preferred_...  24.1 us
    all_to_all x1, waiting for transfers between devices, shards(): lax.all_to_all(spread_cols, 'mp', split_axis=0, concat_axis=0, tiled=True)  22.2 us
    unnamed x47, local copies, waits for them, and re-layouts  14.2 us
    all_to_all x2, waiting for transfers between devices, shards(): lax.all_to_all(summed, 'dp', split_axis=0, concat_axis=0, tiled=True)  11.8 us
    reduce_scatter x1, waiting for transfers between devices, shards(): lax.psum_scatter(expert_partial.astype(jnp.bfloat16), 'mp', scatter_dimen...  10.1 us
    gather x2, local copies, waits for them, and re-layouts, level_rows(): jnp.take(page_pool, page_list.reshape(-1), axis=1)  9.71 us
  transfers between devices with their start and end apart: 8, of which 8 were waited for; matrix products, arithmetic and copies ran while one was open for 23% of the time, Pallas kernels for 0%

profile of v6, /device:TPU:0, one launch (start us, length us, event | category | flops | bytes accessed | tf_op | source)
XLA Modules:
  0.0 332.5 jit_solution(9256506905591715621)
XLA Ops:
  6.5 0.7 fusion.129
  7.3 1.3 fusion.130
  9.2 1.4 fusion.128
  10.9 0.8 scatter_custom_fusion.1
  13.5 0.7 fusion.124
  14.2 1.3 gather_fusion
  15.5 0.7 broadcast_select_fusion.4
  16.2 1.2 gather_fusion.1
  17.7 0.9 select_reduce_fusion
  18.6 0.7 select_reduce_fusion.1
  20.6 8.6 %all_gather.3 = bf16[512,512]{1,0:T(8,128)(2,1)S(1)} all-gather(bf16[128,512]{1,0:T(8,128)(2,1)S(1)} %constant_dynamic-slice_fusion), channel_id=1, replica_groups=mesh['dp'=4,'mp'=8] {'dp'}, dimensions={0}, use_global_device_ids=true | all-gather | bytes 655360 | tf_op jit(solution)/shard_map/all_gather | solution.py:85
  29.3 6.0 %gather_fusion.2 = bf16[64,2,128,128]{3,2,1,0:T(8,128)(2,1)} fusion(bf16[2,96,128,128]{3,2,1,0:T(8,128)(2,1)} %bitcast.240, s32[1024]{0:T(1024)S(1)} %pad_clamp_fusion.3), kind=kCustom, calls=%fused_computation.2 | custom fusion | bytes 8388864 | tf_op jit(solution)/shard_map/jit(_take)/gather | solution.py:117
  35.3 2.6 select_bitcast_fusion
  38.5 0.7 fusion.39
  39.2 2.8 fusion.6
  42.0 5.1 %fusion.7 = f32[2,128,4]{1,2,0:T(4,128)S(1)} fusion(f32[2,128,4,4096]{3,1,2,0:T(8,128)S(1)} %get-tuple-element.35, f32[2,128,4]{1,2,0:T(4,128)S(1)} %get-tuple-element.34, pred[2,4096]{1,0:T(4,128)(4,1)S(1)} %broadcast_compare_fusion), kind=kLoop, calls=%fused_computation.19 | loop fusion | flops 20970496 | bytes 16793600 | tf_op jit(solution)/shard_map/vmap()/reduce_sum | solution.py:39
  47.1 4.2 %fusion.12 = f32[2,128,4,128]{1,3,2,0:T(8,128)S(1)} fusion(bf16[2,4096,128,1]{2,1,3,0:T(8,128)(2,1)S(1)} %bitcast.245, f32[2,128,4,4096]{3,1,2,0:T(8,128)S(1)} %get-tuple-element.35, f32[2,128,4]{1,2,0:T(4,128)S(1)} %get-tuple-element.34, pred[2,4096]{1,0:T(4,128)(4,1)S(1)} %broadcast_compare_fusion), kind=kOutput, calls=%fused_computation.24 | convolution fusion | flops 1094713344 | bytes 19410944 | tf_op jit(solution)/shard_map/vmap(sgl,ld->sgd)/dot_general | solution.py:40
  51.7 1.0 convolution_bitcast_fusion.1
  52.7 0.8 slice.288
  54.3 1.3 broadcast_select_fusion.3
  57.6 1.1 reduce-window.36
  59.2 3.7 %gather_fusion.5 = bf16[32,2,128,128]{3,2,1,0:T(8,128)(2,1)S(1)} fusion(bf16[2,96,128,128]{3,2,1,0:T(8,128)(2,1)} %bitcast.241, s32[1024]{0:T(1024)S(1)} %pad_clamp_fusion.1), kind=kCustom, calls=%fused_computation.5 | custom fusion | bytes 4194432 | tf_op jit(solution)/shard_map/jit(_take)/gather | solution.py:117
  65.3 0.7 fusion.36
  66.8 0.9 convolution_bitcast_fusion
  68.8 1.1 fusion.38
  69.9 3.7 %all-to-all-start = ((bf16[4,128,1152]{2,1,0:T(8,128)(2,1)}), bf16[4,128,1152]{2,1,0:T(8,128)(2,1)S(1)}, u32[]{:S(2)}, u32[]{:S(2)}) async-start(bf16[4,128,1152]{2,1,0:T(8,128)(2,1)} %bitcast.33), calls=%async_computation | async-start | bytes 2359296 | tf_op jit(solution)/shard_map/all_to_all | solution.py:172
  73.8 4.5 %fusion.156 = (f32[128,4]{1,0:T(8,128)S(1)}, f32[128,4,128]{2,1,0:T(4,128)S(1)}) fusion(bf16[128,4,128]{2,1,0:T(4,128)(2,1)S(1)} %reshape.734, bf16[2,128,1,128,128]{4,3,1,2,0:T(8,128)(2,1)} %bitcast.260, pred[128,128]{1,0:T(8,128)(4,1)S(1)} %iota_compare_fusion.9), kind=kOutput, calls=%fused_computation.287 | convolution fusion | flops 16973312 | bytes 4605952 | tf_op jit(solution)/shard_map/rgd,rtd->rgt/dot_general | solution.py:198
  78.8 0.8 fusion.103
  80.0 9.5 %all-to-all-done = bf16[4,128,1152]{2,1,0:T(8,128)(2,1)S(1)} async-done(((bf16[4,128,1152]{2,1,0:T(8,128)(2,1)}), bf16[4,128,1152]{2,1,0:T(8,128)(2,1)S(1)}, u32[]{:S(2)}, u32[]{:S(2)}) %all-to-all-start) | async-done | bytes 1179680 | tf_op jit(solution)/shard_map/all_to_all | solution.py:172
  91.0 3.2 fusion.56
  94.4 0.7 fusion.94
  95.6 31.2 %all_to_all.40 = bf16[8,128,512]{2,1,0:T(8,128)(2,1)S(1)} all-to-all(bf16[8,128,512]{2,1,0:T(8,128)(2,1)S(1)} %bitcast.243), channel_id=1, replica_groups=mesh['dp'=4,'mp'=8] {'mp'}, dimensions={0} | all-to-all | bytes 2097152 | tf_op jit(solution)/shard_map/all_to_all | solution.py:255
  127.2 1.1 broadcast_in_dim.242
  128.3 3.6 %all-to-all-start.2 = ((bf16[8,128,512]{1,2,0:T(8,128)(2,1)}), bf16[8,128,512]{1,2,0:T(8,128)(2,1)S(1)}, u32[]{:S(2)}, u32[]{:S(2)}) async-start(bf16[8,128,512]{1,2,0:T(8,128)(2,1)} %broadcast_in_dim.242), calls=%async_computation.2 | async-start | bytes 2097152 | tf_op jit(solution)/shard_map/all_to_all | solution.py:260
  133.6 1.4 scatter_custom_fusion.2
  135.2 22.2 %all-to-all-done.2 = bf16[8,128,512]{1,2,0:T(8,128)(2,1)S(1)} async-done(((bf16[8,128,512]{1,2,0:T(8,128)(2,1)}), bf16[8,128,512]{1,2,0:T(8,128)(2,1)S(1)}, u32[]{:S(2)}, u32[]{:S(2)}) %all-to-all-start.2) | async-done | bytes 1048608 | tf_op jit(solution)/shard_map/all_to_all | solution.py:260
  158.0 0.7 multiply_convert_fusion
  158.7 2.0 convolution_convert_fusion.1
  160.8 4.4 %all-to-all-start.3 = ((bf16[4,64,4096]{2,1,0:T(8,128)(2,1)}), bf16[4,64,4096]{2,1,0:T(8,128)(2,1)}, u32[]{:S(2)}, u32[]{:S(2)}) async-start(bf16[4,64,4096]{2,1,0:T(8,128)(2,1)} %convolution_convert_fusion.1), calls=%async_computation.3 | async-start | bytes 4194304 | tf_op jit(solution)/shard_map/all_to_all | solution.py:285
  165.2 7.7 %slice.159 = bf16[1,1024,4096]{2,1,0:T(8,128)(2,1)} slice(bf16[2,1024,4096]{2,1,0:T(8,128)(2,1)} %param.28), slice={[1:2], [0:1024], [0:4096]} | slice | bytes 16777216 | tf_op jit(solution)/shard_map/slice | solution.py:293
  172.9 12.0 %copy.288 = bf16[1,1024,4096]{1,2,0:T(8,128)(2,1)} copy(bf16[1,1024,4096]{2,1,0:T(8,128)(2,1)} %slice.159) | data formatting | bytes 16777216
  184.9 2.0 convolution_convert_fusion
  186.9 4.1 %all-to-all-done.3 = bf16[4,64,4096]{2,1,0:T(8,128)(2,1)} async-done(((bf16[4,64,4096]{2,1,0:T(8,128)(2,1)}), bf16[4,64,4096]{2,1,0:T(8,128)(2,1)}, u32[]{:S(2)}, u32[]{:S(2)}) %all-to-all-start.3) | async-done | bytes 2097184 | tf_op jit(solution)/shard_map/all_to_all | solution.py:285
  191.0 3.6 %all-to-all-start.5 = ((bf16[4,64,4096]{2,1,0:T(8,128)(2,1)}), bf16[4,64,4096]{2,1,0:T(8,128)(2,1)S(1)}, u32[]{:S(2)}, u32[]{:S(2)}) async-start(bf16[4,64,4096]{2,1,0:T(8,128)(2,1)} %convolution_convert_fusion), calls=%async_computation.6 | async-start | bytes 4194304 | tf_op jit(solution)/shard_map/all_to_all | solution.py:285
  194.9 12.3 %fusion.26 = f32[2,4,64,1024]{3,2,0,1:T(8,128)} fusion(bf16[2,2,1024,4096]{3,2,1,0:T(8,128)(2,1)} %param.27, bf16[4,64,4096]{2,1,0:T(8,128)(2,1)} %all-to-all-done.3), kind=kOutput, calls=%fused_computation.50 | convolution fusion | flops 4294967296 | bytes 20971520 | tf_op jit(solution)/shard_map/scd,kfd->kscf/dot_general | solution.py:286
  207.2 7.8 %fusion.15 = bf16[4,64,4096]{2,1,0:T(8,128)(2,1)} fusion(bf16[2,1024,4096]{2,1,0:T(8,128)(2,1)} %param.28, f32[2,4,64,1024]{3,2,0,1:T(8,128)} %fusion.26), kind=kOutput, calls=%fused_computation.26 | convolution fusion | flops 2150105088 | bytes 12582912 | tf_op jit(solution)/shard_map/scf,fd->scd/dot_general | solution.py:299
  215.0 5.2 %all-to-all-done.5 = bf16[4,64,4096]{2,1,0:T(8,128)(2,1)S(1)} async-done(((bf16[4,64,4096]{2,1,0:T(8,128)(2,1)}), bf16[4,64,4096]{2,1,0:T(8,128)(2,1)S(1)}, u32[]{:S(2)}, u32[]{:S(2)}) %all-to-all-start.5) | async-done | bytes 2097184 | tf_op jit(solution)/shard_map/all_to_all | solution.py:285
  220.2 11.8 %fusion.31 = f32[2,4,64,1024]{3,2,0,1:T(8,128)} fusion(bf16[2,2,1024,4096]{3,2,1,0:T(8,128)(2,1)} %param.27, bf16[4,64,4096]{2,1,0:T(8,128)(2,1)S(1)} %all-to-all-done.5), kind=kOutput, calls=%fused_computation.51 | convolution fusion | flops 4294967296 | bytes 20971520 | tf_op jit(solution)/shard_map/scd,kfd->kscf/dot_general | solution.py:286
  232.0 6.8 %convert_bitcast_fusion = bf16[8,4,64,512]{3,2,0,1:T(8,128)(2,1)S(1)} fusion(bf16[1024,8,512,1]{0,2,1,3:T(8,128)(2,1)} %bitcast.238, f32[2,4,64,1024]{3,2,0,1:T(8,128)} %fusion.31), kind=kOutput, calls=%fused_computation.43 | convolution fusion | flops 2150105088 | bytes 12582912 | tf_op jit(solution)/shard_map/scf,fmd->mscd/dot_general | solution.py:291
  238.9 1.5 copy.265
  240.4 3.6 %all-to-all-start.6 = ((bf16[8,4,64,512]{3,2,1,0:T(8,128)(2,1)}), bf16[8,4,64,512]{3,2,1,0:T(8,128)(2,1)S(1)}, u32[]{:S(2)}, u32[]{:S(2)}) async-start(bf16[8,4,64,512]{3,2,1,0:T(8,128)(2,1)} %copy.265), calls=%async_computation.7 | async-start | bytes 4194304 | tf_op jit(solution)/shard_map/all_to_all | solution.py:296
  244.0 0.8 reduce_sum.155
  245.4 0.7 compare_and_fusion
  247.0 1.3 fusion.24
  248.5 43.8 %all-to-all-done.6 = bf16[8,4,64,512]{3,2,1,0:T(8,128)(2,1)S(1)} async-done(((bf16[8,4,64,512]{3,2,1,0:T(8,128)(2,1)}), bf16[8,4,64,512]{3,2,1,0:T(8,128)(2,1)S(1)}, u32[]{:S(2)}, u32[]{:S(2)}) %all-to-all-start.6) | async-done | bytes 2097184 | tf_op jit(solution)/shard_map/all_to_all | solution.py:296
  292.3 1.1 reduce_sum.157
  293.4 3.4 %all-to-all-start.7 = ((bf16[4,64,512]{2,1,0:T(8,128)(2,1)}), bf16[4,64,512]{2,1,0:T(8,128)(2,1)S(1)}, u32[]{:S(2)}, u32[]{:S(2)}) async-start(bf16[4,64,512]{2,1,0:T(8,128)(2,1)} %reduce_sum.157), calls=%async_computation.8 | async-start | bytes 524288 | tf_op jit(solution)/shard_map/all_to_all | solution.py:307
  296.9 5.9 %all-to-all-done.7 = bf16[4,64,512]{2,1,0:T(8,128)(2,1)S(1)} async-done(((bf16[4,64,512]{2,1,0:T(8,128)(2,1)}), bf16[4,64,512]{2,1,0:T(8,128)(2,1)S(1)}, u32[]{:S(2)}, u32[]{:S(2)}) %all-to-all-start.7) | async-done | bytes 262176 | tf_op jit(solution)/shard_map/all_to_all | solution.py:307
  302.8 10.1 %reduce-scatter.2.cloned.1.call-done = bf16[4,64,512]{2,1,0:T(8,128)(2,1)} async-done(((bf16[4,64,4096]{2,1,0:T(8,128)(2,1)}), bf16[4,64,512]{2,1,0:T(8,128)(2,1)}) %reduce-scatter.2.cloned.1.call-update) | async-done | bytes 262160 | tf_op jit(solution)/shard_map/reduce_scatter | solution.py:303
  312.9 3.4 %all-to-all-start.4 = ((bf16[4,64,512]{2,1,0:T(8,128)(2,1)}), bf16[4,64,512]{2,1,0:T(8,128)(2,1)S(1)}, u32[]{:S(2)}, u32[]{:S(2)}) async-start(bf16[4,64,512]{2,1,0:T(8,128)(2,1)} %reduce-scatter.2.cloned.1.call-done), calls=%async_computation.5 | async-start | bytes 524288 | tf_op jit(solution)/shard_map/all_to_all | solution.py:307
  316.4 5.9 %all-to-all-done.4 = bf16[4,64,512]{2,1,0:T(8,128)(2,1)S(1)} async-done(((bf16[4,64,512]{2,1,0:T(8,128)(2,1)}), bf16[4,64,512]{2,1,0:T(8,128)(2,1)S(1)}, u32[]{:S(2)}, u32[]{:S(2)}) %all-to-all-start.4) | async-done | bytes 262176 | tf_op jit(solution)/shard_map/all_to_all | solution.py:307
  322.4 1.2 gather_fusion.6
  323.6 0.8 multiply_reduce_fusion.1
  324.5 0.7 add_convert_fusion
  (172 shorter events, 20.7 us)
Async XLA Ops:
  6.5 14.1 %copy-start = (bf16[128,4096]{1,0:T(8,128)(2,1)S(1)}, bf16[128,4096]{1,0:T(8,128)(2,1)}, u32[]{:S(2)}) copy-start(bf16[128,4096]{1,0:T(8,128)(2,1)} %param.21) | copy-start | bytes 3145732
  29.3 9.2 %copy-start.5 = (bf16[512,512]{1,0:T(8,128)(2,1)}, bf16[512,512]{1,0:T(8,128)(2,1)S(1)}, u32[]{:S(2)}) copy-start(bf16[512,512]{1,0:T(8,128)(2,1)S(1)} %all_gather.3) | copy-start | bytes 1572868
  51.5 2.1 copy-start.2
  51.6 4.0 %copy-start.16 = (s32[32,4]{0,1:T(4,128)S(1)}, s32[32,4]{0,1:T(4,128)}, u32[]{:S(2)}) copy-start(s32[32,4]{0,1:T(4,128)} %param.37) | copy-start | bytes 1540
  63.3 0.6 copy-start.19
  63.3 1.0 copy-start.6
  63.3 1.0 copy-start.14
  63.3 1.3 copy-start.17
  67.7 1.0 copy-start.4
  68.8 4.8 %copy-start.18 = (s32[128]{0:T(128)S(1)}, s32[128]{0:T(128)}, u32[]{:S(2)}) copy-start(s32[128]{0:T(128)} %param.40) | copy-start | bytes 1540
  69.9 19.6 %all-to-all-start = ((bf16[4,128,1152]{2,1,0:T(8,128)(2,1)}), bf16[4,128,1152]{2,1,0:T(8,128)(2,1)S(1)}, u32[]{:S(2)}, u32[]{:S(2)}) async-start(bf16[4,128,1152]{2,1,0:T(8,128)(2,1)} %bitcast.33), calls=%async_computation | async-start | bytes 2359296 | tf_op jit(solution)/shard_map/all_to_all | solution.py:172
  91.0 3.5 %copy-start.3 = (bf16[512,4096]{1,0:T(8,128)(2,1)S(1)}, bf16[512,4096]{1,0:T(8,128)(2,1)}, u32[]{:S(2)}) copy-start(bf16[512,4096]{1,0:T(8,128)(2,1)} %param.24) | copy-start | bytes 12582916
  94.4 0.9 copy-start.7
  127.0 4.9 %copy-start.10 = (s32[128,2]{0,1:T(2,128)S(1)}, s32[128,2]{0,1:T(2,128)}, u32[]{:S(2)}) copy-start(s32[128,2]{0,1:T(2,128)} %param.41) | copy-start | bytes 3076
  127.0 5.3 %copy-start.8 = (f32[4096]{0:T(1024)S(1)}, f32[4096]{0:T(1024)}, u32[]{:S(2)}) copy-start(f32[4096]{0:T(1024)} %param.25) | copy-start | bytes 49156
  128.3 29.1 %all-to-all-start.2 = ((bf16[8,128,512]{1,2,0:T(8,128)(2,1)}), bf16[8,128,512]{1,2,0:T(8,128)(2,1)S(1)}, u32[]{:S(2)}, u32[]{:S(2)}) async-start(bf16[8,128,512]{1,2,0:T(8,128)(2,1)} %broadcast_in_dim.242), calls=%async_computation.2 | async-start | bytes 2097152 | tf_op jit(solution)/shard_map/all_to_all | solution.py:260
  133.5 1.4 copy-start.12
  133.6 27.2 %copy-start.13 = (s32[256,1]{0,1:T(1,128)}, s32[256,1]{0,1:T(1,128)S(1)}, u32[]{:S(2)}) copy-start(s32[256,1]{0,1:T(1,128)S(1)} %compare_select_fusion.2) | copy-start | bytes 3076
  158.0 2.7 copy-start.15
  160.8 30.2 %all-to-all-start.3 = ((bf16[4,64,4096]{2,1,0:T(8,128)(2,1)}), bf16[4,64,4096]{2,1,0:T(8,128)(2,1)}, u32[]{:S(2)}, u32[]{:S(2)}) async-start(bf16[4,64,4096]{2,1,0:T(8,128)(2,1)} %convolution_convert_fusion.1), calls=%async_computation.3 | async-start | bytes 4194304 | tf_op jit(solution)/shard_map/all_to_all | solution.py:285
  191.0 29.3 %all-to-all-start.5 = ((bf16[4,64,4096]{2,1,0:T(8,128)(2,1)}), bf16[4,64,4096]{2,1,0:T(8,128)(2,1)S(1)}, u32[]{:S(2)}, u32[]{:S(2)}) async-start(bf16[4,64,4096]{2,1,0:T(8,128)(2,1)} %convolution_convert_fusion), calls=%async_computation.6 | async-start | bytes 4194304 | tf_op jit(solution)/shard_map/all_to_all | solution.py:285
  194.6 118.3 %reduce-scatter.2.cloned.1.call-start = ((), (), s32[]{:S(2)}) async-start(), calls=%async_computation.9 | async-start | bytes 2359296 | tf_op jit(solution)/shard_map/reduce_scatter | solution.py:303
  240.4 51.9 %all-to-all-start.6 = ((bf16[8,4,64,512]{3,2,1,0:T(8,128)(2,1)}), bf16[8,4,64,512]{3,2,1,0:T(8,128)(2,1)S(1)}, u32[]{:S(2)}, u32[]{:S(2)}) async-start(bf16[8,4,64,512]{3,2,1,0:T(8,128)(2,1)} %copy.265), calls=%async_computation.7 | async-start | bytes 4194304 | tf_op jit(solution)/shard_map/all_to_all | solution.py:296
  244.0 4.3 %copy-start.9 = (bf16[4096,8]{0,1:T(8,128)(2,1)S(1)}, bf16[4096,8]{0,1:T(8,128)(2,1)}, u32[]{:S(2)}) copy-start(bf16[4096,8]{0,1:T(8,128)(2,1)} %param.26) | copy-start | bytes 196612
  248.3 48.5 %copy-start.11 = (s32[128,2]{0,1:T(2,128)S(1)}, s32[128,2]{0,1:T(2,128)}, u32[]{:S(2)}) copy-start(s32[128,2]{0,1:T(2,128)} %param.41) | copy-start | bytes 3076
  293.4 9.4 %all-to-all-start.7 = ((bf16[4,64,512]{2,1,0:T(8,128)(2,1)}), bf16[4,64,512]{2,1,0:T(8,128)(2,1)S(1)}, u32[]{:S(2)}, u32[]{:S(2)}) async-start(bf16[4,64,512]{2,1,0:T(8,128)(2,1)} %reduce_sum.157), calls=%async_computation.8 | async-start | bytes 524288 | tf_op jit(solution)/shard_map/all_to_all | solution.py:307
  312.9 9.4 %all-to-all-start.4 = ((bf16[4,64,512]{2,1,0:T(8,128)(2,1)}), bf16[4,64,512]{2,1,0:T(8,128)(2,1)S(1)}, u32[]{:S(2)}, u32[]{:S(2)}) async-start(bf16[4,64,512]{2,1,0:T(8,128)(2,1)} %reduce-scatter.2.cloned.1.call-done), calls=%async_computation.5 | async-start | bytes 524288 | tf_op jit(solution)/shard_map/all_to_all | solution.py:307
  322.3 2.9 copy-start.1
Sparse Core Ops, SparseCore 0:
  215.1 97.6 reduce-scatter.1

commit v7 on v6

--- a/solution.py
+++ b/solution.py
@@ -307,9 +307,13 @@
             lax.all_to_all(summed, "dp", split_axis=0, concat_axis=0, tiled=True)
         )
     returned_rows = jnp.stack(returned_parts, axis=1)
-    results = jnp.take(returned_rows.reshape(-1, slice_width), pair_slot, axis=0).reshape(
-        local_rows, TOP, slice_width
-    )
+    result_pick = (
+        pair_slot[:, None] == jnp.arange(EXPERTS * E_CAP)[None, :]
+    ).astype(jnp.bfloat16)
+    results = jnp.einsum(
+        "pq,qd->pd", result_pick, returned_rows.reshape(-1, slice_width),
+        preferred_element_type=jnp.float32,
+    ).reshape(local_rows, TOP, slice_width)
     layer_out = kept_cols + jnp.sum(gate_weights[:, :, None] * results.astype(jnp.float32), axis=1)
     return layer_out.astype(jnp.bfloat16)
 

time: 339 us -> 337 us (level)
    unnamed x47 -> x45, local copies, waits for them, and re-layouts: 14.2 us -> 14.2 us
where the time goes in v7:
time: 337 us; the launch traced here: 330 us
  waiting for transfers between devices  109 us (32%)
  matrix products  62.9 us (19%)
  local copies, waits for them, and re-layouts  45.6 us (14%)
  blocking collectives  39.9 us (12%)
  other arithmetic  32.3 us (10%)
  starting transfers between devices  26.2 us (8%)
  between operations  14.6 us (4%)
    all_to_all x1, waiting for transfers between devices, shards(): lax.all_to_all(pieces, 'mp', split_axis=0, concat_axis=0, tiled=True)  46.2 us
    all_to_all x1, blocking collectives, shards(): lax.all_to_all(terms, 'mp', split_axis=0, concat_axis=0, tiled=True)  31.2 us
    dot_general x2, matrix products, shards(): jnp.einsum('scd,kfd->kscf', incoming, expert_in[expert_index], preferred_...  24.1 us
    all_to_all x1, waiting for transfers between devices, shards(): lax.all_to_all(spread_cols, 'mp', split_axis=0, concat_axis=0, tiled=True)  22.2 us
    unnamed x45, local copies, waits for them, and re-layouts  14.2 us
    all_to_all x2, waiting for transfers between devices, shards(): lax.all_to_all(summed, 'dp', split_axis=0, concat_axis=0, tiled=True)  11.9 us
    reduce_scatter x1, waiting for transfers between devices, shards(): lax.psum_scatter(expert_partial.astype(jnp.bfloat16), 'mp', scatter_dimen...  9.79 us
    gather x2, local copies, waits for them, and re-layouts, level_rows(): jnp.take(page_pool, page_list.reshape(-1), axis=1)  9.71 us
  transfers between devices with their start and end apart: 8, of which 8 were waited for; matrix products, arithmetic and copies ran while one was open for 23% of the time, Pallas kernels for 0%

profile of v7, /device:TPU:0, one launch (start us, length us, event | category | flops | bytes accessed | tf_op | source)
XLA Modules:
  0.0 330.4 jit_solution(2429613616015883031)
XLA Ops:
  6.5 0.7 fusion.133
  7.3 1.3 fusion.134
  8.6 0.7 fusion.131
  9.2 1.4 fusion.132
  10.9 0.8 scatter_custom_fusion.1
  12.0 0.7 fusion.127
  13.5 0.7 fusion.128
  14.2 1.3 gather_fusion
  15.5 0.7 broadcast_select_fusion.3
  16.2 1.2 gather_fusion.1
  17.7 0.9 select_reduce_fusion
  18.6 0.7 select_reduce_fusion.1
  20.6 8.6 %all_gather.3 = bf16[512,512]{1,0:T(8,128)(2,1)S(1)} all-gather(bf16[128,512]{1,0:T(8,128)(2,1)S(1)} %constant_dynamic-slice_fusion), channel_id=1, replica_groups=mesh['dp'=4,'mp'=8] {'dp'}, dimensions={0}, use_global_device_ids=true | all-gather | bytes 655360 | tf_op jit(solution)/shard_map/all_gather | solution.py:85
  29.3 6.0 %gather_fusion.2 = bf16[64,2,128,128]{3,2,1,0:T(8,128)(2,1)} fusion(bf16[2,96,128,128]{3,2,1,0:T(8,128)(2,1)} %bitcast.245, s32[1024]{0:T(1024)S(1)} %pad_clamp_fusion.2), kind=kCustom, calls=%fused_computation.2 | custom fusion | bytes 8388864 | tf_op jit(solution)/shard_map/jit(_take)/gather | solution.py:117
  35.3 2.6 select_bitcast_fusion
  38.5 0.7 fusion.40
  39.2 2.8 fusion.6
  42.0 5.1 %fusion.7 = f32[2,128,4]{1,2,0:T(4,128)S(1)} fusion(f32[2,128,4,4096]{3,1,2,0:T(8,128)S(1)} %get-tuple-element.37, f32[2,128,4]{1,2,0:T(4,128)S(1)} %get-tuple-element.36, pred[2,4096]{1,0:T(4,128)(4,1)S(1)} %broadcast_compare_fusion), kind=kLoop, calls=%fused_computation.18 | loop fusion | flops 20970496 | bytes 16793600 | tf_op jit(solution)/shard_map/vmap()/reduce_sum | solution.py:39
  47.1 4.2 %fusion.12 = f32[2,128,4,128]{1,3,2,0:T(8,128)S(1)} fusion(bf16[2,4096,128,1]{2,1,3,0:T(8,128)(2,1)S(1)} %bitcast.250, f32[2,128,4,4096]{3,1,2,0:T(8,128)S(1)} %get-tuple-element.37, f32[2,128,4]{1,2,0:T(4,128)S(1)} %get-tuple-element.36, pred[2,4096]{1,0:T(4,128)(4,1)S(1)} %broadcast_compare_fusion), kind=kOutput, calls=%fused_computation.23 | convolution fusion | flops 1094713344 | bytes 19410944 | tf_op jit(solution)/shard_map/vmap(sgl,ld->sgd)/dot_general | solution.py:40
  51.7 1.0 convolution_bitcast_fusion.1
  52.7 0.8 slice.286
  53.6 0.6 gather_fusion.3
  54.3 1.3 broadcast_select_fusion.2
  56.9 0.7 broadcast_compare_fusion.2
  57.6 1.1 reduce-window.36
  59.2 3.7 %gather_fusion.5 = bf16[32,2,128,128]{3,2,1,0:T(8,128)(2,1)S(1)} fusion(bf16[2,96,128,128]{3,2,1,0:T(8,128)(2,1)} %bitcast.246, s32[1024]{0:T(1024)S(1)} %pad_clamp_fusion), kind=kCustom, calls=%fused_computation.5 | custom fusion | bytes 4194432 | tf_op jit(solution)/shard_map/jit(_take)/gather | solution.py:117
  65.3 0.7 fusion.36
  66.8 0.9 convolution_bitcast_fusion
  68.8 1.1 fusion.39
  69.9 3.7 %all-to-all-start = ((bf16[4,128,1152]{2,1,0:T(8,128)(2,1)}), bf16[4,128,1152]{2,1,0:T(8,128)(2,1)S(1)}, u32[]{:S(2)}, u32[]{:S(2)}) async-start(bf16[4,128,1152]{2,1,0:T(8,128)(2,1)} %bitcast.33), calls=%async_computation | async-start | bytes 2359296 | tf_op jit(solution)/shard_map/all_to_all | solution.py:172
  73.8 4.5 %fusion.161 = (f32[128,4]{1,0:T(8,128)S(1)}, f32[128,4,128]{2,1,0:T(4,128)S(1)}) fusion(bf16[128,4,128]{2,1,0:T(4,128)(2,1)S(1)} %reshape.747, bf16[2,128,1,128,128]{4,3,1,2,0:T(8,128)(2,1)} %bitcast.265, pred[128,128]{1,0:T(8,128)(4,1)S(1)} %iota_compare_fusion.10), kind=kOutput, calls=%fused_computation.287 | convolution fusion | flops 16973312 | bytes 4605952 | tf_op jit(solution)/shard_map/rgd,rtd->rgt/dot_general | solution.py:198
  78.8 0.8 fusion.107
  80.0 9.5 %all-to-all-done = bf16[4,128,1152]{2,1,0:T(8,128)(2,1)S(1)} async-done(((bf16[4,128,1152]{2,1,0:T(8,128)(2,1)}), bf16[4,128,1152]{2,1,0:T(8,128)(2,1)S(1)}, u32[]{:S(2)}, u32[]{:S(2)}) %all-to-all-start) | async-done | bytes 1179680 | tf_op jit(solution)/shard_map/all_to_all | solution.py:172
  91.0 3.2 fusion.57
  94.4 0.7 fusion.98
  95.6 31.2 %all_to_all.40 = bf16[8,128,512]{2,1,0:T(8,128)(2,1)S(1)} all-to-all(bf16[8,128,512]{2,1,0:T(8,128)(2,1)S(1)} %bitcast.248), channel_id=1, replica_groups=mesh['dp'=4,'mp'=8] {'mp'}, dimensions={0} | all-to-all | bytes 2097152 | tf_op jit(solution)/shard_map/all_to_all | solution.py:255
  127.2 1.1 broadcast_in_dim.234
  128.3 3.6 %all-to-all-start.2 = ((bf16[8,128,512]{1,2,0:T(8,128)(2,1)}), bf16[8,128,512]{1,2,0:T(8,128)(2,1)S(1)}, u32[]{:S(2)}, u32[]{:S(2)}) async-start(bf16[8,128,512]{1,2,0:T(8,128)(2,1)} %broadcast_in_dim.234), calls=%async_computation.2 | async-start | bytes 2097152 | tf_op jit(solution)/shard_map/all_to_all | solution.py:260
  133.6 1.4 scatter_custom_fusion.2
  135.2 22.2 %all-to-all-done.2 = bf16[8,128,512]{1,2,0:T(8,128)(2,1)S(1)} async-done(((bf16[8,128,512]{1,2,0:T(8,128)(2,1)}), bf16[8,128,512]{1,2,0:T(8,128)(2,1)S(1)}, u32[]{:S(2)}, u32[]{:S(2)}) %all-to-all-start.2) | async-done | bytes 1048608 | tf_op jit(solution)/shard_map/all_to_all | solution.py:260
  158.0 0.7 multiply_convert_fusion
  158.7 2.0 convolution_convert_fusion.1
  160.8 4.4 %all-to-all-start.3 = ((bf16[4,64,4096]{2,1,0:T(8,128)(2,1)}), bf16[4,64,4096]{2,1,0:T(8,128)(2,1)}, u32[]{:S(2)}, u32[]{:S(2)}) async-start(bf16[4,64,4096]{2,1,0:T(8,128)(2,1)} %convolution_convert_fusion.1), calls=%async_computation.3 | async-start | bytes 4194304 | tf_op jit(solution)/shard_map/all_to_all | solution.py:285
  165.2 7.7 %slice.159 = bf16[1,1024,4096]{2,1,0:T(8,128)(2,1)} slice(bf16[2,1024,4096]{2,1,0:T(8,128)(2,1)} %param.28), slice={[1:2], [0:1024], [0:4096]} | slice | bytes 16777216 | tf_op jit(solution)/shard_map/slice | solution.py:293
  172.9 12.0 %copy.287 = bf16[1,1024,4096]{1,2,0:T(8,128)(2,1)} copy(bf16[1,1024,4096]{2,1,0:T(8,128)(2,1)} %slice.159) | data formatting | bytes 16777216
  184.9 2.0 convolution_convert_fusion
  186.9 4.1 %all-to-all-done.3 = bf16[4,64,4096]{2,1,0:T(8,128)(2,1)} async-done(((bf16[4,64,4096]{2,1,0:T(8,128)(2,1)}), bf16[4,64,4096]{2,1,0:T(8,128)(2,1)}, u32[]{:S(2)}, u32[]{:S(2)}) %all-to-all-start.3) | async-done | bytes 2097184 | tf_op jit(solution)/shard_map/all_to_all | solution.py:285
  191.0 3.6 %all-to-all-start.5 = ((bf16[4,64,4096]{2,1,0:T(8,128)(2,1)}), bf16[4,64,4096]{2,1,0:T(8,128)(2,1)S(1)}, u32[]{:S(2)}, u32[]{:S(2)}) async-start(bf16[4,64,4096]{2,1,0:T(8,128)(2,1)} %convolution_convert_fusion), calls=%async_computation.6 | async-start | bytes 4194304 | tf_op jit(solution)/shard_map/all_to_all | solution.py:285
  194.9 12.3 %fusion.26 = f32[2,4,64,1024]{3,2,0,1:T(8,128)} fusion(bf16[2,2,1024,4096]{3,2,1,0:T(8,128)(2,1)} %param.27, bf16[4,64,4096]{2,1,0:T(8,128)(2,1)} %all-to-all-done.3), kind=kOutput, calls=%fused_computation.49 | convolution fusion | flops 4294967296 | bytes 20971520 | tf_op jit(solution)/shard_map/scd,kfd->kscf/dot_general | solution.py:286
  207.2 7.8 %fusion.15 = bf16[4,64,4096]{2,1,0:T(8,128)(2,1)} fusion(bf16[2,1024,4096]{2,1,0:T(8,128)(2,1)} %param.28, f32[2,4,64,1024]{3,2,0,1:T(8,128)} %fusion.26), kind=kOutput, calls=%fused_computation.25 | convolution fusion | flops 2150105088 | bytes 12582912 | tf_op jit(solution)/shard_map/scf,fd->scd/dot_general | solution.py:299
  215.0 5.2 %all-to-all-done.5 = bf16[4,64,4096]{2,1,0:T(8,128)(2,1)S(1)} async-done(((bf16[4,64,4096]{2,1,0:T(8,128)(2,1)}), bf16[4,64,4096]{2,1,0:T(8,128)(2,1)S(1)}, u32[]{:S(2)}, u32[]{:S(2)}) %all-to-all-start.5) | async-done | bytes 2097184 | tf_op jit(solution)/shard_map/all_to_all | solution.py:285
  220.2 11.8 %fusion.31 = f32[2,4,64,1024]{3,2,0,1:T(8,128)} fusion(bf16[2,2,1024,4096]{3,2,1,0:T(8,128)(2,1)} %param.27, bf16[4,64,4096]{2,1,0:T(8,128)(2,1)S(1)} %all-to-all-done.5), kind=kOutput, calls=%fused_computation.50 | convolution fusion | flops 4294967296 | bytes 20971520 | tf_op jit(solution)/shard_map/scd,kfd->kscf/dot_general | solution.py:286
  232.0 6.6 %convert_bitcast_fusion = bf16[8,4,64,512]{3,2,0,1:T(8,128)(2,1)S(1)} fusion(bf16[1024,8,512,1]{0,2,1,3:T(8,128)(2,1)} %bitcast.243, f32[2,4,64,1024]{3,2,0,1:T(8,128)} %fusion.31), kind=kOutput, calls=%fused_computation.42 | convolution fusion | flops 2150105088 | bytes 12582912 | tf_op jit(solution)/shard_map/scf,fmd->mscd/dot_general | solution.py:291
  238.6 1.5 copy.264
  240.1 3.6 %all-to-all-start.6 = ((bf16[8,4,64,512]{3,2,1,0:T(8,128)(2,1)}), bf16[8,4,64,512]{3,2,1,0:T(8,128)(2,1)S(1)}, u32[]{:S(2)}, u32[]{:S(2)}) async-start(bf16[8,4,64,512]{3,2,1,0:T(8,128)(2,1)} %copy.264), calls=%async_computation.7 | async-start | bytes 4194304 | tf_op jit(solution)/shard_map/all_to_all | solution.py:296
  244.3 1.3 fusion.24
  245.9 46.2 %all-to-all-done.6 = bf16[8,4,64,512]{3,2,1,0:T(8,128)(2,1)S(1)} async-done(((bf16[8,4,64,512]{3,2,1,0:T(8,128)(2,1)}), bf16[8,4,64,512]{3,2,1,0:T(8,128)(2,1)S(1)}, u32[]{:S(2)}, u32[]{:S(2)}) %all-to-all-start.6) | async-done | bytes 2097184 | tf_op jit(solution)/shard_map/all_to_all | solution.py:296
  292.1 1.1 reduce_sum.157
  293.2 3.5 %all-to-all-start.7 = ((bf16[4,64,512]{2,1,0:T(8,128)(2,1)}), bf16[4,64,512]{2,1,0:T(8,128)(2,1)S(1)}, u32[]{:S(2)}, u32[]{:S(2)}) async-start(bf16[4,64,512]{2,1,0:T(8,128)(2,1)} %reduce_sum.157), calls=%async_computation.8 | async-start | bytes 524288 | tf_op jit(solution)/shard_map/all_to_all | solution.py:307
  296.8 5.9 %all-to-all-done.7 = bf16[4,64,512]{2,1,0:T(8,128)(2,1)S(1)} async-done(((bf16[4,64,512]{2,1,0:T(8,128)(2,1)}), bf16[4,64,512]{2,1,0:T(8,128)(2,1)S(1)}, u32[]{:S(2)}, u32[]{:S(2)}) %all-to-all-start.7) | async-done | bytes 262176 | tf_op jit(solution)/shard_map/all_to_all | solution.py:307
  302.8 9.8 %reduce-scatter.2.cloned.1.call-done = bf16[4,64,512]{2,1,0:T(8,128)(2,1)} async-done(((bf16[4,64,4096]{2,1,0:T(8,128)(2,1)}), bf16[4,64,512]{2,1,0:T(8,128)(2,1)}) %reduce-scatter.2.cloned.1.call-update) | async-done | bytes 262160 | tf_op jit(solution)/shard_map/reduce_scatter | solution.py:303
  312.6 3.4 %all-to-all-start.4 = ((bf16[4,64,512]{2,1,0:T(8,128)(2,1)}), bf16[4,64,512]{2,1,0:T(8,128)(2,1)S(1)}, u32[]{:S(2)}, u32[]{:S(2)}) async-start(bf16[4,64,512]{2,1,0:T(8,128)(2,1)} %reduce-scatter.2.cloned.1.call-done), calls=%async_computation.5 | async-start | bytes 524288 | tf_op jit(solution)/shard_map/all_to_all | solution.py:307
  316.0 6.0 %all-to-all-done.4 = bf16[4,64,512]{2,1,0:T(8,128)(2,1)S(1)} async-done(((bf16[4,64,512]{2,1,0:T(8,128)(2,1)}), bf16[4,64,512]{2,1,0:T(8,128)(2,1)S(1)}, u32[]{:S(2)}, u32[]{:S(2)}) %all-to-all-start.4) | async-done | bytes 262176 | tf_op jit(solution)/shard_map/all_to_all | solution.py:307
  322.4 0.7 add_convert_fusion
  (163 shorter events, 17.4 us)
Async XLA Ops:
  6.5 14.1 %copy-start = (bf16[128,4096]{1,0:T(8,128)(2,1)S(1)}, bf16[128,4096]{1,0:T(8,128)(2,1)}, u32[]{:S(2)}) copy-start(bf16[128,4096]{1,0:T(8,128)(2,1)} %param.21) | copy-start | bytes 3145732
  29.3 9.2 %copy-start.5 = (bf16[512,512]{1,0:T(8,128)(2,1)}, bf16[512,512]{1,0:T(8,128)(2,1)S(1)}, u32[]{:S(2)}) copy-start(bf16[512,512]{1,0:T(8,128)(2,1)S(1)} %all_gather.3) | copy-start | bytes 1572868
  51.5 2.1 copy-start.2
  51.6 4.0 %copy-start.14 = (s32[32,4]{0,1:T(4,128)S(1)}, s32[32,4]{0,1:T(4,128)}, u32[]{:S(2)}) copy-start(s32[32,4]{0,1:T(4,128)} %param.37) | copy-start | bytes 1540
  63.3 0.6 copy-start.18
  63.3 1.0 copy-start.6
  63.3 1.0 copy-start.12
  63.3 1.3 copy-start.15
  67.7 1.0 copy-start.4
  68.8 4.8 %copy-start.17 = (s32[128]{0:T(128)S(1)}, s32[128]{0:T(128)}, u32[]{:S(2)}) copy-start(s32[128]{0:T(128)} %param.40) | copy-start | bytes 1540
  69.9 19.6 %all-to-all-start = ((bf16[4,128,1152]{2,1,0:T(8,128)(2,1)}), bf16[4,128,1152]{2,1,0:T(8,128)(2,1)S(1)}, u32[]{:S(2)}, u32[]{:S(2)}) async-start(bf16[4,128,1152]{2,1,0:T(8,128)(2,1)} %bitcast.33), calls=%async_computation | async-start | bytes 2359296 | tf_op jit(solution)/shard_map/all_to_all | solution.py:172
  91.0 3.5 %copy-start.3 = (bf16[512,4096]{1,0:T(8,128)(2,1)S(1)}, bf16[512,4096]{1,0:T(8,128)(2,1)}, u32[]{:S(2)}) copy-start(bf16[512,4096]{1,0:T(8,128)(2,1)} %param.24) | copy-start | bytes 12582916
  94.4 0.9 copy-start.7
  127.0 4.9 %copy-start.10 = (s32[128,2]{0,1:T(2,128)S(1)}, s32[128,2]{0,1:T(2,128)}, u32[]{:S(2)}) copy-start(s32[128,2]{0,1:T(2,128)} %param.41) | copy-start | bytes 3076
  127.0 5.3 %copy-start.8 = (f32[4096]{0:T(1024)S(1)}, f32[4096]{0:T(1024)}, u32[]{:S(2)}) copy-start(f32[4096]{0:T(1024)} %param.25) | copy-start | bytes 49156
  128.3 29.1 %all-to-all-start.2 = ((bf16[8,128,512]{1,2,0:T(8,128)(2,1)}), bf16[8,128,512]{1,2,0:T(8,128)(2,1)S(1)}, u32[]{:S(2)}, u32[]{:S(2)}) async-start(bf16[8,128,512]{1,2,0:T(8,128)(2,1)} %broadcast_in_dim.234), calls=%async_computation.2 | async-start | bytes 2097152 | tf_op jit(solution)/shard_map/all_to_all | solution.py:260
  158.0 2.7 copy-start.13
  160.8 30.2 %all-to-all-start.3 = ((bf16[4,64,4096]{2,1,0:T(8,128)(2,1)}), bf16[4,64,4096]{2,1,0:T(8,128)(2,1)}, u32[]{:S(2)}, u32[]{:S(2)}) async-start(bf16[4,64,4096]{2,1,0:T(8,128)(2,1)} %convolution_convert_fusion.1), calls=%async_computation.3 | async-start | bytes 4194304 | tf_op jit(solution)/shard_map/all_to_all | solution.py:285
  191.0 29.3 %all-to-all-start.5 = ((bf16[4,64,4096]{2,1,0:T(8,128)(2,1)}), bf16[4,64,4096]{2,1,0:T(8,128)(2,1)S(1)}, u32[]{:S(2)}, u32[]{:S(2)}) async-start(bf16[4,64,4096]{2,1,0:T(8,128)(2,1)} %convolution_convert_fusion), calls=%async_computation.6 | async-start | bytes 4194304 | tf_op jit(solution)/shard_map/all_to_all | solution.py:285
  194.6 118.0 %reduce-scatter.2.cloned.1.call-start = ((), (), s32[]{:S(2)}) async-start(), calls=%async_computation.9 | async-start | bytes 2359296 | tf_op jit(solution)/shard_map/reduce_scatter | solution.py:303
  240.1 52.1 %all-to-all-start.6 = ((bf16[8,4,64,512]{3,2,1,0:T(8,128)(2,1)}), bf16[8,4,64,512]{3,2,1,0:T(8,128)(2,1)S(1)}, u32[]{:S(2)}, u32[]{:S(2)}) async-start(bf16[8,4,64,512]{3,2,1,0:T(8,128)(2,1)} %copy.264), calls=%async_computation.7 | async-start | bytes 4194304 | tf_op jit(solution)/shard_map/all_to_all | solution.py:296
  243.7 2.0 copy-start.9
  245.7 51.1 %copy-start.11 = (s32[128,2]{0,1:T(2,128)S(1)}, s32[128,2]{0,1:T(2,128)}, u32[]{:S(2)}) copy-start(s32[128,2]{0,1:T(2,128)} %param.41) | copy-start | bytes 3076
  293.2 28.9 %copy-start.16 = (s32[128,2]{0,1:T(2,128)S(1)}, s32[128,2]{0,1:T(2,128)}, u32[]{:S(2)}) copy-start(s32[128,2]{0,1:T(2,128)} %copy.258) | copy-start | bytes 3076
  293.2 9.5 %all-to-all-start.7 = ((bf16[4,64,512]{2,1,0:T(8,128)(2,1)}), bf16[4,64,512]{2,1,0:T(8,128)(2,1)S(1)}, u32[]{:S(2)}, u32[]{:S(2)}) async-start(bf16[4,64,512]{2,1,0:T(8,128)(2,1)} %reduce_sum.157), calls=%async_computation.8 | async-start | bytes 524288 | tf_op jit(solution)/shard_map/all_to_all | solution.py:307
  296.8 26.3 %copy-start.1 = (bf16[128,4096]{1,0:T(8,128)(2,1)S(1)}, bf16[128,4096]{1,0:T(8,128)(2,1)}, u32[]{:S(2)}) copy-start(bf16[128,4096]{1,0:T(8,128)(2,1)} %param.21) | copy-start | bytes 3145732
  312.6 9.4 %all-to-all-start.4 = ((bf16[4,64,512]{2,1,0:T(8,128)(2,1)}), bf16[4,64,512]{2,1,0:T(8,128)(2,1)S(1)}, u32[]{:S(2)}, u32[]{:S(2)}) async-start(bf16[4,64,512]{2,1,0:T(8,128)(2,1)} %reduce-scatter.2.cloned.1.call-done), calls=%async_computation.5 | async-start | bytes 524288 | tf_op jit(solution)/shard_map/all_to_all | solution.py:307
Sparse Core Ops, SparseCore 0:
  215.1 97.3 reduce-scatter.1
